TPU v7x, 128 devices: a whole 4x4x4 slice. The times are simulated.
128 devices in a mesh: lon: 16 (over x_hi, y, core), lat: 8 (over x_lo, z).
Axes of the slice: x: 4 (x_hi: 2, x_lo: 2; x = x_hi * 2 + x_lo), y: 4, z: 4, core: 2. Of those that a mesh axis runs over, the one named last changes fastest.
Arguments:
- state: float32 [32, 128, 2048], P(None, 'lat', 'lon'), may hold values from -6 to 6
- land_mask: int32 [128, 2048], P('lat', 'lon'), may hold values 0 or 1
- observations: float32 [32, 131072], P(None, ('lon', 'lat')), may hold values from -6 to 6
- profile_cells: int32 [131072], P(('lon', 'lat')), may hold values from 0 to 2047
- profile_counts: int32 [128, 128], P(('lon', 'lat')), may hold values from 1 to 32, 1024 in all within a row
- w_in: bfloat16 [64, 32, 5, 5], replicated, may hold values from -0.21875 to 0.21875
- w_out: bfloat16 [32, 64, 5, 5], replicated, may hold values from -0.15625 to 0.15625
Outputs:
- final_state: float32 [32, 128, 2048], P(None, 'lat', 'lon')
- misfit: float32 [], replicated
- grad_in: float32 [64, 32, 5, 5], replicated
- grad_out: float32 [32, 64, 5, 5], replicated
- adjoint_state: float32 [32, 128, 2048], P(None, 'lat', 'lon')
Inputs may be any that keep to these rules, and one draw needn't show every extreme that they name: `profile_counts`: each row sums to 1024, and in every row some entry equals 32.
All inputs are finite; a program needn't handle non-finite values. No bound on the sum of `land_mask` on one device may be relied on, other than what follows from the above.
Results may differ from a plain program's by a relative error of at most 0.0046.
Values may be sent and summed in bfloat16 or wider, within the bound.
No kernel may reach another device: no remote copies, remote signals or barrier semaphores. Data moves between devices by JAX's collectives and lax.ppermute only.
A program may use at most 64 MiB of HBM per device.

v0:
```python
import jax
import jax.numpy as jnp
from jax import lax
from jax.sharding import PartitionSpec as P

STEPS = 2
CAP = 32


diffusion = 0.2


def extended_2(cells, sides, width):
    for axis, dim in sides:
        count = lax.axis_size(axis)
        head = lax.slice_in_dim(cells, 0, width, axis=dim)
        tail = lax.slice_in_dim(cells, cells.shape[dim] - width, cells.shape[dim], axis=dim)
        cells = jnp.concatenate(
            [
                lax.ppermute(tail, axis, [(i, (i + 1) % count) for i in range(count)]),
                cells,
                lax.ppermute(head, axis, [((i + 1) % count, i) for i in range(count)]),
            ],
            axis=dim,
        )
    return cells


def laplace(extended, border):
    height = extended.shape[1] - 2 * border
    breadth = extended.shape[2] - 2 * border

    def neighbour(offset_y, offset_x):
        return extended[
            :,
            border + offset_y : border + offset_y + height,
            border + offset_x : border + offset_x + breadth,
        ]

    return (
        neighbour(-1, 0)
        + neighbour(1, 0)
        + neighbour(0, -1)
        + neighbour(0, 1)
        - 4.0 * neighbour(0, 0)
    )


def conv_valid(padded, kernel):
    return lax.conv_general_dilated(
        padded[None],
        kernel,
        (1, 1),
        "VALID",
        dimension_numbers=("NCHW", "OIHW", "NCHW"),
        preferred_element_type=jnp.float32,
    )[0]


def flipped(kernel):
    return jnp.transpose(kernel[:, :, ::-1, ::-1], (1, 0, 2, 3))


def kernel_grad(padded, cotangent):
    height, breadth = (cotangent.shape[1], cotangent.shape[2])
    width = padded.shape[2] - breadth + 1
    stripes = []
    for shift_y in range(width):
        pieces = []
        for shift_x in range(width):
            window = padded[:, shift_y : shift_y + height, shift_x : shift_x + breadth]
            pieces.append(
                jnp.einsum("ohw,chw->oc", cotangent, window, preferred_element_type=jnp.float32)
            )
        stripes.append(jnp.stack(pieces, axis=-1))
    return jnp.stack(stripes, axis=-2)


def inside_rows(tile_rows, border):
    first_row = lax.axis_index("lat") * tile_rows
    global_rows = first_row + jnp.arange(-border, tile_rows + border, dtype=jnp.int32)
    row_limit = tile_rows * lax.axis_size("lat")
    return ((global_rows >= 0) & (global_rows < row_limit)).astype(jnp.float32)[None, :, None]


def on_device(state, land_mask, observations, profile_cells, profile_counts, w_in, w_out):
    levels, tile_rows, tile_cols = state.shape
    ocean = land_mask.astype(jnp.float32)
    back_in = flipped(w_in)
    back_out = flipped(w_out)
    current = state
    history = []
    for step_index in range(STEPS):
        extended = extended_2(current, (("lon", 2), ("lat", 1)), 4) * inside_rows(tile_rows, 4)
        coarse = extended.astype(jnp.bfloat16)
        activity = jnp.tanh(conv_valid(coarse, w_in))
        hidden = (activity * inside_rows(tile_rows, 2)).astype(jnp.bfloat16)
        closure = conv_valid(hidden, w_out)
        history.append((coarse[:, 2:-2, 2:-2], activity, hidden))
        current = current + ocean * (diffusion * laplace(extended, 4) + closure)
    devices = lax.axis_size("lon") * lax.axis_size("lat")
    profile_dev = observations.shape[1]
    cell_count = tile_rows * tile_cols
    sent_rows = profile_counts[0]
    finish = jnp.cumsum(sent_rows)
    starts = finish - sent_rows
    slot_index = jnp.arange(CAP, dtype=jnp.int32)
    source_row = starts[:, None] + slot_index[None, :]
    filled = (slot_index[None, :] < sent_rows[:, None]).reshape(1, -1)
    picked = jnp.clip(source_row, 0, profile_dev - 1).reshape(-1)
    sent_values = jnp.where(filled, jnp.take(observations, picked, axis=1), 0.0)
    sent_cells = jnp.where(filled, jnp.take(profile_cells, picked)[None, :], cell_count).astype(
        jnp.float32
    )
    payload = jnp.concatenate([sent_values, sent_cells], axis=0)
    arrived = lax.all_to_all(payload, ("lon", "lat"), split_axis=1, concat_axis=1, tiled=True)
    received_values = arrived[:levels]
    received_cells = arrived[levels:].astype(jnp.int32)
    occupied = received_cells < cell_count
    target = jnp.where(occupied, received_cells, 0)[0]
    flat_state = current.reshape(levels, cell_count)
    misfits = jnp.where(occupied, jnp.take(flat_state, target, axis=1) - received_values, 0.0)
    square_sum = jnp.sum(misfits * misfits)
    tangent = (
        jnp.zeros((levels, cell_count), jnp.float32)
        .at[:, target]
        .add(misfits / profile_dev)
        .reshape(levels, tile_rows, tile_cols)
    )
    grad_in = jnp.zeros(w_in.shape, jnp.float32)
    grad_out = jnp.zeros(w_out.shape, jnp.float32)
    for step_index in reversed(range(STEPS)):
        coarse, activity, hidden = history[step_index]
        forcing = ocean * tangent
        forcing_low = forcing.astype(jnp.bfloat16)
        grad_out = grad_out + kernel_grad(hidden, forcing_low)
        derivative = 1.0 - activity * activity
        beside_all = extended_2(forcing, (("lon", 2), ("lat", 1)), 2) * inside_rows(tile_rows, 2)
        spread = conv_valid(beside_all.astype(jnp.bfloat16), back_out)
        sensitivity = (spread * derivative[:, 2:-2, 2:-2]).astype(jnp.bfloat16)
        grad_in = grad_in + kernel_grad(coarse, sensitivity)
        margin = extended_2(sensitivity, (("lon", 2), ("lat", 1)), 2) * inside_rows(
            tile_rows, 2
        ).astype(jnp.bfloat16)
        tangent = tangent + diffusion * laplace(beside_all, 2) + conv_valid(margin, back_in)
    grad_in, grad_out, square_sum = lax.psum((grad_in, grad_out, square_sum), ("lon", "lat"))
    misfit = square_sum / (2.0 * profile_dev * devices * levels)
    return (current, misfit, grad_in, grad_out, tangent * profile_dev)


def solution(mesh):
    placed = (
        P(None, "lat", "lon"),
        P("lat", "lon"),
        P(None, ("lon", "lat")),
        P(("lon", "lat")),
        P(("lon", "lat"), None),
        P(),
        P(),
    )
    return jax.shard_map(
        on_device,
        mesh=mesh,
        in_specs=placed,
        out_specs=(P(None, "lat", "lon"), P(), P(), P(), P(None, "lat", "lon")),
        check_vma=False,
    )
```

profile of v0, /device:TPU:1, one launch (start us, length us, event | category | flops | bytes accessed | tf_op | source)
XLA Modules:
  0.0 529.8 jit_solution(15204486380802402568)
XLA Ops:
  13.2 16.7 %gather_fusion.1 = s32[4096]{0:T(1024)S(1)} fusion(s32[1024]{0:T(1024)S(1)} %copy-done.1, s32[4096]{0:T(1024)S(1)} %broadcast_clamp_fusion.1), kind=kCustom, calls=%fused_computation.1 | custom fusion | bytes 49152 | tf_op jit(solution)/shard_map/jit(_take)/gather | solution.py:112
  30.1 1.9 copy.269
  32.3 14.2 %gather_fusion = f32[4096,32]{1,0:T(8,128)} fusion(f32[32,1024]{0,1:T(8,128)S(1)} %copy.267, s32[4096]{0:T(1024)S(1)} %broadcast_clamp_fusion.1), kind=kCustom, calls=%fused_computation | custom fusion | bytes 1064960 | tf_op jit(solution)/shard_map/jit(_take)/gather | solution.py:111
  46.6 3.2 select_select_fusion
  49.8 2.0 fusion.254
  51.7 4.6 reshape.790
  56.3 13.8 %all-to-all-start = ((f32[128,1,1056]{2,1,0:T(1,128)}), f32[128,1,1056]{2,1,0:T(1,128)}, u32[]{:S(2)}, u32[]{:S(2)}) async-start(f32[128,1,1056]{2,1,0:T(1,128)} %reshape.790), calls=%async_computation | async-start | bytes 1179648 | tf_op jit(solution)/shard_map/all_to_all | solution.py:116
  71.6 4.2 collective-permute-start.3
  77.6 4.7 collective-permute-done.3
  82.3 1.8 collective-permute-done.2
  85.5 3.0 select_tanh_fusion.1
  89.5 4.0 fusion.26
  96.9 2.0 collective-permute-start.5
  99.9 1.9 copy.318
  105.7 2.2 collective-permute-done.7
  107.9 2.6 collective-permute-done.6
  111.4 3.0 select_tanh_fusion
  115.6 4.0 fusion.30
  125.2 3.2 copy.315
  128.4 2.1 multiply_convert_fusion.2
  131.0 3.9 reduce.2
  134.9 4.8 reshape.791
  139.7 3.6 slice.695
  143.3 2.7 copy.313
  146.5 14.2 %gather_fusion.2 = f32[4096,32]{1,0:T(8,128)} fusion(f32[32,2048]{0,1:T(8,128)S(1)} %bitcast.392, s32[4096]{0:T(1024)S(1)} %broadcast_clamp_fusion), kind=kCustom, calls=%fused_computation.2 | custom fusion | bytes 1064960 | tf_op jit(solution)/shard_map/jit(_take)/gather | solution.py:122
  160.7 5.6 %fusion.241 = (f32[32,128,32]{0,2,1:T(8,128)S(1)}, f32[]{:T(128)}) fusion(f32[33,128,32]{0,2,1:T(8,128)} %bitcast.394, f32[32,128,32]{0,2,1:T(8,128)} %bitcast.395, pred[128,32]{1,0:T(8,128)(4,1)S(1)} %copy.272, pred[128,32]{1,0:T(8,128)(4,1)S(1)} %copy.271), kind=kLoop, calls=%fused_computation.433 | loop fusion | flops 655359 | bytes 1581060 | tf_op jit(solution)/shard_map/slice | solution.py:117
  166.4 2.8 fusion.3
  169.1 25.6 %scatter_custom_fusion = f32[32,2048]{0,1:T(8,128)S(1)} fusion(s32[4096]{0:T(1024)S(1)} %bitcast.427, f32[32,4096]{0,1:T(8,128)} %fusion.3, f32[]{:T(128)} %constant.41.clone.1), kind=kCustom, calls=%fused_computation.5 | custom fusion | flops 131072 | bytes 786436 | tf_op jit(solution)/shard_map/scatter-add | solution.py:127
  198.6 7.8 %collective-permute-start.9 = (f32[32,16,2]{2,0,1:T(8,128)}, f32[32,16,2]{2,0,1:T(8,128)S(1)}, u32[]{:S(2)}, u32[]{:S(2)}) collective-permute-start(f32[32,16,2]{2,0,1:T(8,128)} %get-tuple-element.67), channel_id=1, source_target_pairs={{8,0},{16,8},{24,16},{32,24},{40,32},{48,40},{56,48},{64,56},{72,6... | collective-permute-start | bytes 12296 | tf_op jit(solution)/shard_map/ppermute | solution.py:22
  214.6 66.7 %psum.21 = f32[]{:T(128)} all-reduce(f32[]{:T(128)} %get-tuple-element.47), channel_id=1, replica_groups=mesh['lon'=16,'lat'=8] {'lon','lat'}, use_global_device_ids=true, to_apply=%region_2.3 | all-reduce | flops 1 | bytes 8 | tf_op jit(solution)/shard_map/psum | solution.py:146
  285.5 3.3 collective-permute-done.10
  292.2 2.6 convolution_select_fusion.3
  305.8 2.1 collective-permute-start.13
  308.8 3.6 collective-permute-done.13
  316.3 2.1 collective-permute-done.14
  321.4 4.0 convolution_select_fusion.2
  326.8 2.1 fusion.236
  330.0 6.8 %collective-permute-start.17 = (f32[32,16,2]{2,0,1:T(8,128)S(1)}, f32[32,16,2]{2,0,1:T(8,128)S(1)}, u32[]{:S(2)}, u32[]{:S(2)}) collective-permute-start(f32[32,16,2]{2,0,1:T(8,128)S(1)} %get-tuple-element.63), channel_id=1, source_target_pairs={{8,0},{16,8},{24,16},{32,24},{40,32},{48,40},{56,48},{64,56},{72,6... | collective-permute-start | bytes 12296 | tf_op jit(solution)/shard_map/ppermute | solution.py:22
  343.2 1.8 add.262
  348.6 2.4 collective-permute-done.18
  352.6 2.6 convolution_select_fusion.1
  365.0 2.5 collective-permute-start.21
  368.8 2.1 collective-permute-done.21
  375.1 2.7 collective-permute-done.22
  378.9 4.0 convolution_select_fusion
  385.4 132.5 %all-reduce.3.cloned.1.call-done = (f32[64,32,5,5]{0,1,3,2:T(8,128)}, f32[32,64,5,5]{1,0,3,2:T(8,128)}) async-done(((f32[64,32,5,5]{0,1,3,2:T(8,128)}, f32[32,64,5,5]{1,0,3,2:T(8,128)}), (f32[64,32,5,5]{0,1,3,2:T(8,128)}, f32[32,64,5,5]{1,0,3,2:T(8,128)})) %all-reduce.3.cloned.1.call-update) | async-done | bytes 409616 | tf_op jit(solution)/shard_map/psum | solution.py:146
  517.9 1.8 copy.423
  519.7 1.8 copy.424
  (333 shorter events, 98.8 us)
Async XLA Ops:
  7.2 78.3 %copy-start = (bf16[64,32,5,5]{0,1,3,2:T(8,128)(2,1)S(1)}, bf16[64,32,5,5]{0,1,3,2:T(8,128)(2,1)}, u32[]{:S(2)}) copy-start(bf16[64,32,5,5]{0,1,3,2:T(8,128)(2,1)} %param.12) | copy-start | bytes 307204
  7.2 5.7 %copy-start.21 = (s32[1,128]{1,0:T(1,128)S(1)}, s32[1,128]{1,0:T(1,128)}, u32[]{:S(2)}) copy-start(s32[1,128]{1,0:T(1,128)} %param.11) | copy-start | bytes 1540
  7.2 6.0 %copy-start.1 = (s32[1024]{0:T(1024)S(1)}, s32[1024]{0:T(1024)}, u32[]{:S(2)}) copy-start(s32[1024]{0:T(1024)} %param.10) | copy-start | bytes 12292
  9.1 61.1 %collective-permute-start.1 = (f32[32,16,4]{2,0,1:T(8,128)}, f32[32,16,4]{2,0,1:T(8,128)S(1)}, u32[]{:S(2)}, u32[]{:S(2)}) collective-permute-start(f32[32,16,4]{2,0,1:T(8,128)} %get-tuple-element.71), channel_id=1, source_target_pairs={{8,0},{16,8},{24,16},{32,24},{40,32},{48,40},{56,48},{64,56},{72,6... | collective-permute-start | bytes 24584 | tf_op jit(solution)/shard_map/ppermute | solution.py:22
  10.5 59.7 %collective-permute-start = (f32[32,16,4]{2,0,1:T(8,128)}, f32[32,16,4]{2,0,1:T(8,128)}, u32[]{:S(2)}, u32[]{:S(2)}) collective-permute-start(f32[32,16,4]{2,0,1:T(8,128)} %get-tuple-element.70), channel_id=1, source_target_pairs={{0,8},{8,16},{16,24},{24,32},{32,40},{40,48},{48,56},{56,64},{64,7... | collective-permute-start | bytes 24584 | tf_op jit(solution)/shard_map/ppermute | solution.py:20
  29.9 2.2 copy-start.16
  51.7 18.5 %copy-start.20 = (s32[16,128]{1,0:T(8,128)S(1)}, s32[16,128]{1,0:T(8,128)}, u32[]{:S(2)}) copy-start(s32[16,128]{1,0:T(8,128)} %param.8) | copy-start | bytes 24580
  56.3 74.2 %all-to-all-start = ((f32[128,1,1056]{2,1,0:T(1,128)}), f32[128,1,1056]{2,1,0:T(1,128)}, u32[]{:S(2)}, u32[]{:S(2)}) async-start(f32[128,1,1056]{2,1,0:T(1,128)} %reshape.790), calls=%async_computation | async-start | bytes 1179648 | tf_op jit(solution)/shard_map/all_to_all | solution.py:116
  70.1 447.8 %all-reduce.3.cloned.1.call-start = ((), (), s32[]{:S(2)}) async-start(), calls=%async_computation.1 | async-start | bytes 1638400 | tf_op jit(solution)/shard_map/psum | solution.py:146
  70.3 14.6 %copy-start.4 = (f32[32,16,4]{2,0,1:T(8,128)}, f32[32,16,4]{2,0,1:T(8,128)S(1)}, u32[]{:S(2)}) copy-start(f32[32,16,4]{2,0,1:T(8,128)S(1)} %collective-permute-done.1) | copy-start | bytes 24580
  71.6 10.7 %collective-permute-start.3 = (f32[32,4,136]{2,0,1:T(8,128)S(1)}, f32[32,4,136]{2,0,1:T(8,128)S(1)}, u32[]{:S(2)}, u32[]{:S(2)}) collective-permute-start(f32[32,4,136]{2,0,1:T(8,128)S(1)} %get-tuple-element.59), channel_id=1, source_target_pairs={{1,0},{2,1},{3,2},{4,3},{5,4},{6,5},{7,6},{0,7},{9,8},{10,9},{11,1... | collective-permute-start | bytes 208904 | tf_op jit(solution)/shard_map/ppermute | solution.py:22
  75.8 8.2 %collective-permute-start.2 = (f32[32,4,136]{2,0,1:T(8,128)S(1)}, f32[32,4,136]{2,0,1:T(8,128)S(1)}, u32[]{:S(2)}, u32[]{:S(2)}) collective-permute-start(f32[32,4,136]{2,0,1:T(8,128)S(1)} %get-tuple-element.58), channel_id=1, source_target_pairs={{0,1},{1,2},{2,3},{3,4},{4,5},{5,6},{6,7},{7,0},{8,9},{9,10},{10,1... | collective-permute-start | bytes 208904 | tf_op jit(solution)/shard_map/ppermute | solution.py:20
  94.9 1.4 copy-start.11
  94.9 1.4 copy-start.12
  96.9 6.5 %collective-permute-start.5 = (f32[32,16,4]{2,0,1:T(8,128)S(1)}, f32[32,16,4]{2,0,1:T(8,128)S(1)}, u32[]{:S(2)}, u32[]{:S(2)}) collective-permute-start(f32[32,16,4]{2,0,1:T(8,128)S(1)} %get-tuple-element.69), channel_id=1, source_target_pairs={{8,0},{16,8},{24,16},{32,24},{40,32},{48,40},{56,48},{64,56},{72,6... | collective-permute-start | bytes 24584 | tf_op jit(solution)/shard_map/ppermute | solution.py:22
  98.9 4.6 collective-permute-start.4
  103.8 4.2 collective-permute-start.7
  104.5 6.1 %collective-permute-start.6 = (f32[32,4,136]{2,0,1:T(8,128)S(1)}, f32[32,4,136]{2,0,1:T(8,128)S(1)}, u32[]{:S(2)}, u32[]{:S(2)}) collective-permute-start(f32[32,4,136]{2,0,1:T(8,128)S(1)} %get-tuple-element.56), channel_id=1, source_target_pairs={{0,1},{1,2},{2,3},{3,4},{4,5},{5,6},{6,7},{7,0},{8,9},{9,10},{10,1... | collective-permute-start | bytes 208904 | tf_op jit(solution)/shard_map/ppermute | solution.py:20
  114.4 5.2 copy-start.3
  114.4 1.2 copy-start.23
  160.7 5.6 %copy-start.2 = (f32[4096,32]{1,0:T(8,128)S(1)}, f32[4096,32]{1,0:T(8,128)}, u32[]{:S(2)}) copy-start(f32[4096,32]{1,0:T(8,128)} %gather_fusion.2) | copy-start | bytes 1572868
  198.6 83.4 %collective-permute-start.9 = (f32[32,16,2]{2,0,1:T(8,128)}, f32[32,16,2]{2,0,1:T(8,128)S(1)}, u32[]{:S(2)}, u32[]{:S(2)}) collective-permute-start(f32[32,16,2]{2,0,1:T(8,128)} %get-tuple-element.67), channel_id=1, source_target_pairs={{8,0},{16,8},{24,16},{32,24},{40,32},{48,40},{56,48},{64,56},{72,6... | collective-permute-start | bytes 12296 | tf_op jit(solution)/shard_map/ppermute | solution.py:22
  206.4 75.6 %collective-permute-start.8 = (f32[32,16,2]{2,0,1:T(8,128)S(1)}, f32[32,16,2]{2,0,1:T(8,128)S(1)}, u32[]{:S(2)}, u32[]{:S(2)}) collective-permute-start(f32[32,16,2]{2,0,1:T(8,128)S(1)} %get-tuple-element.66), channel_id=1, source_target_pairs={{0,8},{8,16},{16,24},{24,32},{32,40},{40,48},{48,56},{56,64},{64,7... | collective-permute-start | bytes 12296 | tf_op jit(solution)/shard_map/ppermute | solution.py:20
  212.7 76.1 %copy-start.17 = (f32[32,64,5]{1,0,2:T(8,128)}, f32[32,64,5]{1,0,2:T(8,128)S(1)}, u32[]{:S(2)}) copy-start(f32[32,64,5]{1,0,2:T(8,128)S(1)} %convolution_dynamic-update-slice_fusion.25) | copy-start | bytes 122884
  282.0 6.8 %copy-start.6 = (f32[32,16,2]{2,0,1:T(8,128)}, f32[32,16,2]{2,0,1:T(8,128)S(1)}, u32[]{:S(2)}) copy-start(f32[32,16,2]{2,0,1:T(8,128)S(1)} %collective-permute-done.9) | copy-start | bytes 12292
  282.0 6.8 %copy-start.8 = (f32[32,16,2]{2,0,1:T(8,128)}, f32[32,16,2]{2,0,1:T(8,128)S(1)}, u32[]{:S(2)}) copy-start(f32[32,16,2]{2,0,1:T(8,128)S(1)} %collective-permute-done.8) | copy-start | bytes 12292
  282.3 3.2 collective-permute-start.11
  283.6 5.2 collective-permute-start.10
  291.2 0.9 copy-start.24
  304.0 4.5 copy-start.7
  304.0 4.5 copy-start.9
  305.8 6.6 %collective-permute-start.13 = (bf16[64,16,2]{2,0,1:T(8,128)(2,1)S(1)}, bf16[64,16,2]{2,0,1:T(8,128)(2,1)S(1)}, u32[]{:S(2)}, u32[]{:S(2)}) collective-permute-start(bf16[64,16,2]{2,0,1:T(8,128)(2,1)S(1)} %get-tuple-element.65), channel_id=1, source_target_pairs={{8,0},{16,8},{24,16},{32,24},{40,32},{48,40},{56,48},{64,56},{72,6... | collective-permute-start | bytes 12296 | tf_op jit(solution)/shard_map/ppermute | solution.py:22
  307.9 4.5 collective-permute-start.12
  308.8 6.0 %copy-start.13 = (f32[64,32,5,5]{0,1,3,2:T(8,128)}, f32[64,32,5,5]{0,1,3,2:T(8,128)S(1)}, u32[]{:S(2)}) copy-start(f32[64,32,5,5]{0,1,3,2:T(8,128)S(1)} %constant_dynamic-update-slice_fusion) | copy-start | bytes 614404
  312.8 3.5 collective-permute-start.15
  312.9 5.5 %collective-permute-start.14 = (bf16[64,2,132]{2,0,1:T(8,128)(2,1)S(1)}, bf16[64,2,132]{2,0,1:T(8,128)(2,1)S(1)}, u32[]{:S(2)}, u32[]{:S(2)}) collective-permute-start(bf16[64,2,132]{2,0,1:T(8,128)(2,1)S(1)} %get-tuple-element.52), channel_id=1, source_target_pairs={{0,1},{1,2},{2,3},{3,4},{4,5},{5,6},{6,7},{7,0},{8,9},{9,10},{10,1... | collective-permute-start | bytes 101384 | tf_op jit(solution)/shard_map/ppermute | solution.py:20
  325.6 1.2 copy-start.5
  330.0 15.0 %collective-permute-start.17 = (f32[32,16,2]{2,0,1:T(8,128)S(1)}, f32[32,16,2]{2,0,1:T(8,128)S(1)}, u32[]{:S(2)}, u32[]{:S(2)}) collective-permute-start(f32[32,16,2]{2,0,1:T(8,128)S(1)} %get-tuple-element.63), channel_id=1, source_target_pairs={{8,0},{16,8},{24,16},{32,24},{40,32},{48,40},{56,48},{64,56},{72,6... | collective-permute-start | bytes 12296 | tf_op jit(solution)/shard_map/ppermute | solution.py:22
  336.9 8.2 %collective-permute-start.16 = (f32[32,16,2]{2,0,1:T(8,128)S(1)}, f32[32,16,2]{2,0,1:T(8,128)S(1)}, u32[]{:S(2)}, u32[]{:S(2)}) collective-permute-start(f32[32,16,2]{2,0,1:T(8,128)S(1)} %get-tuple-element.62), channel_id=1, source_target_pairs={{0,8},{8,16},{16,24},{24,32},{32,40},{40,48},{48,56},{56,64},{64,7... | collective-permute-start | bytes 12296 | tf_op jit(solution)/shard_map/ppermute | solution.py:20
  340.5 2.0 copy-start.18
  345.4 3.2 collective-permute-start.19
  345.5 5.5 %collective-permute-start.18 = (f32[32,2,132]{2,0,1:T(8,128)S(1)}, f32[32,2,132]{2,0,1:T(8,128)S(1)}, u32[]{:S(2)}, u32[]{:S(2)}) collective-permute-start(f32[32,2,132]{2,0,1:T(8,128)S(1)} %get-tuple-element.50), channel_id=1, source_target_pairs={{0,1},{1,2},{2,3},{3,4},{4,5},{5,6},{6,7},{7,0},{8,9},{9,10},{10,1... | collective-permute-start | bytes 101384 | tf_op jit(solution)/shard_map/ppermute | solution.py:20
  363.2 4.4 copy-start.14
  365.0 5.9 %collective-permute-start.21 = (bf16[64,16,2]{2,0,1:T(8,128)(2,1)S(1)}, bf16[64,16,2]{2,0,1:T(8,128)(2,1)S(1)}, u32[]{:S(2)}, u32[]{:S(2)}) collective-permute-start(bf16[64,16,2]{2,0,1:T(8,128)(2,1)S(1)} %get-tuple-element.61), channel_id=1, source_target_pairs={{8,0},{16,8},{24,16},{32,24},{40,32},{48,40},{56,48},{64,56},{72,6... | collective-permute-start | bytes 12296 | tf_op jit(solution)/shard_map/ppermute | solution.py:22
  367.5 4.0 collective-permute-start.20
  371.9 3.2 collective-permute-start.23
  372.0 5.8 %collective-permute-start.22 = (bf16[64,2,132]{2,0,1:T(8,128)(2,1)S(1)}, bf16[64,2,132]{2,0,1:T(8,128)(2,1)S(1)}, u32[]{:S(2)}, u32[]{:S(2)}) collective-permute-start(bf16[64,2,132]{2,0,1:T(8,128)(2,1)S(1)} %get-tuple-element.48), channel_id=1, source_target_pairs={{0,1},{1,2},{2,3},{3,4},{4,5},{5,6},{6,7},{7,0},{8,9},{9,10},{10,1... | collective-permute-start | bytes 101384 | tf_op jit(solution)/shard_map/ppermute | solution.py:20
  383.2 1.0 copy-start.10
  (5 other events, 4.1 us)
Sparse Core Ops, SparseCore 0:
  368.6 149.3 all-reduce.2
where the time goes:
time: 537 us; the launch traced here: 530 us
  waiting for transfers between devices  168 us (31%)
  local copies, waits for them, and re-layouts  106 us (20%)
  blocking collectives  66.7 us (12%)
  other arithmetic  66.3 us (12%)
  matrix products  53.4 us (10%)
  starting transfers between devices  52 us (10%)
  between operations  17.4 us (3%)
    psum x1, waiting for transfers between devices, on_device(): lax.psum((grad_in, grad_out, square_sum), ('lon', 'lat'))  133 us
    psum x1, blocking collectives, on_device(): lax.psum((grad_in, grad_out, square_sum), ('lon', 'lat'))  66.7 us
    unnamed x91, local copies, waits for them, and re-layouts  40.6 us
    ppermute x12, starting transfers between devices, extended_2(): lax.ppermute(head, axis, [((i + 1) % count, i) for i in range(count)])  29.1 us
    conv_general_dilated x8, matrix products, conv_valid(): lax.conv_general_dilated(padded[None], kernel, (1, 1), 'VALID', dimension...  27.3 us
    dot_general x100, matrix products, kernel_grad(): jnp.einsum('ohw,chw->oc', cotangent, window, preferred_element_type=jnp.f...  26.1 us
    scatter-add x1, other arithmetic, on_device(): tangent = jnp.zeros((levels, cell_count), jnp.float32).at[:, target].add(...  25.6 us
    ppermute x12, waiting for transfers between devices, extended_2(): lax.ppermute(head, axis, [((i + 1) % count, i) for i in range(count)])  19.4 us
  transfers between devices with their start and end apart: 26, of which 17 were waited for; matrix products, arithmetic and copies ran while one was open for 20% of the time, Pallas kernels for 0%

commit v1 on v0

--- a/solution.py
+++ b/solution.py
@@ -76,6 +76,24 @@
     return jnp.stack(stripes, axis=-2)
 
 
+def all_sum(parts, axes):
+    count = 1
+    for axis in axes:
+        count *= lax.axis_size(axis)
+    flat = jnp.concatenate([part.reshape(-1) for part in parts])
+    size = flat.shape[0]
+    chunk = -(-size // count)
+    rows = jnp.pad(flat, (0, chunk * count - size)).reshape(count, chunk)
+    mine = jnp.sum(lax.all_to_all(rows, axes, 0, 0, tiled=True), axis=0)
+    spread = lax.all_to_all(jnp.broadcast_to(mine[None], (count, chunk)), axes, 0, 0, tiled=True)
+    flat = spread.reshape(-1)
+    sums, offset = [], 0
+    for part in parts:
+        sums.append(flat[offset : offset + part.size].reshape(part.shape))
+        offset += part.size
+    return tuple(sums)
+
+
 def inside_rows(tile_rows, border):
     first_row = lax.axis_index("lat") * tile_rows
     global_rows = first_row + jnp.arange(-border, tile_rows + border, dtype=jnp.int32)
@@ -143,7 +161,7 @@
             tile_rows, 2
         ).astype(jnp.bfloat16)
         tangent = tangent + diffusion * laplace(beside_all, 2) + conv_valid(margin, back_in)
-    grad_in, grad_out, square_sum = lax.psum((grad_in, grad_out, square_sum), ("lon", "lat"))
+    grad_in, grad_out, square_sum = all_sum((grad_in, grad_out, square_sum), ("lon", "lat"))
     misfit = square_sum / (2.0 * profile_dev * devices * levels)
     return (current, misfit, grad_in, grad_out, tangent * profile_dev)
 

time: 537 us -> 397 us (0.74)
  waiting for transfers between devices: 168 us -> 46.6 us
  blocking collectives: 66.7 us -> 0 us
  local copies, waits for them, and re-layouts: 106 us -> 145 us
  starting transfers between devices: 52 us -> 74 us
  between operations: 17.4 us -> 4.08 us
    psum x1 -> x0, waiting for transfers between devices: 133 us -> none  [on_device(): lax.psum((grad_in, grad_out, square_sum), ('lon', 'lat'))]
    psum x1 -> x0, blocking collectives: 66.7 us -> none  [on_device(): lax.psum((grad_in, grad_out, square_sum), ('lon', 'lat'))]
    add x0 -> x4, local copies, waits for them, and re-layouts: none -> 22.4 us  [the longest x2 12.6 us: on_device(): grad_in = grad_in + kernel_grad(coarse, sensitivity)]
    all_to_all x0 -> x2, starting transfers between devices: none -> 16.7 us  [the longest x1 9.68 us: all_sum(): lax.all_to_all(jnp.broadcast_to(mine[None], (count, chunk)), axes, 0, 0,...]
    reshape x0 -> x3, local copies, waits for them, and re-layouts: none -> 9.17 us  [the longest x2 8.84 us: all_sum(): sums.append(flat[offset:offset + part.size].reshape(part.shape))]
    all_to_all x0 -> x2, waiting for transfers between devices: none -> 6.65 us  [the longest x1 6.64 us: all_sum(): lax.all_to_all(jnp.broadcast_to(mine[None], (count, chunk)), axes, 0, 0,...]
    ppermute x12, starting transfers between devices: 29.1 us -> 34.7 us  [extended_2(): lax.ppermute(head, axis, [((i + 1) % count, i) for i in range(count)])]
    unnamed x91 -> x109, local copies, waits for them, and re-layouts: 40.6 us -> 45.8 us
  transfers between devices with their start and end apart: 26 -> 27, of which waited for: 17 -> 17; matrix products, arithmetic and copies ran while one was open for 20% -> 27% of each run, Pallas kernels for 0% -> 0%
where the time goes in v1:
time: 397 us; the launch traced here: 389 us
  local copies, waits for them, and re-layouts  145 us (37%)
  starting transfers between devices  74 us (19%)
  other arithmetic  65.9 us (17%)
  matrix products  53.4 us (13%)
  waiting for transfers between devices  46.6 us (12%)
  between operations  4.08 us (1%)
    unnamed x109, local copies, waits for them, and re-layouts  45.8 us
    ppermute x12, starting transfers between devices, extended_2(): lax.ppermute(head, axis, [((i + 1) % count, i) for i in range(count)])  34.7 us
    conv_general_dilated x8, matrix products, conv_valid(): lax.conv_general_dilated(padded[None], kernel, (1, 1), 'VALID', dimension...  27.3 us
    dot_general x100, matrix products, kernel_grad(): jnp.einsum('ohw,chw->oc', cotangent, window, preferred_element_type=jnp.f...  26.1 us
    scatter-add x1, other arithmetic, on_device(): tangent = jnp.zeros((levels, cell_count), jnp.float32).at[:, target].add(...  25.7 us
    ppermute x12, waiting for transfers between devices, extended_2(): lax.ppermute(head, axis, [((i + 1) % count, i) for i in range(count)])  22.2 us
    ppermute x12, waiting for transfers between devices, extended_2(): lax.ppermute(tail, axis, [(i, (i + 1) % count) for i in range(count)])  17.8 us
    gather x3, local copies, waits for them, and re-layouts, on_device(): jnp.take(profile_cells, picked)[None, :]  16.8 us
  transfers between devices with their start and end apart: 27, of which 17 were waited for; matrix products, arithmetic and copies ran while one was open for 27% of the time, Pallas kernels for 0%

profile of v1, /device:TPU:1, one launch (start us, length us, event | category | flops | bytes accessed | tf_op | source)
XLA Modules:
  0.0 389.4 jit_solution(1752695489584638763)
XLA Ops:
  6.6 16.7 %gather_fusion.1 = s32[4096]{0:T(1024)S(1)} fusion(s32[1024]{0:T(1024)S(1)} %copy-done.1, s32[4096]{0:T(1024)S(1)} %broadcast_clamp_fusion.1), kind=kCustom, calls=%fused_computation.1 | custom fusion | bytes 49152 | tf_op jit(solution)/shard_map/jit(_take)/gather | solution.py:130
  25.7 14.1 %gather_fusion = f32[4096,32]{1,0:T(8,128)} fusion(f32[32,1024]{0,1:T(8,128)S(1)} %copy.286, s32[4096]{0:T(1024)S(1)} %broadcast_clamp_fusion.1), kind=kCustom, calls=%fused_computation | custom fusion | bytes 1064960 | tf_op jit(solution)/shard_map/jit(_take)/gather | solution.py:129
  39.9 3.2 select_select_fusion
  45.1 4.6 %reshape.829 = f32[128,1,1056]{2,1,0:T(1,128)} reshape(f32[128,32,33]{2,1,0:T(8,128)} %fusion.255) | data formatting | bytes 1081344
  49.7 13.8 %all-to-all-start = ((f32[128,1,1056]{2,1,0:T(1,128)}), f32[128,1,1056]{2,1,0:T(1,128)}, u32[]{:S(2)}, u32[]{:S(2)}) async-start(f32[128,1,1056]{2,1,0:T(1,128)} %reshape.829), calls=%async_computation | async-start | bytes 1179648 | tf_op jit(solution)/shard_map/all_to_all | solution.py:134
  64.9 4.2 %collective-permute-start.3 = (f32[32,4,136]{2,0,1:T(8,128)S(1)}, f32[32,4,136]{2,0,1:T(8,128)S(1)}, u32[]{:S(2)}, u32[]{:S(2)}) collective-permute-start(f32[32,4,136]{2,0,1:T(8,128)S(1)} %get-tuple-element.57), channel_id=1, source_target_pairs={{1,0},{2,1},{3,2},{4,3},{5,4},{6,5},{7,6},{0,7},{9,8},{10,9},{11,1... | collective-permute-start | bytes 208904 | tf_op jit(solution)/shard_map/ppermute | solution.py:22
  70.8 4.8 %collective-permute-done.3 = f32[32,4,136]{2,0,1:T(8,128)S(1)} collective-permute-done((f32[32,4,136]{2,0,1:T(8,128)S(1)}, f32[32,4,136]{2,0,1:T(8,128)S(1)}, u32[]{:S(2)}, u32[]{:S(2)}) %collective-permute-start.3) | collective-permute-done | bytes 69664 | tf_op jit(solution)/shard_map/ppermute | solution.py:22
  78.8 3.0 select_tanh_fusion.1
  82.8 4.0 %fusion.26 = f32[16,8,17,32]{3,1,2,0:T(8,128)S(1)} fusion(bf16[32,64,5,5]{1,0,3,2:T(8,128)(2,1)S(1)} %copy-done.29, bf16[20,1,7,4,64]{4,2,3,0,1:T(8,128)(2,1)S(1)} %slice.693, bf16[20,1,8,17,64]{4,2,3,0,1:T(8,128)(2,1)S(1)} %fusion.65), kind=kOutput, calls=%fused_computation.147 | convolution fusion | flops 224112640 | bytes 800768 | tf_op jit(solution)/shard_map/conv_general_dilated | solution.py:50
  99.0 2.2 collective-permute-done.7
  101.2 2.7 collective-permute-done.6
  104.7 3.0 select_tanh_fusion
  108.9 4.0 %fusion.30 = f32[16,8,17,32]{3,1,2,0:T(8,128)S(1)} fusion(bf16[32,64,5,5]{1,0,3,2:T(8,128)(2,1)S(1)} %copy-done.30, bf16[20,1,7,4,64]{4,2,3,0,1:T(8,128)(2,1)S(1)} %slice.705, bf16[20,1,8,17,64]{4,2,3,0,1:T(8,128)(2,1)S(1)} %fusion.67), kind=kOutput, calls=%fused_computation.150 | convolution fusion | flops 224112640 | bytes 800768 | tf_op jit(solution)/shard_map/conv_general_dilated | solution.py:50
  118.6 3.3 copy.339
  121.8 2.1 multiply_convert_fusion.2
  124.4 3.9 %reduce.4 = f32[128,1056]{1,0:T(8,128)} reduce(f32[128,1,1056]{2,1,0:T(1,128)} %all-to-all-done, f32[]{:T(128)} %broadcast.529), dimensions={1}, to_apply=%all_to_all.14.reduce_sub_computation | reduce | bytes 1081348 | tf_op jit(solution)/shard_map/all_to_all | solution.py:134
  128.4 4.8 %reshape.830 = f32[128,32,33]{2,1,0:T(8,128)} reshape(f32[128,1056]{1,0:T(8,128)} %reduce.4) | data formatting | bytes 1081344
  133.1 3.5 slice.707
  136.7 2.7 copy.337
  140.0 14.1 %gather_fusion.2 = f32[4096,32]{1,0:T(8,128)} fusion(f32[32,2048]{0,1:T(8,128)S(1)} %bitcast.394, s32[4096]{0:T(1024)S(1)} %broadcast_clamp_fusion), kind=kCustom, calls=%fused_computation.2 | custom fusion | bytes 1064960 | tf_op jit(solution)/shard_map/jit(_take)/gather | solution.py:140
  154.0 5.6 %fusion.241 = (f32[32,128,32]{0,2,1:T(8,128)S(1)}, f32[]{:T(128)}) fusion(f32[33,128,32]{0,2,1:T(8,128)} %bitcast.396, f32[32,128,32]{0,2,1:T(8,128)} %bitcast.397, pred[128,32]{1,0:T(8,128)(4,1)S(1)} %copy.319, pred[128,32]{1,0:T(8,128)(4,1)S(1)} %copy.318), kind=kLoop, calls=%fused_computation.436 | loop fusion | flops 655359 | bytes 1581060 | tf_op jit(solution)/shard_map/slice | solution.py:135
  159.7 2.8 fusion.3
  162.5 25.7 %scatter_custom_fusion = f32[32,2048]{0,1:T(8,128)S(1)} fusion(s32[4096]{0:T(1024)S(1)} %bitcast.429, f32[32,4096]{0,1:T(8,128)} %fusion.3, f32[]{:T(128)} %constant.40.clone.1), kind=kCustom, calls=%fused_computation.5 | custom fusion | flops 131072 | bytes 786436 | tf_op jit(solution)/shard_map/scatter-add | solution.py:145
  197.1 7.5 %collective-permute-start.9 = (f32[32,16,2]{2,0,1:T(8,128)S(1)}, f32[32,16,2]{2,0,1:T(8,128)S(1)}, u32[]{:S(2)}, u32[]{:S(2)}) collective-permute-start(f32[32,16,2]{2,0,1:T(8,128)S(1)} %get-tuple-element.67), channel_id=1, source_target_pairs={{8,0},{16,8},{24,16},{32,24},{40,32},{48,40},{56,48},{64,56},{72,6... | collective-permute-start | bytes 12296 | tf_op jit(solution)/shard_map/ppermute | solution.py:22
  205.8 2.2 collective-permute-done.8
  211.7 2.5 collective-permute-done.10
  217.6 2.6 convolution_select_fusion.3
  225.9 7.7 %collective-permute-start.13 = (bf16[64,16,2]{2,0,1:T(8,128)(2,1)S(1)}, bf16[64,16,2]{2,0,1:T(8,128)(2,1)S(1)}, u32[]{:S(2)}, u32[]{:S(2)}) collective-permute-start(bf16[64,16,2]{2,0,1:T(8,128)(2,1)S(1)} %get-tuple-element.65), channel_id=1, source_target_pairs={{8,0},{16,8},{24,16},{32,24},{40,32},{48,40},{56,48},{64,56},{72,6... | collective-permute-start | bytes 12296 | tf_op jit(solution)/shard_map/ppermute | solution.py:22
  243.1 2.3 collective-permute-done.14
  248.4 4.0 %convolution_select_fusion.2 = f32[16,8,17,32]{3,1,2,0:T(8,128)S(1)} fusion(bf16[64,32,5,5]{0,1,3,2:T(8,128)(2,1)S(1)} %copy-done, bf16[64,20,1,7,4]{0,3,4,1,2:T(8,128)(2,1)S(1)} %slice.751, bf16[64,20,1,8,17]{0,3,4,1,2:T(8,128)(2,1)S(1)} %copy.306, pred[8,17]{0,1:T(8,128)(4,1)S(1)} %copy-done.33), kind=kOutput, calls=%fused_computation.31 | convolution fusion | flops 224182272 | bytes 800904 | tf_op jit(solution)/shard_map/conv_general_dilated | solution.py:50
  262.8 5.5 %collective-permute-start.17 = (f32[32,16,2]{2,0,1:T(8,128)S(1)}, f32[32,16,2]{2,0,1:T(8,128)S(1)}, u32[]{:S(2)}, u32[]{:S(2)}) collective-permute-start(f32[32,16,2]{2,0,1:T(8,128)S(1)} %get-tuple-element.63), channel_id=1, source_target_pairs={{8,0},{16,8},{24,16},{32,24},{40,32},{48,40},{56,48},{64,56},{72,6... | collective-permute-start | bytes 12296 | tf_op jit(solution)/shard_map/ppermute | solution.py:22
  268.5 4.8 %copy.317 = f32[32,64,5,5]{3,2,1,0:T(8,128)} copy(f32[32,64,5,5]{1,0,3,2:T(8,128)S(1)} %add.266) | data formatting | bytes 409600 | tf_op jit(solution)/shard_map/add | solution.py:154
  273.3 5.0 %add.267 = f32[51200]{0:T(1024)S(1)} reshape(f32[32,64,5,5]{3,2,1,0:T(8,128)} %copy.317) | data formatting | bytes 409600 | tf_op jit(solution)/shard_map/add | solution.py:154
  281.8 2.6 collective-permute-done.18
  286.0 2.6 convolution_select_fusion.1
  298.4 7.6 %copy.316 = f32[64,32,5,5]{3,2,1,0:T(8,128)} copy(f32[64,32,5,5]{0,1,3,2:T(8,128)S(1)} %add.264) | data formatting | bytes 409600 | tf_op jit(solution)/shard_map/add | solution.py:159
  306.0 5.0 %add.265 = f32[51200]{0:T(1024)S(1)} reshape(f32[64,32,5,5]{3,2,1,0:T(8,128)} %copy.316) | data formatting | bytes 409600 | tf_op jit(solution)/shard_map/add | solution.py:159
  313.2 7.1 %all-to-all-start.1 = ((f32[128,1,801]{2,1,0:T(1,128)}), f32[128,1,801]{2,1,0:T(1,128)S(1)}, u32[]{:S(2)}, u32[]{:S(2)}) async-start(f32[128,1,801]{2,1,0:T(1,128)} %all_to_all.18), calls=%async_computation.1 | async-start | bytes 917504 | tf_op jit(solution)/shard_map/all_to_all | solution.py:87
  322.5 7.6 %collective-permute-done.21 = bf16[64,16,2]{2,0,1:T(8,128)(2,1)S(1)} collective-permute-done((bf16[64,16,2]{2,0,1:T(8,128)(2,1)}, bf16[64,16,2]{2,0,1:T(8,128)(2,1)S(1)}, u32[]{:S(2)}, u32[]{:S(2)}) %collective-permute-start.21) | collective-permute-done | bytes 4128 | tf_op jit(solution)/shard_map/ppermute | solution.py:22
  330.4 3.9 %collective-permute-start.23 = (bf16[64,2,132]{2,0,1:T(8,128)(2,1)S(1)}, bf16[64,2,132]{2,0,1:T(8,128)(2,1)S(1)}, u32[]{:S(2)}, u32[]{:S(2)}) collective-permute-start(bf16[64,2,132]{2,0,1:T(8,128)(2,1)S(1)} %get-tuple-element.47), channel_id=1, source_target_pairs={{1,0},{2,1},{3,2},{4,3},{5,4},{6,5},{7,6},{0,7},{9,8},{10,9},{11,1... | collective-permute-start | bytes 101384 | tf_op jit(solution)/shard_map/ppermute | solution.py:22
  335.7 3.9 collective-permute-done.22
  342.1 9.7 %all-to-all-start.2 = ((f32[128,1,801]{2,1,0:T(1,128)}), f32[128,1,801]{2,1,0:T(1,128)S(1)}, u32[]{:S(2)}, u32[]{:S(2)}) async-start(f32[128,1,801]{2,1,0:T(1,128)} %broadcast_in_dim.114), calls=%async_computation.2 | async-start | bytes 917504 | tf_op jit(solution)/shard_map/all_to_all | solution.py:88
  351.8 4.0 %convolution_select_fusion = f32[16,8,17,32]{3,1,2,0:T(8,128)S(1)} fusion(bf16[64,32,5,5]{0,1,3,2:T(8,128)(2,1)S(1)} %copy-done, bf16[64,20,1,7,4]{0,3,4,1,2:T(8,128)(2,1)S(1)} %slice.848, bf16[64,20,1,8,17]{0,3,4,1,2:T(8,128)(2,1)S(1)} %copy.323, pred[8,17]{0,1:T(8,128)(4,1)S(1)} %copy-done.35), kind=kOutput, calls=%fused_computation.29 | convolution fusion | flops 224182272 | bytes 800904 | tf_op jit(solution)/shard_map/conv_general_dilated | solution.py:50
  358.2 6.6 %all-to-all-done.2 = f32[128,1,801]{2,1,0:T(1,128)S(1)} async-done(((f32[128,1,801]{2,1,0:T(1,128)}), f32[128,1,801]{2,1,0:T(1,128)S(1)}, u32[]{:S(2)}, u32[]{:S(2)}) %all-to-all-start.2) | async-done | bytes 410144 | tf_op jit(solution)/shard_map/all_to_all | solution.py:88
  366.8 4.4 %reshape.611 = f32[64,32,5,5]{3,2,1,0:T(8,128)} reshape(f32[51200]{0:T(1024)S(1)} %get-tuple-element.59) | data formatting | bytes 409600 | tf_op jit(solution)/shard_map/reshape | solution.py:92
  371.3 6.2 %copy.327 = f32[64,32,5,5]{0,1,3,2:T(8,128)} copy(f32[64,32,5,5]{3,2,1,0:T(8,128)} %reshape.611) | data formatting | bytes 409600
  377.4 4.4 %reshape.612 = f32[32,64,5,5]{3,2,1,0:T(8,128)} reshape(f32[51200]{0:T(1024)S(1)} %get-tuple-element.58) | data formatting | bytes 409600 | tf_op jit(solution)/shard_map/reshape | solution.py:92
  381.8 5.6 %copy.328 = f32[32,64,5,5]{1,0,3,2:T(8,128)} copy(f32[32,64,5,5]{3,2,1,0:T(8,128)} %reshape.612) | data formatting | bytes 409600
  (365 shorter events, 111.2 us)
Async XLA Ops:
  0.6 78.1 %copy-start = (bf16[64,32,5,5]{0,1,3,2:T(8,128)(2,1)S(1)}, bf16[64,32,5,5]{0,1,3,2:T(8,128)(2,1)}, u32[]{:S(2)}) copy-start(bf16[64,32,5,5]{0,1,3,2:T(8,128)(2,1)} %param.12) | copy-start | bytes 307204
  0.6 5.7 %copy-start.26 = (s32[1,128]{1,0:T(1,128)S(1)}, s32[1,128]{1,0:T(1,128)}, u32[]{:S(2)}) copy-start(s32[1,128]{1,0:T(1,128)} %param.11) | copy-start | bytes 1540
  0.7 6.0 %copy-start.1 = (s32[1024]{0:T(1024)S(1)}, s32[1024]{0:T(1024)}, u32[]{:S(2)}) copy-start(s32[1024]{0:T(1024)} %param.10) | copy-start | bytes 12292
  2.6 60.9 %collective-permute-start.1 = (f32[32,16,4]{2,0,1:T(8,128)}, f32[32,16,4]{2,0,1:T(8,128)S(1)}, u32[]{:S(2)}, u32[]{:S(2)}) collective-permute-start(f32[32,16,4]{2,0,1:T(8,128)} %get-tuple-element.71), channel_id=1, source_target_pairs={{8,0},{16,8},{24,16},{32,24},{40,32},{48,40},{56,48},{64,56},{72,6... | collective-permute-start | bytes 24584 | tf_op jit(solution)/shard_map/ppermute | solution.py:22
  4.0 59.6 %collective-permute-start = (f32[32,16,4]{2,0,1:T(8,128)}, f32[32,16,4]{2,0,1:T(8,128)}, u32[]{:S(2)}, u32[]{:S(2)}) collective-permute-start(f32[32,16,4]{2,0,1:T(8,128)} %get-tuple-element.70), channel_id=1, source_target_pairs={{0,8},{8,16},{16,24},{24,32},{32,40},{40,48},{48,56},{56,64},{64,7... | collective-permute-start | bytes 24584 | tf_op jit(solution)/shard_map/ppermute | solution.py:20
  23.3 2.2 copy-start.18
  45.0 18.5 %copy-start.25 = (s32[16,128]{1,0:T(8,128)S(1)}, s32[16,128]{1,0:T(8,128)}, u32[]{:S(2)}) copy-start(s32[16,128]{1,0:T(8,128)} %param.8) | copy-start | bytes 24580
  49.7 74.2 %all-to-all-start = ((f32[128,1,1056]{2,1,0:T(1,128)}), f32[128,1,1056]{2,1,0:T(1,128)}, u32[]{:S(2)}, u32[]{:S(2)}) async-start(f32[128,1,1056]{2,1,0:T(1,128)} %reshape.829), calls=%async_computation | async-start | bytes 1179648 | tf_op jit(solution)/shard_map/all_to_all | solution.py:134
  63.5 175.4 %copy-start.21 = (f32[20]{0:T(128)}, f32[20]{0:T(128)S(1)}, u32[]{:S(2)}) copy-start(f32[20]{0:T(128)S(1)} %and_convert_fusion) | copy-start | bytes 244
  63.6 14.5 %copy-start.4 = (f32[32,16,4]{2,0,1:T(8,128)}, f32[32,16,4]{2,0,1:T(8,128)S(1)}, u32[]{:S(2)}) copy-start(f32[32,16,4]{2,0,1:T(8,128)S(1)} %collective-permute-done.1) | copy-start | bytes 24580
  64.9 10.7 %collective-permute-start.3 = (f32[32,4,136]{2,0,1:T(8,128)S(1)}, f32[32,4,136]{2,0,1:T(8,128)S(1)}, u32[]{:S(2)}, u32[]{:S(2)}) collective-permute-start(f32[32,4,136]{2,0,1:T(8,128)S(1)} %get-tuple-element.57), channel_id=1, source_target_pairs={{1,0},{2,1},{3,2},{4,3},{5,4},{6,5},{7,6},{0,7},{9,8},{10,9},{11,1... | collective-permute-start | bytes 208904 | tf_op jit(solution)/shard_map/ppermute | solution.py:22
  69.2 8.2 %collective-permute-start.2 = (f32[32,4,136]{2,0,1:T(8,128)S(1)}, f32[32,4,136]{2,0,1:T(8,128)S(1)}, u32[]{:S(2)}, u32[]{:S(2)}) collective-permute-start(f32[32,4,136]{2,0,1:T(8,128)S(1)} %get-tuple-element.56), channel_id=1, source_target_pairs={{0,1},{1,2},{2,3},{3,4},{4,5},{5,6},{6,7},{7,0},{8,9},{9,10},{10,1... | collective-permute-start | bytes 208904 | tf_op jit(solution)/shard_map/ppermute | solution.py:20
  90.2 6.5 %collective-permute-start.5 = (f32[32,16,4]{2,0,1:T(8,128)S(1)}, f32[32,16,4]{2,0,1:T(8,128)S(1)}, u32[]{:S(2)}, u32[]{:S(2)}) collective-permute-start(f32[32,16,4]{2,0,1:T(8,128)S(1)} %get-tuple-element.69), channel_id=1, source_target_pairs={{8,0},{16,8},{24,16},{32,24},{40,32},{48,40},{56,48},{64,56},{72,6... | collective-permute-start | bytes 24584 | tf_op jit(solution)/shard_map/ppermute | solution.py:22
  92.2 4.5 %collective-permute-start.4 = (f32[32,16,4]{2,0,1:T(8,128)S(1)}, f32[32,16,4]{2,0,1:T(8,128)S(1)}, u32[]{:S(2)}, u32[]{:S(2)}) collective-permute-start(f32[32,16,4]{2,0,1:T(8,128)S(1)} %get-tuple-element.68), channel_id=1, source_target_pairs={{0,8},{8,16},{16,24},{24,32},{32,40},{40,48},{48,56},{56,64},{64,7... | collective-permute-start | bytes 24584 | tf_op jit(solution)/shard_map/ppermute | solution.py:20
  92.8 152.6 %copy-start.27 = (bf16[20]{0:T(256)(128)(2,1)}, bf16[20]{0:T(256)(128)(2,1)S(1)}, u32[]{:S(2)}) copy-start(bf16[20]{0:T(256)(128)(2,1)S(1)} %fusion.235) | copy-start | bytes 124
  97.1 4.2 %collective-permute-start.7 = (f32[32,4,136]{2,0,1:T(8,128)S(1)}, f32[32,4,136]{2,0,1:T(8,128)S(1)}, u32[]{:S(2)}, u32[]{:S(2)}) collective-permute-start(f32[32,4,136]{2,0,1:T(8,128)S(1)} %get-tuple-element.55), channel_id=1, source_target_pairs={{1,0},{2,1},{3,2},{4,3},{5,4},{6,5},{7,6},{0,7},{9,8},{10,9},{11,1... | collective-permute-start | bytes 208904 | tf_op jit(solution)/shard_map/ppermute | solution.py:22
  97.9 6.1 %collective-permute-start.6 = (f32[32,4,136]{2,0,1:T(8,128)S(1)}, f32[32,4,136]{2,0,1:T(8,128)S(1)}, u32[]{:S(2)}, u32[]{:S(2)}) collective-permute-start(f32[32,4,136]{2,0,1:T(8,128)S(1)} %get-tuple-element.54), channel_id=1, source_target_pairs={{0,1},{1,2},{2,3},{3,4},{4,5},{5,6},{6,7},{7,0},{8,9},{9,10},{10,1... | collective-permute-start | bytes 208904 | tf_op jit(solution)/shard_map/ppermute | solution.py:20
  107.8 5.2 %copy-start.3 = (f32[20,8,17,64]{3,1,2,0:T(8,128)}, f32[20,8,17,64]{3,1,2,0:T(8,128)S(1)}, u32[]{:S(2)}) copy-start(f32[20,8,17,64]{3,1,2,0:T(8,128)S(1)} %select_tanh_fusion) | copy-start | bytes 2088964
  154.0 5.6 %copy-start.2 = (f32[4096,32]{1,0:T(8,128)S(1)}, f32[4096,32]{1,0:T(8,128)}, u32[]{:S(2)}) copy-start(f32[4096,32]{1,0:T(8,128)} %gather_fusion.2) | copy-start | bytes 1572868
  196.9 13.5 %copy-start.19 = (f32[32,64,5]{1,0,2:T(8,128)}, f32[32,64,5]{1,0,2:T(8,128)S(1)}, u32[]{:S(2)}) copy-start(f32[32,64,5]{1,0,2:T(8,128)S(1)} %convolution_dynamic-update-slice_fusion.25) | copy-start | bytes 122884
  197.1 8.7 %collective-permute-start.9 = (f32[32,16,2]{2,0,1:T(8,128)S(1)}, f32[32,16,2]{2,0,1:T(8,128)S(1)}, u32[]{:S(2)}, u32[]{:S(2)}) collective-permute-start(f32[32,16,2]{2,0,1:T(8,128)S(1)} %get-tuple-element.67), channel_id=1, source_target_pairs={{8,0},{16,8},{24,16},{32,24},{40,32},{48,40},{56,48},{64,56},{72,6... | collective-permute-start | bytes 12296 | tf_op jit(solution)/shard_map/ppermute | solution.py:22
  204.6 3.3 collective-permute-start.8
  205.8 9.3 %copy-start.6 = (f32[32,16,2]{2,0,1:T(8,128)}, f32[32,16,2]{2,0,1:T(8,128)S(1)}, u32[]{:S(2)}) copy-start(f32[32,16,2]{2,0,1:T(8,128)S(1)} %collective-permute-done.9) | copy-start | bytes 12292
  207.9 7.1 %copy-start.8 = (f32[32,16,2]{2,0,1:T(8,128)}, f32[32,16,2]{2,0,1:T(8,128)S(1)}, u32[]{:S(2)}) copy-start(f32[32,16,2]{2,0,1:T(8,128)S(1)} %collective-permute-done.8) | copy-start | bytes 12292
  208.2 3.5 collective-permute-start.11
  208.6 5.6 %collective-permute-start.10 = (f32[32,2,132]{2,0,1:T(8,128)S(1)}, f32[32,2,132]{2,0,1:T(8,128)S(1)}, u32[]{:S(2)}, u32[]{:S(2)}) collective-permute-start(f32[32,2,132]{2,0,1:T(8,128)S(1)} %get-tuple-element.52), channel_id=1, source_target_pairs={{0,1},{1,2},{2,3},{3,4},{4,5},{5,6},{6,7},{7,0},{8,9},{9,10},{10,1... | collective-permute-start | bytes 101384 | tf_op jit(solution)/shard_map/ppermute | solution.py:20
  225.9 13.3 %collective-permute-start.13 = (bf16[64,16,2]{2,0,1:T(8,128)(2,1)S(1)}, bf16[64,16,2]{2,0,1:T(8,128)(2,1)S(1)}, u32[]{:S(2)}, u32[]{:S(2)}) collective-permute-start(bf16[64,16,2]{2,0,1:T(8,128)(2,1)S(1)} %get-tuple-element.65), channel_id=1, source_target_pairs={{8,0},{16,8},{24,16},{32,24},{40,32},{48,40},{56,48},{64,56},{72,6... | collective-permute-start | bytes 12296 | tf_op jit(solution)/shard_map/ppermute | solution.py:22
  233.6 5.7 %collective-permute-start.12 = (bf16[64,16,2]{2,0,1:T(8,128)(2,1)S(1)}, bf16[64,16,2]{2,0,1:T(8,128)(2,1)S(1)}, u32[]{:S(2)}, u32[]{:S(2)}) collective-permute-start(bf16[64,16,2]{2,0,1:T(8,128)(2,1)S(1)} %get-tuple-element.64), channel_id=1, source_target_pairs={{0,8},{8,16},{16,24},{24,32},{32,40},{40,48},{48,56},{56,64},{64,7... | collective-permute-start | bytes 12296 | tf_op jit(solution)/shard_map/ppermute | solution.py:20
  237.0 1.9 copy-start.7
  239.6 3.5 collective-permute-start.15
  240.0 5.4 %collective-permute-start.14 = (bf16[64,2,132]{2,0,1:T(8,128)(2,1)S(1)}, bf16[64,2,132]{2,0,1:T(8,128)(2,1)S(1)}, u32[]{:S(2)}, u32[]{:S(2)}) collective-permute-start(bf16[64,2,132]{2,0,1:T(8,128)(2,1)S(1)} %get-tuple-element.50), channel_id=1, source_target_pairs={{0,1},{1,2},{2,3},{3,4},{4,5},{5,6},{6,7},{7,0},{8,9},{9,10},{10,1... | collective-permute-start | bytes 101384 | tf_op jit(solution)/shard_map/ppermute | solution.py:20
  261.2 7.2 %copy-start.14 = (f32[32,64,5,5]{1,0,3,2:T(8,128)S(1)}, f32[32,64,5,5]{1,0,3,2:T(8,128)}, u32[]{:S(2)}) copy-start(f32[32,64,5,5]{1,0,3,2:T(8,128)} %copy-done.13) | copy-start | bytes 614404
  261.2 7.2 %copy-start.20 = (f32[32,64,5]{1,0,2:T(8,128)S(1)}, f32[32,64,5]{1,0,2:T(8,128)}, u32[]{:S(2)}) copy-start(f32[32,64,5]{1,0,2:T(8,128)} %copy-done.19) | copy-start | bytes 122884
  262.8 15.5 %collective-permute-start.17 = (f32[32,16,2]{2,0,1:T(8,128)S(1)}, f32[32,16,2]{2,0,1:T(8,128)S(1)}, u32[]{:S(2)}, u32[]{:S(2)}) collective-permute-start(f32[32,16,2]{2,0,1:T(8,128)S(1)} %get-tuple-element.63), channel_id=1, source_target_pairs={{8,0},{16,8},{24,16},{32,24},{40,32},{48,40},{56,48},{64,56},{72,6... | collective-permute-start | bytes 12296 | tf_op jit(solution)/shard_map/ppermute | solution.py:22
  268.3 10.0 %collective-permute-start.16 = (f32[32,16,2]{2,0,1:T(8,128)S(1)}, f32[32,16,2]{2,0,1:T(8,128)S(1)}, u32[]{:S(2)}, u32[]{:S(2)}) collective-permute-start(f32[32,16,2]{2,0,1:T(8,128)S(1)} %get-tuple-element.62), channel_id=1, source_target_pairs={{0,8},{8,16},{16,24},{24,32},{32,40},{40,48},{48,56},{56,64},{64,7... | collective-permute-start | bytes 12296 | tf_op jit(solution)/shard_map/ppermute | solution.py:20
  278.3 6.1 %copy-start.22 = (f32[20]{0:T(128)S(1)}, f32[20]{0:T(128)}, u32[]{:S(2)}) copy-start(f32[20]{0:T(128)} %copy-done.21) | copy-start | bytes 244
  278.6 3.2 collective-permute-start.19
  278.7 5.7 %collective-permute-start.18 = (f32[32,2,132]{2,0,1:T(8,128)S(1)}, f32[32,2,132]{2,0,1:T(8,128)S(1)}, u32[]{:S(2)}, u32[]{:S(2)}) collective-permute-start(f32[32,2,132]{2,0,1:T(8,128)S(1)} %get-tuple-element.48), channel_id=1, source_target_pairs={{0,1},{1,2},{2,3},{3,4},{4,5},{5,6},{6,7},{7,0},{8,9},{9,10},{10,1... | collective-permute-start | bytes 101384 | tf_op jit(solution)/shard_map/ppermute | solution.py:20
  296.4 1.9 copy-start.16
  310.9 11.2 %copy-start.23 = (f32[20]{0:T(128)S(1)}, f32[20]{0:T(128)}, u32[]{:S(2)}) copy-start(f32[20]{0:T(128)} %copy-done.21) | copy-start | bytes 244
  313.2 27.5 %all-to-all-start.1 = ((f32[128,1,801]{2,1,0:T(1,128)}), f32[128,1,801]{2,1,0:T(1,128)S(1)}, u32[]{:S(2)}, u32[]{:S(2)}) async-start(f32[128,1,801]{2,1,0:T(1,128)} %all_to_all.18), calls=%async_computation.1 | async-start | bytes 917504 | tf_op jit(solution)/shard_map/all_to_all | solution.py:87
  320.2 9.8 %collective-permute-start.21 = (bf16[64,16,2]{2,0,1:T(8,128)(2,1)}, bf16[64,16,2]{2,0,1:T(8,128)(2,1)S(1)}, u32[]{:S(2)}, u32[]{:S(2)}) collective-permute-start(bf16[64,16,2]{2,0,1:T(8,128)(2,1)} %get-tuple-element.61), channel_id=1, source_target_pairs={{8,0},{16,8},{24,16},{32,24},{40,32},{48,40},{56,48},{64,56},{72,6... | collective-permute-start | bytes 12296 | tf_op jit(solution)/shard_map/ppermute | solution.py:22
  321.4 8.7 %collective-permute-start.20 = (bf16[64,16,2]{2,0,1:T(8,128)(2,1)}, bf16[64,16,2]{2,0,1:T(8,128)(2,1)S(1)}, u32[]{:S(2)}, u32[]{:S(2)}) collective-permute-start(bf16[64,16,2]{2,0,1:T(8,128)(2,1)} %get-tuple-element.60), channel_id=1, source_target_pairs={{0,8},{8,16},{16,24},{24,32},{32,40},{40,48},{48,56},{56,64},{64,7... | collective-permute-start | bytes 12296 | tf_op jit(solution)/shard_map/ppermute | solution.py:20
  322.5 17.1 %copy-start.28 = (bf16[20]{0:T(256)(128)(2,1)S(1)}, bf16[20]{0:T(256)(128)(2,1)}, u32[]{:S(2)}) copy-start(bf16[20]{0:T(256)(128)(2,1)} %copy-done.27) | copy-start | bytes 124
  330.4 5.2 %collective-permute-start.23 = (bf16[64,2,132]{2,0,1:T(8,128)(2,1)S(1)}, bf16[64,2,132]{2,0,1:T(8,128)(2,1)S(1)}, u32[]{:S(2)}, u32[]{:S(2)}) collective-permute-start(bf16[64,2,132]{2,0,1:T(8,128)(2,1)S(1)} %get-tuple-element.47), channel_id=1, source_target_pairs={{1,0},{2,1},{3,2},{4,3},{5,4},{6,5},{7,6},{0,7},{9,8},{10,9},{11,1... | collective-permute-start | bytes 101384 | tf_op jit(solution)/shard_map/ppermute | solution.py:22
  334.3 5.2 %collective-permute-start.22 = (bf16[64,2,132]{2,0,1:T(8,128)(2,1)S(1)}, bf16[64,2,132]{2,0,1:T(8,128)(2,1)S(1)}, u32[]{:S(2)}, u32[]{:S(2)}) collective-permute-start(bf16[64,2,132]{2,0,1:T(8,128)(2,1)S(1)} %get-tuple-element.46), channel_id=1, source_target_pairs={{0,1},{1,2},{2,3},{3,4},{4,5},{5,6},{6,7},{7,0},{8,9},{9,10},{10,1... | collective-permute-start | bytes 101384 | tf_op jit(solution)/shard_map/ppermute | solution.py:20
  340.5 11.2 %copy-start.35 = (pred[8,17]{0,1:T(8,128)(4,1)S(1)}, pred[8,17]{0,1:T(8,128)(4,1)}, u32[]{:S(2)}) copy-start(pred[8,17]{0,1:T(8,128)(4,1)} %constant.121) | copy-start | bytes 412
  342.1 22.8 %all-to-all-start.2 = ((f32[128,1,801]{2,1,0:T(1,128)}), f32[128,1,801]{2,1,0:T(1,128)S(1)}, u32[]{:S(2)}, u32[]{:S(2)}) async-start(f32[128,1,801]{2,1,0:T(1,128)} %broadcast_in_dim.114), calls=%async_computation.2 | async-start | bytes 917504 | tf_op jit(solution)/shard_map/all_to_all | solution.py:88
  (15 other events, 16.0 us)

commit v2 on v1

--- a/solution.py
+++ b/solution.py
@@ -1,6 +1,8 @@
 import jax
 import jax.numpy as jnp
 from jax import lax
+from jax.experimental import pallas as pl
+from jax.experimental.pallas import tpu as pltpu
 from jax.sharding import PartitionSpec as P
 
 STEPS = 2
@@ -74,6 +76,66 @@
             )
         stripes.append(jnp.stack(pieces, axis=-1))
     return jnp.stack(stripes, axis=-2)
+
+
+def split3(values):
+    high = values.astype(jnp.bfloat16)
+    rest = values - high.astype(jnp.float32)
+    middle = rest.astype(jnp.bfloat16)
+    low = (rest - middle.astype(jnp.float32)).astype(jnp.bfloat16)
+    return high, middle, low
+
+
+def exact_dot(values, onehot):
+    high, middle, low = split3(values)
+    dims = (((1,), (0,)), ((), ()))
+    total = lax.dot_general(high, onehot, dims, preferred_element_type=jnp.float32)
+    total = total + lax.dot_general(middle, onehot, dims, preferred_element_type=jnp.float32)
+    return total + lax.dot_general(low, onehot, dims, preferred_element_type=jnp.float32)
+
+
+def pick_columns(values, index, block=512):
+    rows, width = values.shape
+    count = index.shape[1]
+
+    def body(values_ref, index_ref, out_ref):
+        rows_iota = lax.broadcasted_iota(jnp.int32, (width, block), 0)
+        onehot = (rows_iota == index_ref[...]).astype(jnp.bfloat16)
+        out_ref[...] = exact_dot(values_ref[...], onehot)
+
+    return pl.pallas_call(
+        body,
+        grid=(count // block,),
+        in_specs=[
+            pl.BlockSpec((rows, width), lambda i: (0, 0)),
+            pl.BlockSpec((1, block), lambda i: (0, i)),
+        ],
+        out_specs=pl.BlockSpec((rows, block), lambda i: (0, i)),
+        out_shape=jax.ShapeDtypeStruct((rows, count), jnp.float32),
+        compiler_params=pltpu.CompilerParams(dimension_semantics=("parallel",)),
+    )(values, index)
+
+
+def add_columns(values, index_col, width, block=256):
+    rows, count = values.shape
+
+    def body(values_ref, index_ref, out_ref):
+        start = pl.program_id(0) * block
+        cols_iota = lax.broadcasted_iota(jnp.int32, (count, block), 1) + start
+        onehot = (cols_iota == index_ref[...]).astype(jnp.bfloat16)
+        out_ref[...] = exact_dot(values_ref[...], onehot)
+
+    return pl.pallas_call(
+        body,
+        grid=(width // block,),
+        in_specs=[
+            pl.BlockSpec((rows, count), lambda i: (0, 0)),
+            pl.BlockSpec((count, 1), lambda i: (0, 0)),
+        ],
+        out_specs=pl.BlockSpec((rows, block), lambda i: (0, i)),
+        out_shape=jax.ShapeDtypeStruct((rows, width), jnp.float32),
+        compiler_params=pltpu.CompilerParams(dimension_semantics=("parallel",)),
+    )(values, index_col)
 
 
 def all_sum(parts, axes):
@@ -125,25 +187,24 @@
     slot_index = jnp.arange(CAP, dtype=jnp.int32)
     source_row = starts[:, None] + slot_index[None, :]
     filled = (slot_index[None, :] < sent_rows[:, None]).reshape(1, -1)
-    picked = jnp.clip(source_row, 0, profile_dev - 1).reshape(-1)
-    sent_values = jnp.where(filled, jnp.take(observations, picked, axis=1), 0.0)
-    sent_cells = jnp.where(filled, jnp.take(profile_cells, picked)[None, :], cell_count).astype(
-        jnp.float32
-    )
+    picked = jnp.where(filled, source_row.reshape(1, -1), profile_dev)
+    source = jnp.concatenate(
+        [observations, profile_cells[None, :].astype(jnp.float32)], axis=0
+    )
+    gathered = pick_columns(source, picked)
+    sent_values = gathered[:levels]
+    sent_cells = jnp.where(filled, gathered[levels:], float(cell_count))
     payload = jnp.concatenate([sent_values, sent_cells], axis=0)
     arrived = lax.all_to_all(payload, ("lon", "lat"), split_axis=1, concat_axis=1, tiled=True)
     received_values = arrived[:levels]
     received_cells = arrived[levels:].astype(jnp.int32)
     occupied = received_cells < cell_count
-    target = jnp.where(occupied, received_cells, 0)[0]
+    target = jnp.where(occupied, received_cells, cell_count)
     flat_state = current.reshape(levels, cell_count)
-    misfits = jnp.where(occupied, jnp.take(flat_state, target, axis=1) - received_values, 0.0)
+    misfits = jnp.where(occupied, pick_columns(flat_state, target) - received_values, 0.0)
     square_sum = jnp.sum(misfits * misfits)
-    tangent = (
-        jnp.zeros((levels, cell_count), jnp.float32)
-        .at[:, target]
-        .add(misfits / profile_dev)
-        .reshape(levels, tile_rows, tile_cols)
+    tangent = add_columns(misfits / profile_dev, target.reshape(-1, 1), cell_count).reshape(
+        levels, tile_rows, tile_cols
     )
     grad_in = jnp.zeros(w_in.shape, jnp.float32)
     grad_out = jnp.zeros(w_out.shape, jnp.float32)

time: 397 us -> 390 us (0.982)
  local copies, waits for them, and re-layouts: 145 us -> 96.5 us
  matrix products: 53.4 us -> 92.6 us
  Pallas kernels: 0 us -> 33 us
  other arithmetic: 65.9 us -> 43.1 us
  waiting for transfers between devices: 46.6 us -> 27.5 us
  starting transfers between devices: 74 us -> 87 us
    gather x5 -> x0, local copies, waits for them, and re-layouts: 45 us -> none  [the longest x3 16.8 us: on_device(): jnp.take(profile_cells, picked)[None, :]]
    conv_general_dilated x8, matrix products: 27.3 us -> 69.8 us  [conv_valid(): lax.conv_general_dilated(padded[None], kernel, (1, 1), 'VALID', dimension...]
    pallas_call x0 -> x3, Pallas kernels: none -> 33 us  [the longest x2 18.7 us: pick_columns(): pl.pallas_call(body, grid=(count // block,), in_specs=[pl.BlockSpec((rows...]
    scatter-add x1 -> x0, other arithmetic: 25.7 us -> none  [on_device(): tangent = jnp.zeros((levels, cell_count), jnp.float32).at[:, target].add(...]
    ppermute x12, waiting for transfers between devices: 22.2 us -> 2 us  [extended_2(): lax.ppermute(head, axis, [((i + 1) % count, i) for i in range(count)])]
    unnamed x109 -> x196, local copies, waits for them, and re-layouts: 45.8 us -> 30 us
    ppermute x12, starting transfers between devices: 34.7 us -> 45.1 us  [extended_2(): lax.ppermute(head, axis, [((i + 1) % count, i) for i in range(count)])]
    slice x1 -> x0, other arithmetic: 5.63 us -> none  [on_device(): received_values = arrived[:levels]]
  transfers between devices with their start and end apart: 27 -> 27, of which waited for: 17 -> 11; matrix products, arithmetic and copies ran while one was open for 27% -> 37% of each run, Pallas kernels for 0% -> 2%
where the time goes in v2:
time: 390 us; the launch traced here: 384 us
  local copies, waits for them, and re-layouts  96.5 us (25%)
  matrix products  92.6 us (24%)
  starting transfers between devices  87 us (22%)
  other arithmetic  43.1 us (11%)
  Pallas kernels  33 us (8%)
  waiting for transfers between devices  27.5 us (7%)
  between operations  4.38 us (1%)
    conv_general_dilated x8, matrix products, conv_valid(): lax.conv_general_dilated(padded[None], kernel, (1, 1), 'VALID', dimension...  69.8 us
    ppermute x12, starting transfers between devices, extended_2(): lax.ppermute(head, axis, [((i + 1) % count, i) for i in range(count)])  45.1 us
    unnamed x196, local copies, waits for them, and re-layouts  30 us
    dot_general x100, matrix products, kernel_grad(): jnp.einsum('ohw,chw->oc', cotangent, window, preferred_element_type=jnp.f...  22.8 us
    pallas_call x2, Pallas kernels, pick_columns(): pl.pallas_call(body, grid=(count // block,), in_specs=[pl.BlockSpec((rows...  18.7 us
    ppermute x12, waiting for transfers between devices, extended_2(): lax.ppermute(tail, axis, [(i, (i + 1) % count) for i in range(count)])  17.9 us
    pallas_call x1, Pallas kernels, add_columns(): pl.pallas_call(body, grid=(width // block,), in_specs=[pl.BlockSpec((rows...  14.3 us
    add x2, local copies, waits for them, and re-layouts, on_device(): grad_in = grad_in + kernel_grad(coarse, sensitivity)  12.6 us
  transfers between devices with their start and end apart: 27, of which 11 were waited for; matrix products, arithmetic and copies ran while one was open for 37% of the time, Pallas kernels for 2%

profile of v2, /device:TPU:1, one launch (start us, length us, event | category | flops | bytes accessed | tf_op | source)
XLA Modules:
  0.0 384.1 jit_solution(1817873802474058585)
XLA Ops:
  2.6 2.7 collective-permute-start
  10.9 7.0 %shard_map.110 = f32[33,4096]{1,0:T(8,128)} custom-call(f32[33,1024]{1,0:T(8,128)} %pad_maximum_fusion.7.values_ref, s32[1,4096]{1,0:T(1,128)} %broadcast_select_fusion.index_ref), custom_call_target="tpu_custom_call" | custom-call | tf_op jit(solution)/shard_map/pallas_call | solution.py:106
  20.7 3.6 reshape.624
  24.3 11.9 %all-to-all-start = ((f32[128,1,1056]{2,1,0:T(1,128)}), f32[128,1,1056]{2,1,0:T(1,128)}, u32[]{:S(2)}, u32[]{:S(2)}) async-start(f32[128,1,1056]{2,1,0:T(1,128)} %reshape.624), calls=%async_computation | async-start | bytes 1179648 | tf_op jit(solution)/shard_map/all_to_all | solution.py:198
  39.7 3.0 collective-permute-start.3
  43.9 6.4 %collective-permute-done.2 = f32[32,4,136]{2,1,0:T(4,128)S(1)} collective-permute-done((f32[32,4,136]{2,1,0:T(4,128)S(1)}, f32[32,4,136]{2,1,0:T(4,128)S(1)}, u32[]{:S(2)}, u32[]{:S(2)}) %collective-permute-start.2) | collective-permute-done | bytes 69664 | tf_op jit(solution)/shard_map/ppermute | solution.py:22
  52.7 7.0 %convolution_tanh_fusion.1 = f32[1,64,20,132]{1,0,3,2:T(1,128)S(1)} fusion(bf16[1,32,24,136]{1,0,3,2:T(2,128)(2,1)S(1)} %copy.1088, bf16[64,32,5,5]{0,1,3,2:T(8,128)(2,1)S(1)} %copy-done), kind=kOutput, calls=%fused_computation.10 | convolution fusion | flops 270336000 | bytes 987136 | tf_op jit(solution)/shard_map/conv_general_dilated | solution.py:52
  60.7 20.3 %fusion.4 = f32[1,32,16,128]{1,0,3,2:T(1,128)S(1)} fusion(bf16[32,64,5,5]{1,0,3,2:T(8,128)(2,1)S(1)} %copy-done.77, f32[1,64,20,132]{1,0,3,2:T(1,128)S(1)} %convolution_tanh_fusion.1, f32[20]{0:T(128)S(1)} %and_convert_fusion), kind=kOutput, calls=%fused_computation.13 | convolution fusion | flops 210053120 | bytes 1040464 | tf_op jit(solution)/shard_map/conv_general_dilated | solution.py:52
  89.1 2.7 copy.1144
  92.3 3.6 collective-permute-start.7
  99.1 3.4 copy.1090
  102.6 8.5 %convolution_tanh_fusion = f32[1,64,20,132]{1,0,3,2:T(1,128)S(1)} fusion(bf16[1,32,24,136]{1,0,3,2:T(2,128)(2,1)} %copy.1090, bf16[64,32,5,5]{0,1,3,2:T(8,128)(2,1)S(1)} %copy-done), kind=kOutput, calls=%fused_computation.9 | convolution fusion | flops 270336000 | bytes 987136 | tf_op jit(solution)/shard_map/conv_general_dilated | solution.py:52
  112.2 20.8 %fusion.5 = f32[1,32,16,128]{1,0,3,2:T(1,128)} fusion(bf16[32,64,5,5]{1,0,3,2:T(8,128)(2,1)S(1)} %copy-done.78, f32[1,64,20,132]{1,0,3,2:T(1,128)S(1)} %convolution_tanh_fusion, f32[20]{0:T(128)S(1)} %and_convert_fusion), kind=kOutput, calls=%fused_computation.14 | convolution fusion | flops 210053120 | bytes 1040464 | tf_op jit(solution)/shard_map/conv_general_dilated | solution.py:52
  133.0 2.7 copy.1105
  135.7 2.9 copy.1091
  147.5 3.1 reduce.7
  150.6 2.7 reshape.625
  153.3 2.8 compare_reduce_fusion
  156.1 2.8 fusion.231
  162.3 3.1 compare_select_fusion.index_ref
  165.4 11.7 %shard_map.111 = f32[32,4096]{1,0:T(8,128)} custom-call(f32[32,2048]{1,0:T(8,128)} %bitcast.318, s32[1,4096]{1,0:T(1,128)} %compare_select_fusion.1.index_ref), custom_call_target="tpu_custom_call" | custom-call | tf_op jit(solution)/shard_map/pallas_call | solution.py:106
  177.0 2.6 broadcast_multiply_fusion
  179.6 14.3 %shard_map.112 = f32[32,2048]{1,0:T(8,128)} custom-call(f32[32,4096]{1,0:T(8,128)} %get-tuple-element.44.values_ref, s32[4096,1]{1,0:T(8,128)} %compare_select_fusion.index_ref), custom_call_target="tpu_custom_call" | custom-call | tf_op jit(solution)/shard_map/pallas_call | solution.py:128
  201.8 3.0 collective-permute-start.8
  204.7 3.1 collective-permute-start.9
  211.0 4.1 %collective-permute-start.11 = (f32[32,2,132]{2,1,0:T(2,128)S(1)}, f32[32,2,132]{2,1,0:T(2,128)S(1)}, u32[]{:S(2)}, u32[]{:S(2)}) collective-permute-start(f32[32,2,132]{2,1,0:T(2,128)S(1)} %get-tuple-element.53), channel_id=1, source_target_pairs={{1,0},{2,1},{3,2},{4,3},{5,4},{6,5},{7,6},{0,7},{9,8},{10,9},{11,1... | collective-permute-start | bytes 101384 | tf_op jit(solution)/shard_map/ppermute | solution.py:24
  218.6 2.6 convolution_select_fusion.3
  225.7 7.1 %collective-permute-start.13 = (bf16[64,16,2]{2,0,1:T(8,128)(2,1)S(1)}, bf16[64,16,2]{2,0,1:T(8,128)(2,1)S(1)}, u32[]{:S(2)}, u32[]{:S(2)}) collective-permute-start(bf16[64,16,2]{2,0,1:T(8,128)(2,1)S(1)} %get-tuple-element.115), channel_id=1, source_target_pairs={{8,0},{16,8},{24,16},{32,24},{40,32},{48,40},{56,48},{64,56},{72,6... | collective-permute-start | bytes 12296 | tf_op jit(solution)/shard_map/ppermute | solution.py:24
  237.7 4.4 %collective-permute-start.15 = (bf16[64,2,132]{2,0,1:T(8,128)(2,1)S(1)}, bf16[64,2,132]{2,0,1:T(8,128)(2,1)S(1)}, u32[]{:S(2)}, u32[]{:S(2)}) collective-permute-start(bf16[64,2,132]{2,0,1:T(8,128)(2,1)S(1)} %get-tuple-element.51), channel_id=1, source_target_pairs={{1,0},{2,1},{3,2},{4,3},{5,4},{6,5},{7,6},{0,7},{9,8},{10,9},{11,1... | collective-permute-start | bytes 101384 | tf_op jit(solution)/shard_map/ppermute | solution.py:24
  244.8 4.0 %convolution_select_fusion.2 = f32[16,8,17,32]{3,1,2,0:T(8,128)S(1)} fusion(bf16[64,32,5,5]{0,1,3,2:T(8,128)(2,1)S(1)} %copy-done, bf16[64,20,1,7,4]{0,3,4,1,2:T(8,128)(2,1)S(1)} %slice.738, bf16[64,20,1,8,17]{0,3,4,1,2:T(8,128)(2,1)S(1)} %copy.1133, pred[8,17]{0,1:T(8,128)(4,1)S(1)} %copy-done.81), kind=kOutput, calls=%fused_computation.17 | convolution fusion | flops 224182272 | bytes 800904 | tf_op jit(solution)/shard_map/conv_general_dilated | solution.py:52
  257.6 6.5 %collective-permute-start.17 = (f32[32,16,2]{2,1,0:T(8,128)S(1)}, f32[32,16,2]{2,1,0:T(8,128)S(1)}, u32[]{:S(2)}, u32[]{:S(2)}) collective-permute-start(f32[32,16,2]{2,1,0:T(8,128)S(1)} %get-tuple-element.113), channel_id=1, source_target_pairs={{8,0},{16,8},{24,16},{32,24},{40,32},{48,40},{56,48},{64,56},{72,6... | collective-permute-start | bytes 12296 | tf_op jit(solution)/shard_map/ppermute | solution.py:24
  264.3 4.8 %copy.1221 = f32[32,64,5,5]{3,2,1,0:T(8,128)} copy(f32[32,64,5,5]{1,0,3,2:T(8,128)S(1)} %add.182) | data formatting | bytes 409600 | tf_op jit(solution)/shard_map/add | solution.py:215
  269.1 5.0 %add.183 = f32[51200]{0:T(1024)S(1)} reshape(f32[32,64,5,5]{3,2,1,0:T(8,128)} %copy.1221) | data formatting | bytes 409600 | tf_op jit(solution)/shard_map/add | solution.py:215
  274.9 3.9 %collective-permute-start.19 = (f32[32,2,132]{2,1,0:T(2,128)S(1)}, f32[32,2,132]{2,1,0:T(2,128)S(1)}, u32[]{:S(2)}, u32[]{:S(2)}) collective-permute-start(f32[32,2,132]{2,1,0:T(2,128)S(1)} %get-tuple-element.49), channel_id=1, source_target_pairs={{1,0},{2,1},{3,2},{4,3},{5,4},{6,5},{7,6},{0,7},{9,8},{10,9},{11,1... | collective-permute-start | bytes 101384 | tf_op jit(solution)/shard_map/ppermute | solution.py:24
  282.1 2.6 convolution_select_fusion.1
  289.2 6.4 %collective-permute-start.21 = (bf16[64,16,2]{2,0,1:T(8,128)(2,1)}, bf16[64,16,2]{2,0,1:T(8,128)(2,1)S(1)}, u32[]{:S(2)}, u32[]{:S(2)}) collective-permute-start(bf16[64,16,2]{2,0,1:T(8,128)(2,1)} %get-tuple-element.111), channel_id=1, source_target_pairs={{8,0},{16,8},{24,16},{32,24},{40,32},{48,40},{56,48},{64,56},{72,6... | collective-permute-start | bytes 12296 | tf_op jit(solution)/shard_map/ppermute | solution.py:24
  299.7 7.6 %copy.1170 = f32[64,32,5,5]{3,2,1,0:T(8,128)} copy(f32[64,32,5,5]{0,1,3,2:T(8,128)S(1)} %add.180) | data formatting | bytes 409600 | tf_op jit(solution)/shard_map/add | solution.py:220
  307.3 5.0 %add.181 = f32[51200]{0:T(1024)S(1)} reshape(f32[64,32,5,5]{3,2,1,0:T(8,128)} %copy.1170) | data formatting | bytes 409600 | tf_op jit(solution)/shard_map/add | solution.py:220
  314.5 11.4 %all-to-all-start.1 = ((f32[128,1,801]{2,1,0:T(1,128)}), f32[128,1,801]{2,1,0:T(1,128)S(1)}, u32[]{:S(2)}, u32[]{:S(2)}) async-start(f32[128,1,801]{2,1,0:T(1,128)} %all_to_all.21), calls=%async_computation.1 | async-start | bytes 917504 | tf_op jit(solution)/shard_map/all_to_all | solution.py:149
  328.3 2.7 collective-permute-start.23
  331.3 5.3 %collective-permute-done.22 = bf16[64,2,132]{2,0,1:T(8,128)(2,1)S(1)} collective-permute-done((bf16[64,2,132]{2,0,1:T(8,128)(2,1)S(1)}, bf16[64,2,132]{2,0,1:T(8,128)(2,1)S(1)}, u32[]{:S(2)}, u32[]{:S(2)}) %collective-permute-start.22) | collective-permute-done | bytes 33824 | tf_op jit(solution)/shard_map/ppermute | solution.py:22
  340.2 6.4 %all-to-all-start.2 = ((f32[128,1,801]{2,1,0:T(1,128)}), f32[128,1,801]{2,1,0:T(1,128)S(1)}, u32[]{:S(2)}, u32[]{:S(2)}) async-start(f32[128,1,801]{2,1,0:T(1,128)} %broadcast_in_dim.27), calls=%async_computation.2 | async-start | bytes 917504 | tf_op jit(solution)/shard_map/all_to_all | solution.py:150
  346.7 4.0 %convolution_select_fusion = f32[16,8,17,32]{3,1,2,0:T(8,128)S(1)} fusion(bf16[64,32,5,5]{0,1,3,2:T(8,128)(2,1)S(1)} %copy-done, bf16[64,20,1,7,4]{0,3,4,1,2:T(8,128)(2,1)S(1)} %slice.834, bf16[64,20,1,8,17]{0,3,4,1,2:T(8,128)(2,1)S(1)} %copy.1225, pred[8,17]{0,1:T(8,128)(4,1)S(1)} %copy-done.82), kind=kOutput, calls=%fused_computation.15 | convolution fusion | flops 224182272 | bytes 800904 | tf_op jit(solution)/shard_map/conv_general_dilated | solution.py:52
  353.0 6.5 %all-to-all-done.2 = f32[128,1,801]{2,1,0:T(1,128)S(1)} async-done(((f32[128,1,801]{2,1,0:T(1,128)}), f32[128,1,801]{2,1,0:T(1,128)S(1)}, u32[]{:S(2)}, u32[]{:S(2)}) %all-to-all-start.2) | async-done | bytes 410144 | tf_op jit(solution)/shard_map/all_to_all | solution.py:150
  361.5 4.5 %reshape.475 = f32[32,64,5,5]{3,2,1,0:T(8,128)} reshape(f32[51200]{0:T(1024)S(1)} %get-tuple-element.58) | data formatting | bytes 409600 | tf_op jit(solution)/shard_map/reshape | solution.py:154
  365.9 5.6 %copy.1229 = f32[32,64,5,5]{1,0,3,2:T(8,128)} copy(f32[32,64,5,5]{3,2,1,0:T(8,128)} %reshape.475) | data formatting | bytes 409600
  371.5 4.4 %reshape.474 = f32[64,32,5,5]{3,2,1,0:T(8,128)} reshape(f32[51200]{0:T(1024)S(1)} %get-tuple-element.59) | data formatting | bytes 409600 | tf_op jit(solution)/shard_map/reshape | solution.py:154
  375.9 6.2 %copy.1228 = f32[64,32,5,5]{0,1,3,2:T(8,128)} copy(f32[64,32,5,5]{3,2,1,0:T(8,128)} %reshape.474) | data formatting | bytes 409600
  (440 shorter events, 102.9 us)
Async XLA Ops:
  0.6 52.0 %copy-start = (bf16[64,32,5,5]{0,1,3,2:T(8,128)(2,1)S(1)}, bf16[64,32,5,5]{0,1,3,2:T(8,128)(2,1)}, u32[]{:S(2)}) copy-start(bf16[64,32,5,5]{0,1,3,2:T(8,128)(2,1)} %param.12) | copy-start | bytes 307204
  2.6 34.2 %collective-permute-start = (f32[32,16,4]{2,1,0:T(8,128)}, f32[32,16,4]{2,1,0:T(8,128)S(1)}, u32[]{:S(2)}, u32[]{:S(2)}) collective-permute-start(f32[32,16,4]{2,1,0:T(8,128)} %get-tuple-element.120), channel_id=1, source_target_pairs={{0,8},{8,16},{16,24},{24,32},{32,40},{40,48},{48,56},{56,64},{64,7... | collective-permute-start | bytes 24584 | tf_op jit(solution)/shard_map/ppermute | solution.py:22
  5.3 31.6 %collective-permute-start.1 = (f32[32,16,4]{2,1,0:T(8,128)}, f32[32,16,4]{2,1,0:T(8,128)}, u32[]{:S(2)}, u32[]{:S(2)}) collective-permute-start(f32[32,16,4]{2,1,0:T(8,128)} %get-tuple-element.121), channel_id=1, source_target_pairs={{8,0},{16,8},{24,16},{32,24},{40,32},{48,40},{56,48},{64,56},{72,6... | collective-permute-start | bytes 24584 | tf_op jit(solution)/shard_map/ppermute | solution.py:24
  20.7 16.1 %copy-start.74 = (s32[16,128]{1,0:T(8,128)S(1)}, s32[16,128]{1,0:T(8,128)}, u32[]{:S(2)}) copy-start(s32[16,128]{1,0:T(8,128)} %param.8) | copy-start | bytes 24580
  20.7 16.1 %copy-start.1 = (f32[32,16,128]{2,1,0:T(8,128)S(1)}, f32[32,16,128]{2,1,0:T(8,128)}, u32[]{:S(2)}) copy-start(f32[32,16,128]{2,1,0:T(8,128)} %param.7) | copy-start | bytes 786436
  24.3 122.7 %all-to-all-start = ((f32[128,1,1056]{2,1,0:T(1,128)}), f32[128,1,1056]{2,1,0:T(1,128)}, u32[]{:S(2)}, u32[]{:S(2)}) async-start(f32[128,1,1056]{2,1,0:T(1,128)} %reshape.624), calls=%async_computation | async-start | bytes 1179648 | tf_op jit(solution)/shard_map/all_to_all | solution.py:198
  36.2 109.2 %copy-start.71 = (f32[20]{0:T(128)}, f32[20]{0:T(128)S(1)}, u32[]{:S(2)}) copy-start(f32[20]{0:T(128)S(1)} %and_convert_fusion) | copy-start | bytes 244
  38.1 12.2 %collective-permute-start.2 = (f32[32,4,136]{2,1,0:T(4,128)S(1)}, f32[32,4,136]{2,1,0:T(4,128)S(1)}, u32[]{:S(2)}, u32[]{:S(2)}) collective-permute-start(f32[32,4,136]{2,1,0:T(4,128)S(1)} %get-tuple-element.56), channel_id=1, source_target_pairs={{0,1},{1,2},{2,3},{3,4},{4,5},{5,6},{6,7},{7,0},{8,9},{9,10},{10,1... | collective-permute-start | bytes 208904 | tf_op jit(solution)/shard_map/ppermute | solution.py:22
  39.7 10.7 %collective-permute-start.3 = (f32[32,4,136]{2,1,0:T(4,128)S(1)}, f32[32,4,136]{2,1,0:T(4,128)S(1)}, u32[]{:S(2)}, u32[]{:S(2)}) collective-permute-start(f32[32,4,136]{2,1,0:T(4,128)S(1)} %get-tuple-element.57), channel_id=1, source_target_pairs={{1,0},{2,1},{3,2},{4,3},{5,4},{6,5},{7,6},{0,7},{9,8},{10,9},{11,1... | collective-permute-start | bytes 208904 | tf_op jit(solution)/shard_map/ppermute | solution.py:24
  83.5 8.4 %collective-permute-start.4 = (f32[32,16,4]{2,1,0:T(8,128)S(1)}, f32[32,16,4]{2,1,0:T(8,128)S(1)}, u32[]{:S(2)}, u32[]{:S(2)}) collective-permute-start(f32[32,16,4]{2,1,0:T(8,128)S(1)} %get-tuple-element.118), channel_id=1, source_target_pairs={{0,8},{8,16},{16,24},{24,32},{32,40},{40,48},{48,56},{56,64},{64,7... | collective-permute-start | bytes 24584 | tf_op jit(solution)/shard_map/ppermute | solution.py:22
  85.5 6.4 %collective-permute-start.5 = (f32[32,16,4]{2,1,0:T(8,128)S(1)}, f32[32,16,4]{2,1,0:T(8,128)S(1)}, u32[]{:S(2)}, u32[]{:S(2)}) collective-permute-start(f32[32,16,4]{2,1,0:T(8,128)S(1)} %get-tuple-element.119), channel_id=1, source_target_pairs={{8,0},{16,8},{24,16},{32,24},{40,32},{48,40},{56,48},{64,56},{72,6... | collective-permute-start | bytes 24584 | tf_op jit(solution)/shard_map/ppermute | solution.py:24
  91.8 53.6 %copy-start.2 = (f32[1,64,20,132]{3,1,2,0:T(8,128)}, f32[1,64,20,132]{3,1,2,0:T(8,128)S(1)}, u32[]{:S(2)}) copy-start(f32[1,64,20,132]{3,1,2,0:T(8,128)S(1)} %copy.1144) | copy-start | bytes 2027524
  92.2 6.0 %collective-permute-start.6 = (f32[32,4,136]{2,1,0:T(4,128)S(1)}, f32[32,4,136]{2,1,0:T(4,128)S(1)}, u32[]{:S(2)}, u32[]{:S(2)}) collective-permute-start(f32[32,4,136]{2,1,0:T(4,128)S(1)} %get-tuple-element.54), channel_id=1, source_target_pairs={{0,1},{1,2},{2,3},{3,4},{4,5},{5,6},{6,7},{7,0},{8,9},{9,10},{10,1... | collective-permute-start | bytes 208904 | tf_op jit(solution)/shard_map/ppermute | solution.py:22
  92.3 5.9 %collective-permute-start.7 = (f32[32,4,136]{2,1,0:T(4,128)S(1)}, f32[32,4,136]{2,1,0:T(4,128)S(1)}, u32[]{:S(2)}, u32[]{:S(2)}) collective-permute-start(f32[32,4,136]{2,1,0:T(4,128)S(1)} %get-tuple-element.55), channel_id=1, source_target_pairs={{1,0},{2,1},{3,2},{4,3},{5,4},{6,5},{7,6},{0,7},{9,8},{10,9},{11,1... | collective-permute-start | bytes 208904 | tf_op jit(solution)/shard_map/ppermute | solution.py:24
  98.2 12.9 %copy-start.65 = (f32[32,4,136]{2,1,0:T(4,128)}, f32[32,4,136]{2,1,0:T(4,128)S(1)}, u32[]{:S(2)}) copy-start(f32[32,4,136]{2,1,0:T(4,128)S(1)} %collective-permute-done.6) | copy-start | bytes 208900
  102.6 9.6 %copy-start.78 = (bf16[32,64,5,5]{1,0,3,2:T(8,128)(2,1)S(1)}, bf16[32,64,5,5]{1,0,3,2:T(8,128)(2,1)}, u32[]{:S(2)}) copy-start(bf16[32,64,5,5]{1,0,3,2:T(8,128)(2,1)} %param.13) | copy-start | bytes 307204
  135.7 9.7 %copy-start.3 = (f32[1,64,20,132]{3,1,2,0:T(8,128)}, f32[1,64,20,132]{3,1,2,0:T(8,128)S(1)}, u32[]{:S(2)}) copy-start(f32[1,64,20,132]{3,1,2,0:T(8,128)S(1)} %copy.1105) | copy-start | bytes 2027524
  179.6 15.3 %copy-start.11 = (bf16[64,20,132]{2,0,1:T(8,128)(2,1)S(1)}, bf16[64,20,132]{2,0,1:T(8,128)(2,1)}, u32[]{:S(2)}) copy-start(bf16[64,20,132]{2,0,1:T(8,128)(2,1)} %get-tuple-element.123) | copy-start | bytes 1013764
  201.8 7.0 %collective-permute-start.8 = (f32[32,16,2]{2,1,0:T(8,128)S(1)}, f32[32,16,2]{2,1,0:T(8,128)S(1)}, u32[]{:S(2)}, u32[]{:S(2)}) collective-permute-start(f32[32,16,2]{2,1,0:T(8,128)S(1)} %get-tuple-element.116), channel_id=1, source_target_pairs={{0,8},{8,16},{16,24},{24,32},{32,40},{40,48},{48,56},{56,64},{64,7... | collective-permute-start | bytes 12296 | tf_op jit(solution)/shard_map/ppermute | solution.py:22
  204.7 5.8 %collective-permute-start.9 = (f32[32,16,2]{2,1,0:T(8,128)S(1)}, f32[32,16,2]{2,1,0:T(8,128)S(1)}, u32[]{:S(2)}, u32[]{:S(2)}) collective-permute-start(f32[32,16,2]{2,1,0:T(8,128)S(1)} %get-tuple-element.117), channel_id=1, source_target_pairs={{8,0},{16,8},{24,16},{32,24},{40,32},{48,40},{56,48},{64,56},{72,6... | collective-permute-start | bytes 12296 | tf_op jit(solution)/shard_map/ppermute | solution.py:24
  210.9 5.8 %collective-permute-start.10 = (f32[32,2,132]{2,1,0:T(2,128)S(1)}, f32[32,2,132]{2,1,0:T(2,128)S(1)}, u32[]{:S(2)}, u32[]{:S(2)}) collective-permute-start(f32[32,2,132]{2,1,0:T(2,128)S(1)} %get-tuple-element.52), channel_id=1, source_target_pairs={{0,1},{1,2},{2,3},{3,4},{4,5},{5,6},{6,7},{7,0},{8,9},{9,10},{10,1... | collective-permute-start | bytes 101384 | tf_op jit(solution)/shard_map/ppermute | solution.py:22
  211.0 6.0 %collective-permute-start.11 = (f32[32,2,132]{2,1,0:T(2,128)S(1)}, f32[32,2,132]{2,1,0:T(2,128)S(1)}, u32[]{:S(2)}, u32[]{:S(2)}) collective-permute-start(f32[32,2,132]{2,1,0:T(2,128)S(1)} %get-tuple-element.53), channel_id=1, source_target_pairs={{1,0},{2,1},{3,2},{4,3},{5,4},{6,5},{7,6},{0,7},{9,8},{10,9},{11,1... | collective-permute-start | bytes 101384 | tf_op jit(solution)/shard_map/ppermute | solution.py:24
  223.5 9.3 %copy-start.58 = (bf16[32,16,128]{2,1,0:T(8,128)(2,1)S(1)}, bf16[32,16,128]{2,1,0:T(8,128)(2,1)}, u32[]{:S(2)}) copy-start(bf16[32,16,128]{2,1,0:T(8,128)(2,1)} %get-tuple-element.89) | copy-start | bytes 393220
  223.7 9.3 %copy-start.57 = (bf16[32,16,128]{2,1,0:T(8,128)(2,1)S(1)}, bf16[32,16,128]{2,1,0:T(8,128)(2,1)}, u32[]{:S(2)}) copy-start(bf16[32,16,128]{2,1,0:T(8,128)(2,1)} %get-tuple-element.94) | copy-start | bytes 393220
  223.7 9.5 %copy-start.56 = (bf16[32,16,128]{2,1,0:T(8,128)(2,1)S(1)}, bf16[32,16,128]{2,1,0:T(8,128)(2,1)}, u32[]{:S(2)}) copy-start(bf16[32,16,128]{2,1,0:T(8,128)(2,1)} %get-tuple-element.99) | copy-start | bytes 393220
  223.9 9.5 %copy-start.55 = (bf16[32,16,128]{2,1,0:T(8,128)(2,1)S(1)}, bf16[32,16,128]{2,1,0:T(8,128)(2,1)}, u32[]{:S(2)}) copy-start(bf16[32,16,128]{2,1,0:T(8,128)(2,1)} %get-tuple-element.103) | copy-start | bytes 393220
  224.1 9.5 %copy-start.54 = (bf16[32,16,128]{2,1,0:T(8,128)(2,1)S(1)}, bf16[32,16,128]{2,1,0:T(8,128)(2,1)}, u32[]{:S(2)}) copy-start(bf16[32,16,128]{2,1,0:T(8,128)(2,1)} %get-tuple-element.102) | copy-start | bytes 393220
  224.3 9.5 %copy-start.53 = (bf16[32,16,128]{2,1,0:T(8,128)(2,1)S(1)}, bf16[32,16,128]{2,1,0:T(8,128)(2,1)}, u32[]{:S(2)}) copy-start(bf16[32,16,128]{2,1,0:T(8,128)(2,1)} %get-tuple-element.101) | copy-start | bytes 393220
  224.6 9.5 %copy-start.52 = (bf16[32,16,128]{2,1,0:T(8,128)(2,1)S(1)}, bf16[32,16,128]{2,1,0:T(8,128)(2,1)}, u32[]{:S(2)}) copy-start(bf16[32,16,128]{2,1,0:T(8,128)(2,1)} %get-tuple-element.100) | copy-start | bytes 393220
  225.0 9.4 %copy-start.51 = (bf16[32,16,128]{2,1,0:T(8,128)(2,1)S(1)}, bf16[32,16,128]{2,1,0:T(8,128)(2,1)}, u32[]{:S(2)}) copy-start(bf16[32,16,128]{2,1,0:T(8,128)(2,1)} %get-tuple-element.88) | copy-start | bytes 393220
  225.0 12.3 %collective-permute-start.12 = (bf16[64,16,2]{2,0,1:T(8,128)(2,1)S(1)}, bf16[64,16,2]{2,0,1:T(8,128)(2,1)S(1)}, u32[]{:S(2)}, u32[]{:S(2)}) collective-permute-start(bf16[64,16,2]{2,0,1:T(8,128)(2,1)S(1)} %get-tuple-element.114), channel_id=1, source_target_pairs={{0,8},{8,16},{16,24},{24,32},{32,40},{40,48},{48,56},{56,64},{64,7... | collective-permute-start | bytes 12296 | tf_op jit(solution)/shard_map/ppermute | solution.py:22
  225.7 11.6 %collective-permute-start.13 = (bf16[64,16,2]{2,0,1:T(8,128)(2,1)S(1)}, bf16[64,16,2]{2,0,1:T(8,128)(2,1)S(1)}, u32[]{:S(2)}, u32[]{:S(2)}) collective-permute-start(bf16[64,16,2]{2,0,1:T(8,128)(2,1)S(1)} %get-tuple-element.115), channel_id=1, source_target_pairs={{8,0},{16,8},{24,16},{32,24},{40,32},{48,40},{56,48},{64,56},{72,6... | collective-permute-start | bytes 12296 | tf_op jit(solution)/shard_map/ppermute | solution.py:24
  237.7 6.0 %collective-permute-start.14 = (bf16[64,2,132]{2,0,1:T(8,128)(2,1)S(1)}, bf16[64,2,132]{2,0,1:T(8,128)(2,1)S(1)}, u32[]{:S(2)}, u32[]{:S(2)}) collective-permute-start(bf16[64,2,132]{2,0,1:T(8,128)(2,1)S(1)} %get-tuple-element.50), channel_id=1, source_target_pairs={{0,1},{1,2},{2,3},{3,4},{4,5},{5,6},{6,7},{7,0},{8,9},{9,10},{10,1... | collective-permute-start | bytes 101384 | tf_op jit(solution)/shard_map/ppermute | solution.py:22
  237.7 5.9 %collective-permute-start.15 = (bf16[64,2,132]{2,0,1:T(8,128)(2,1)S(1)}, bf16[64,2,132]{2,0,1:T(8,128)(2,1)S(1)}, u32[]{:S(2)}, u32[]{:S(2)}) collective-permute-start(bf16[64,2,132]{2,0,1:T(8,128)(2,1)S(1)} %get-tuple-element.51), channel_id=1, source_target_pairs={{1,0},{2,1},{3,2},{4,3},{5,4},{6,5},{7,6},{0,7},{9,8},{10,9},{11,1... | collective-permute-start | bytes 101384 | tf_op jit(solution)/shard_map/ppermute | solution.py:24
  257.5 16.6 %collective-permute-start.16 = (f32[32,16,2]{2,1,0:T(8,128)S(1)}, f32[32,16,2]{2,1,0:T(8,128)S(1)}, u32[]{:S(2)}, u32[]{:S(2)}) collective-permute-start(f32[32,16,2]{2,1,0:T(8,128)S(1)} %get-tuple-element.112), channel_id=1, source_target_pairs={{0,8},{8,16},{16,24},{24,32},{32,40},{40,48},{48,56},{56,64},{64,7... | collective-permute-start | bytes 12296 | tf_op jit(solution)/shard_map/ppermute | solution.py:22
  257.6 16.5 %collective-permute-start.17 = (f32[32,16,2]{2,1,0:T(8,128)S(1)}, f32[32,16,2]{2,1,0:T(8,128)S(1)}, u32[]{:S(2)}, u32[]{:S(2)}) collective-permute-start(f32[32,16,2]{2,1,0:T(8,128)S(1)} %get-tuple-element.113), channel_id=1, source_target_pairs={{8,0},{16,8},{24,16},{32,24},{40,32},{48,40},{56,48},{64,56},{72,6... | collective-permute-start | bytes 12296 | tf_op jit(solution)/shard_map/ppermute | solution.py:24
  274.5 5.9 %collective-permute-start.18 = (f32[32,2,132]{2,1,0:T(2,128)S(1)}, f32[32,2,132]{2,1,0:T(2,128)S(1)}, u32[]{:S(2)}, u32[]{:S(2)}) collective-permute-start(f32[32,2,132]{2,1,0:T(2,128)S(1)} %get-tuple-element.48), channel_id=1, source_target_pairs={{0,1},{1,2},{2,3},{3,4},{4,5},{5,6},{6,7},{7,0},{8,9},{9,10},{10,1... | collective-permute-start | bytes 101384 | tf_op jit(solution)/shard_map/ppermute | solution.py:22
  274.9 5.5 %collective-permute-start.19 = (f32[32,2,132]{2,1,0:T(2,128)S(1)}, f32[32,2,132]{2,1,0:T(2,128)S(1)}, u32[]{:S(2)}, u32[]{:S(2)}) collective-permute-start(f32[32,2,132]{2,1,0:T(2,128)S(1)} %get-tuple-element.49), channel_id=1, source_target_pairs={{1,0},{2,1},{3,2},{4,3},{5,4},{6,5},{7,6},{0,7},{9,8},{10,9},{11,1... | collective-permute-start | bytes 101384 | tf_op jit(solution)/shard_map/ppermute | solution.py:24
  289.1 37.2 %collective-permute-start.20 = (bf16[64,16,2]{2,0,1:T(8,128)(2,1)}, bf16[64,16,2]{2,0,1:T(8,128)(2,1)S(1)}, u32[]{:S(2)}, u32[]{:S(2)}) collective-permute-start(bf16[64,16,2]{2,0,1:T(8,128)(2,1)} %get-tuple-element.110), channel_id=1, source_target_pairs={{0,8},{8,16},{16,24},{24,32},{32,40},{40,48},{48,56},{56,64},{64,7... | collective-permute-start | bytes 12296 | tf_op jit(solution)/shard_map/ppermute | solution.py:22
  289.2 37.2 %collective-permute-start.21 = (bf16[64,16,2]{2,0,1:T(8,128)(2,1)}, bf16[64,16,2]{2,0,1:T(8,128)(2,1)S(1)}, u32[]{:S(2)}, u32[]{:S(2)}) collective-permute-start(bf16[64,16,2]{2,0,1:T(8,128)(2,1)} %get-tuple-element.111), channel_id=1, source_target_pairs={{8,0},{16,8},{24,16},{32,24},{40,32},{48,40},{56,48},{64,56},{72,6... | collective-permute-start | bytes 12296 | tf_op jit(solution)/shard_map/ppermute | solution.py:24
  312.3 13.6 %copy-start.68 = (f32[32,2,132]{2,1,0:T(2,128)S(1)}, f32[32,2,132]{2,1,0:T(2,128)}, u32[]{:S(2)}) copy-start(f32[32,2,132]{2,1,0:T(2,128)} %copy-done.67) | copy-start | bytes 101380
  312.3 13.6 %copy-start.73 = (f32[20]{0:T(128)S(1)}, f32[20]{0:T(128)}, u32[]{:S(2)}) copy-start(f32[20]{0:T(128)} %copy-done.71) | copy-start | bytes 244
  314.5 24.4 %all-to-all-start.1 = ((f32[128,1,801]{2,1,0:T(1,128)}), f32[128,1,801]{2,1,0:T(1,128)S(1)}, u32[]{:S(2)}, u32[]{:S(2)}) async-start(f32[128,1,801]{2,1,0:T(1,128)} %all_to_all.21), calls=%async_computation.1 | async-start | bytes 917504 | tf_op jit(solution)/shard_map/all_to_all | solution.py:149
  326.3 10.3 %copy-start.76 = (bf16[20]{0:T(256)(128)(2,1)S(1)}, bf16[20]{0:T(256)(128)(2,1)}, u32[]{:S(2)}) copy-start(bf16[20]{0:T(256)(128)(2,1)} %fusion.180) | copy-start | bytes 124
  326.7 9.9 %collective-permute-start.22 = (bf16[64,2,132]{2,0,1:T(8,128)(2,1)S(1)}, bf16[64,2,132]{2,0,1:T(8,128)(2,1)S(1)}, u32[]{:S(2)}, u32[]{:S(2)}) collective-permute-start(bf16[64,2,132]{2,0,1:T(8,128)(2,1)S(1)} %get-tuple-element.46), channel_id=1, source_target_pairs={{0,1},{1,2},{2,3},{3,4},{4,5},{5,6},{6,7},{7,0},{8,9},{9,10},{10,1... | collective-permute-start | bytes 101384 | tf_op jit(solution)/shard_map/ppermute | solution.py:22
  328.3 8.4 %collective-permute-start.23 = (bf16[64,2,132]{2,0,1:T(8,128)(2,1)S(1)}, bf16[64,2,132]{2,0,1:T(8,128)(2,1)S(1)}, u32[]{:S(2)}, u32[]{:S(2)}) collective-permute-start(bf16[64,2,132]{2,0,1:T(8,128)(2,1)S(1)} %get-tuple-element.47), channel_id=1, source_target_pairs={{1,0},{2,1},{3,2},{4,3},{5,4},{6,5},{7,6},{0,7},{9,8},{10,9},{11,1... | collective-permute-start | bytes 101384 | tf_op jit(solution)/shard_map/ppermute | solution.py:24
  337.6 9.0 %copy-start.82 = (pred[8,17]{0,1:T(8,128)(4,1)S(1)}, pred[8,17]{0,1:T(8,128)(4,1)}, u32[]{:S(2)}) copy-start(pred[8,17]{0,1:T(8,128)(4,1)} %constant.64) | copy-start | bytes 412
  340.2 19.3 %all-to-all-start.2 = ((f32[128,1,801]{2,1,0:T(1,128)}), f32[128,1,801]{2,1,0:T(1,128)S(1)}, u32[]{:S(2)}, u32[]{:S(2)}) async-start(f32[128,1,801]{2,1,0:T(1,128)} %broadcast_in_dim.27), calls=%async_computation.2 | async-start | bytes 917504 | tf_op jit(solution)/shard_map/all_to_all | solution.py:150
  (62 other events, 197.0 us)

commit v3 on v2

--- a/solution.py
+++ b/solution.py
@@ -114,6 +114,34 @@
         out_shape=jax.ShapeDtypeStruct((rows, count), jnp.float32),
         compiler_params=pltpu.CompilerParams(dimension_semantics=("parallel",)),
     )(values, index)
+
+
+def pick_cells(values, where_to, block=512):
+    levels, rows, cols = values.shape
+    count = where_to.shape[1]
+
+    def body(values_ref, where_ref, out_ref):
+        row_of = where_ref[0:1, :]
+        col_of = where_ref[1:2, :]
+        cols_iota = lax.broadcasted_iota(jnp.int32, (cols, block), 0)
+        onehot = (cols_iota == col_of).astype(jnp.bfloat16)
+        total = jnp.zeros((levels, block), jnp.float32)
+        for row in range(rows):
+            picked = exact_dot(values_ref[:, row, :], onehot)
+            total = total + jnp.where(row_of == row, picked, 0.0)
+        out_ref[...] = total
+
+    return pl.pallas_call(
+        body,
+        grid=(count // block,),
+        in_specs=[
+            pl.BlockSpec((levels, rows, cols), lambda i: (0, 0, 0)),
+            pl.BlockSpec((2, block), lambda i: (0, i)),
+        ],
+        out_specs=pl.BlockSpec((levels, block), lambda i: (0, i)),
+        out_shape=jax.ShapeDtypeStruct((levels, count), jnp.float32),
+        compiler_params=pltpu.CompilerParams(dimension_semantics=("parallel",)),
+    )(values, where_to)
 
 
 def add_columns(values, index_col, width, block=256):
@@ -201,9 +229,9 @@
     occupied = received_cells < cell_count
     target = jnp.where(occupied, received_cells, cell_count)
     flat_state = current.reshape(levels, cell_count)
-    misfits = jnp.where(occupied, pick_columns(flat_state, target) - received_values, 0.0)
+    misfits = jnp.where(occupied, jnp.take(flat_state, target[0], axis=1, mode="clip") - received_values, 0.0)
     square_sum = jnp.sum(misfits * misfits)
-    tangent = add_columns(misfits / profile_dev, target.reshape(-1, 1), cell_count).reshape(
+    tangent = jnp.zeros((levels, cell_count), jnp.float32).at[:, jnp.where(occupied, target, 0)[0]].add(misfits / profile_dev).reshape(
         levels, tile_rows, tile_cols
     )
     grad_in = jnp.zeros(w_in.shape, jnp.float32)

time: 390 us -> 371 us (0.951)
  matrix products: 92.6 us -> 54.6 us
  Pallas kernels: 33 us -> 7.07 us
  other arithmetic: 43.1 us -> 62.2 us
  local copies, waits for them, and re-layouts: 96.5 us -> 115 us
  waiting for transfers between devices: 27.5 us -> 34.3 us
    conv_general_dilated x8, matrix products: 69.8 us -> 28.4 us  [conv_valid(): lax.conv_general_dilated(padded[None], kernel, (1, 1), 'VALID', dimension...]
    scatter-add x0 -> x1, other arithmetic: none -> 25.8 us  [on_device(): jnp.zeros((levels, cell_count), jnp.float32)]
    pallas_call x1 -> x0, Pallas kernels: 14.3 us -> none  [add_columns(): pl.pallas_call(body, grid=(width // block,), in_specs=[pl.BlockSpec((rows...]
    gather x0 -> x1, local copies, waits for them, and re-layouts: none -> 14.2 us  [on_device(): jnp.take(flat_state, target[0], axis=1, mode='clip') - received_values]
    unnamed x196 -> x108, local copies, waits for them, and re-layouts: 30 us -> 43.8 us
    pallas_call x2 -> x1, Pallas kernels: 18.7 us -> 7.07 us  [pick_columns(): pl.pallas_call(body, grid=(count // block,), in_specs=[pl.BlockSpec((rows...]
    ppermute x12, waiting for transfers between devices: 17.9 us -> 23 us  [extended_2(): lax.ppermute(tail, axis, [(i, (i + 1) % count) for i in range(count)])]
    convert_element_type x2 -> x1, other arithmetic: 4.76 us -> 0.01 us  [on_device(): received_cells = arrived[levels:].astype(jnp.int32)]
  transfers between devices with their start and end apart: 27 -> 27, of which waited for: 11 -> 15; matrix products, arithmetic and copies ran while one was open for 37% -> 22% of each run, Pallas kernels for 2% -> 2%
where the time goes in v3:
time: 371 us; the launch traced here: 364 us
  local copies, waits for them, and re-layouts  115 us (31%)
  starting transfers between devices  87.1 us (23%)
  other arithmetic  62.2 us (17%)
  matrix products  54.6 us (15%)
  waiting for transfers between devices  34.3 us (9%)
  Pallas kernels  7.07 us (2%)
  between operations  4.08 us (1%)
    ppermute x12, starting transfers between devices, extended_2(): lax.ppermute(head, axis, [((i + 1) % count, i) for i in range(count)])  45.4 us
    unnamed x108, local copies, waits for them, and re-layouts  43.8 us
    conv_general_dilated x8, matrix products, conv_valid(): lax.conv_general_dilated(padded[None], kernel, (1, 1), 'VALID', dimension...  28.4 us
    dot_general x100, matrix products, kernel_grad(): jnp.einsum('ohw,chw->oc', cotangent, window, preferred_element_type=jnp.f...  26.2 us
    scatter-add x1, other arithmetic, on_device(): jnp.zeros((levels, cell_count), jnp.float32)  25.8 us
    ppermute x12, waiting for transfers between devices, extended_2(): lax.ppermute(tail, axis, [(i, (i + 1) % count) for i in range(count)])  23 us
    gather x1, local copies, waits for them, and re-layouts, on_device(): jnp.take(flat_state, target[0], axis=1, mode='clip') - received_values  14.2 us
    add x2, local copies, waits for them, and re-layouts, on_device(): grad_in = grad_in + kernel_grad(coarse, sensitivity)  12.6 us
  transfers between devices with their start and end apart: 27, of which 15 were waited for; matrix products, arithmetic and copies ran while one was open for 22% of the time, Pallas kernels for 2%

profile of v3, /device:TPU:1, one launch (start us, length us, event | category | flops | bytes accessed | tf_op | source)
XLA Modules:
  0.0 363.9 jit_solution(12184771814034211407)
XLA Ops:
  2.6 2.7 collective-permute-start
  9.4 7.1 %shard_map.110 = f32[33,4096]{1,0:T(8,128)} custom-call(f32[33,1024]{1,0:T(8,128)} %pad_maximum_fusion.7.values_ref, s32[1,4096]{1,0:T(1,128)} %broadcast_select_fusion.index_ref), custom_call_target="tpu_custom_call" | custom-call | tf_op jit(solution)/shard_map/pallas_call | solution.py:106
  21.1 3.6 reshape.699
  24.7 11.9 %all-to-all-start = ((f32[128,1,1056]{2,1,0:T(1,128)}), f32[128,1,1056]{2,1,0:T(1,128)}, u32[]{:S(2)}, u32[]{:S(2)}) async-start(f32[128,1,1056]{2,1,0:T(1,128)} %reshape.699), calls=%async_computation | async-start | bytes 1179648 | tf_op jit(solution)/shard_map/all_to_all | solution.py:226
  38.6 2.9 collective-permute-start.3
  41.8 9.0 %collective-permute-done.2 = f32[32,4,136]{2,0,1:T(8,128)S(1)} collective-permute-done((f32[32,4,136]{2,0,1:T(8,128)S(1)}, f32[32,4,136]{2,0,1:T(8,128)S(1)}, u32[]{:S(2)}, u32[]{:S(2)}) %collective-permute-start.2) | collective-permute-done | bytes 69664 | tf_op jit(solution)/shard_map/ppermute | solution.py:22
  51.6 3.0 select_tanh_fusion.1
  55.6 4.0 %fusion.26 = f32[16,8,17,32]{3,1,2,0:T(8,128)S(1)} fusion(bf16[32,64,5,5]{1,0,3,2:T(8,128)(2,1)S(1)} %copy-done.29, bf16[20,1,7,4,64]{4,2,3,0,1:T(8,128)(2,1)S(1)} %slice.697, bf16[20,1,8,17,64]{4,2,3,0,1:T(8,128)(2,1)S(1)} %fusion.65), kind=kOutput, calls=%fused_computation.142 | convolution fusion | flops 224112640 | bytes 800768 | tf_op jit(solution)/shard_map/conv_general_dilated | solution.py:52
  68.4 2.8 collective-permute-done.5
  71.5 3.8 %collective-permute-start.7 = (f32[32,4,136]{2,0,1:T(8,128)S(1)}, f32[32,4,136]{2,0,1:T(8,128)S(1)}, u32[]{:S(2)}, u32[]{:S(2)}) collective-permute-start(f32[32,4,136]{2,0,1:T(8,128)S(1)} %get-tuple-element.45), channel_id=1, source_target_pairs={{1,0},{2,1},{3,2},{4,3},{5,4},{6,5},{7,6},{0,7},{9,8},{10,9},{11,1... | collective-permute-start | bytes 208904 | tf_op jit(solution)/shard_map/ppermute | solution.py:24
  78.2 3.0 select_tanh_fusion
  83.1 4.0 %fusion.30 = f32[16,8,17,32]{3,1,2,0:T(8,128)S(1)} fusion(bf16[32,64,5,5]{1,0,3,2:T(8,128)(2,1)S(1)} %copy-done.30, bf16[20,1,7,4,64]{4,2,3,0,1:T(8,128)(2,1)S(1)} %slice.709, bf16[20,1,8,17,64]{4,2,3,0,1:T(8,128)(2,1)S(1)} %fusion.67), kind=kOutput, calls=%fused_computation.145 | convolution fusion | flops 224112640 | bytes 800768 | tf_op jit(solution)/shard_map/conv_general_dilated | solution.py:52
  89.7 2.7 slice.721
  92.4 3.3 copy.197
  95.7 2.1 multiply_convert_fusion.2
  98.3 3.9 %reduce.4 = f32[128,1056]{1,0:T(8,128)} reduce(f32[128,1,1056]{2,1,0:T(1,128)} %all-to-all-done, f32[]{:T(128)} %broadcast.370), dimensions={1}, to_apply=%all_to_all.17.reduce_sub_computation | reduce | bytes 1081348 | tf_op jit(solution)/shard_map/all_to_all | solution.py:226
  102.2 5.0 %reshape.700 = f32[128,32,33]{2,1,0:T(8,128)} reshape(f32[128,1056]{1,0:T(8,128)} %reduce.4) | data formatting | bytes 1081344
  107.2 3.6 slice.713
  110.7 2.7 copy.195
  114.1 14.2 %gather_fusion = f32[4096,32]{1,0:T(8,128)} fusion(f32[32,2048]{0,1:T(8,128)S(1)} %bitcast.383, s32[4096]{0:T(1024)S(1)} %broadcast_clamp_fusion), kind=kCustom, calls=%fused_computation | custom fusion | bytes 1064960 | tf_op jit(solution)/shard_map/jit(_take)/gather | solution.py:232
  128.2 4.1 %fusion.238 = (f32[32,128,32]{0,2,1:T(8,128)S(1)}, f32[]{:T(128)}) fusion(f32[33,128,32]{0,2,1:T(8,128)} %bitcast.385, f32[32,128,32]{0,2,1:T(8,128)} %bitcast.386, pred[128,32]{1,0:T(8,128)(4,1)S(1)} %copy.176), kind=kLoop, calls=%fused_computation.420 | loop fusion | flops 524287 | bytes 1576964 | tf_op jit(solution)/shard_map/slice | solution.py:227
  132.4 3.1 fusion.3
  135.5 25.8 %scatter_custom_fusion = f32[32,2048]{0,1:T(8,128)S(1)} fusion(s32[4096]{0:T(1024)S(1)} %bitcast.419, f32[32,4096]{0,1:T(8,128)} %fusion.3, f32[]{:T(128)} %constant.24.clone.1), kind=kCustom, calls=%fused_computation.2 | custom fusion | flops 131072 | bytes 786436 | tf_op jit(solution)/shard_map/scatter-add | solution.py:234
  175.2 2.5 collective-permute-done.9
  178.1 4.2 %collective-permute-start.11 = (f32[32,2,132]{2,0,1:T(8,128)S(1)}, f32[32,2,132]{2,0,1:T(8,128)S(1)}, u32[]{:S(2)}, u32[]{:S(2)}) collective-permute-start(f32[32,2,132]{2,0,1:T(8,128)S(1)} %get-tuple-element.43), channel_id=1, source_target_pairs={{1,0},{2,1},{3,2},{4,3},{5,4},{6,5},{7,6},{0,7},{9,8},{10,9},{11,1... | collective-permute-start | bytes 101384 | tf_op jit(solution)/shard_map/ppermute | solution.py:24
  187.0 2.6 convolution_select_fusion.3
  201.7 5.9 %collective-permute-start.13 = (bf16[64,16,2]{2,0,1:T(8,128)(2,1)S(1)}, bf16[64,16,2]{2,0,1:T(8,128)(2,1)S(1)}, u32[]{:S(2)}, u32[]{:S(2)}) collective-permute-start(bf16[64,16,2]{2,0,1:T(8,128)(2,1)S(1)} %get-tuple-element.55), channel_id=1, source_target_pairs={{8,0},{16,8},{24,16},{32,24},{40,32},{48,40},{56,48},{64,56},{72,6... | collective-permute-start | bytes 12296 | tf_op jit(solution)/shard_map/ppermute | solution.py:24
  209.2 4.3 %collective-permute-start.15 = (bf16[64,2,132]{2,0,1:T(8,128)(2,1)S(1)}, bf16[64,2,132]{2,0,1:T(8,128)(2,1)S(1)}, u32[]{:S(2)}, u32[]{:S(2)}) collective-permute-start(bf16[64,2,132]{2,0,1:T(8,128)(2,1)S(1)} %get-tuple-element.41), channel_id=1, source_target_pairs={{1,0},{2,1},{3,2},{4,3},{5,4},{6,5},{7,6},{0,7},{9,8},{10,9},{11,1... | collective-permute-start | bytes 101384 | tf_op jit(solution)/shard_map/ppermute | solution.py:24
  218.5 4.0 %convolution_select_fusion.2 = f32[16,8,17,32]{3,1,2,0:T(8,128)S(1)} fusion(bf16[64,32,5,5]{0,1,3,2:T(8,128)(2,1)S(1)} %copy-done, bf16[64,20,1,7,4]{0,3,4,1,2:T(8,128)(2,1)S(1)} %slice.757, bf16[64,20,1,8,17]{0,3,4,1,2:T(8,128)(2,1)S(1)} %copy.164, pred[8,17]{0,1:T(8,128)(4,1)S(1)} %copy-done.33), kind=kOutput, calls=%fused_computation.26 | convolution fusion | flops 224182272 | bytes 800904 | tf_op jit(solution)/shard_map/conv_general_dilated | solution.py:52
  223.9 2.1 fusion.235
  232.9 9.3 %collective-permute-start.17 = (f32[32,16,2]{2,0,1:T(8,128)S(1)}, f32[32,16,2]{2,0,1:T(8,128)S(1)}, u32[]{:S(2)}, u32[]{:S(2)}) collective-permute-start(f32[32,16,2]{2,0,1:T(8,128)S(1)} %get-tuple-element.53), channel_id=1, source_target_pairs={{8,0},{16,8},{24,16},{32,24},{40,32},{48,40},{56,48},{64,56},{72,6... | collective-permute-start | bytes 12296 | tf_op jit(solution)/shard_map/ppermute | solution.py:24
  242.3 4.8 %copy.175 = f32[32,64,5,5]{3,2,1,0:T(8,128)} copy(f32[32,64,5,5]{1,0,3,2:T(8,128)S(1)} %add.196) | data formatting | bytes 409600 | tf_op jit(solution)/shard_map/add | solution.py:243
  247.2 5.0 %add.197 = f32[51200]{0:T(1024)S(1)} reshape(f32[32,64,5,5]{3,2,1,0:T(8,128)} %copy.175) | data formatting | bytes 409600 | tf_op jit(solution)/shard_map/add | solution.py:243
  252.5 4.1 %collective-permute-start.19 = (f32[32,2,132]{2,0,1:T(8,128)S(1)}, f32[32,2,132]{2,0,1:T(8,128)S(1)}, u32[]{:S(2)}, u32[]{:S(2)}) collective-permute-start(f32[32,2,132]{2,0,1:T(8,128)S(1)} %get-tuple-element.39), channel_id=1, source_target_pairs={{1,0},{2,1},{3,2},{4,3},{5,4},{6,5},{7,6},{0,7},{9,8},{10,9},{11,1... | collective-permute-start | bytes 101384 | tf_op jit(solution)/shard_map/ppermute | solution.py:24
  259.9 2.6 convolution_select_fusion.1
  272.2 6.4 %collective-permute-start.21 = (bf16[64,16,2]{2,0,1:T(8,128)(2,1)}, bf16[64,16,2]{2,0,1:T(8,128)(2,1)S(1)}, u32[]{:S(2)}, u32[]{:S(2)}) collective-permute-start(bf16[64,16,2]{2,0,1:T(8,128)(2,1)} %get-tuple-element.51), channel_id=1, source_target_pairs={{8,0},{16,8},{24,16},{32,24},{40,32},{48,40},{56,48},{64,56},{72,6... | collective-permute-start | bytes 12296 | tf_op jit(solution)/shard_map/ppermute | solution.py:24
  278.7 7.6 %copy.174 = f32[64,32,5,5]{3,2,1,0:T(8,128)} copy(f32[64,32,5,5]{0,1,3,2:T(8,128)S(1)} %add.194) | data formatting | bytes 409600 | tf_op jit(solution)/shard_map/add | solution.py:248
  286.3 5.0 %add.195 = f32[51200]{0:T(1024)S(1)} reshape(f32[64,32,5,5]{3,2,1,0:T(8,128)} %copy.174) | data formatting | bytes 409600 | tf_op jit(solution)/shard_map/add | solution.py:248
  293.5 11.4 %all-to-all-start.1 = ((f32[128,1,801]{2,1,0:T(1,128)}), f32[128,1,801]{2,1,0:T(1,128)S(1)}, u32[]{:S(2)}, u32[]{:S(2)}) async-start(f32[128,1,801]{2,1,0:T(1,128)} %all_to_all.21), calls=%async_computation.1 | async-start | bytes 917504 | tf_op jit(solution)/shard_map/all_to_all | solution.py:177
  307.1 2.7 collective-permute-start.23
  310.2 5.4 %collective-permute-done.22 = bf16[64,2,132]{2,0,1:T(8,128)(2,1)S(1)} collective-permute-done((bf16[64,2,132]{2,0,1:T(8,128)(2,1)S(1)}, bf16[64,2,132]{2,0,1:T(8,128)(2,1)S(1)}, u32[]{:S(2)}, u32[]{:S(2)}) %collective-permute-start.22) | collective-permute-done | bytes 33824 | tf_op jit(solution)/shard_map/ppermute | solution.py:22
  319.2 7.3 %all-to-all-start.2 = ((f32[128,1,801]{2,1,0:T(1,128)}), f32[128,1,801]{2,1,0:T(1,128)S(1)}, u32[]{:S(2)}, u32[]{:S(2)}) async-start(f32[128,1,801]{2,1,0:T(1,128)} %broadcast_in_dim.42), calls=%async_computation.2 | async-start | bytes 917504 | tf_op jit(solution)/shard_map/all_to_all | solution.py:178
  326.5 5.1 %convolution_select_fusion = f32[16,8,17,32]{3,1,2,0:T(8,128)S(1)} fusion(bf16[64,32,5,5]{0,1,3,2:T(8,128)(2,1)S(1)} %copy-done, bf16[64,20,1,7,4]{0,3,4,1,2:T(8,128)(2,1)S(1)} %slice.854, bf16[64,20,1,8,17]{0,3,4,1,2:T(8,128)(2,1)} %copy-done.9, pred[8,17]{0,1:T(8,128)(4,1)S(1)} %copy-done.35), kind=kOutput, calls=%fused_computation.24 | convolution fusion | flops 224182272 | bytes 800904 | tf_op jit(solution)/shard_map/conv_general_dilated | solution.py:52
  334.1 5.3 %all-to-all-done.2 = f32[128,1,801]{2,1,0:T(1,128)S(1)} async-done(((f32[128,1,801]{2,1,0:T(1,128)}), f32[128,1,801]{2,1,0:T(1,128)S(1)}, u32[]{:S(2)}, u32[]{:S(2)}) %all-to-all-start.2) | async-done | bytes 410144 | tf_op jit(solution)/shard_map/all_to_all | solution.py:178
  341.3 4.4 %reshape.498 = f32[32,64,5,5]{3,2,1,0:T(8,128)} reshape(f32[51200]{0:T(1024)S(1)} %get-tuple-element.48) | data formatting | bytes 409600 | tf_op jit(solution)/shard_map/reshape | solution.py:182
  345.8 5.6 %copy.185 = f32[32,64,5,5]{1,0,3,2:T(8,128)} copy(f32[32,64,5,5]{3,2,1,0:T(8,128)} %reshape.498) | data formatting | bytes 409600
  351.3 4.4 %reshape.497 = f32[64,32,5,5]{3,2,1,0:T(8,128)} reshape(f32[51200]{0:T(1024)S(1)} %get-tuple-element.49) | data formatting | bytes 409600 | tf_op jit(solution)/shard_map/reshape | solution.py:182
  355.8 6.2 %copy.184 = f32[64,32,5,5]{0,1,3,2:T(8,128)} copy(f32[64,32,5,5]{3,2,1,0:T(8,128)} %reshape.497) | data formatting | bytes 409600
  (360 shorter events, 103.6 us)
Async XLA Ops:
  0.6 51.0 %copy-start = (bf16[64,32,5,5]{0,1,3,2:T(8,128)(2,1)S(1)}, bf16[64,32,5,5]{0,1,3,2:T(8,128)(2,1)}, u32[]{:S(2)}) copy-start(bf16[64,32,5,5]{0,1,3,2:T(8,128)(2,1)} %param.12) | copy-start | bytes 307204
  0.6 7.2 %copy-start.28 = (s32[1,128]{1,0:T(1,128)S(1)}, s32[1,128]{1,0:T(1,128)}, u32[]{:S(2)}) copy-start(s32[1,128]{1,0:T(1,128)} %param.11) | copy-start | bytes 1540
  0.7 8.0 %copy-start.18 = (f32[32,1024]{1,0:T(8,128)S(1)}, f32[32,1024]{1,0:T(8,128)}, u32[]{:S(2)}) copy-start(f32[32,1024]{1,0:T(8,128)} %param.9) | copy-start | bytes 393220
  2.6 34.1 %collective-permute-start = (f32[32,16,4]{2,0,1:T(8,128)}, f32[32,16,4]{2,0,1:T(8,128)S(1)}, u32[]{:S(2)}, u32[]{:S(2)}) collective-permute-start(f32[32,16,4]{2,0,1:T(8,128)} %get-tuple-element.60), channel_id=1, source_target_pairs={{0,8},{8,16},{16,24},{24,32},{32,40},{40,48},{48,56},{56,64},{64,7... | collective-permute-start | bytes 24584 | tf_op jit(solution)/shard_map/ppermute | solution.py:22
  5.3 31.5 %collective-permute-start.1 = (f32[32,16,4]{2,0,1:T(8,128)S(1)}, f32[32,16,4]{2,0,1:T(8,128)S(1)}, u32[]{:S(2)}, u32[]{:S(2)}) collective-permute-start(f32[32,16,4]{2,0,1:T(8,128)S(1)} %get-tuple-element.61), channel_id=1, source_target_pairs={{8,0},{16,8},{24,16},{32,24},{40,32},{48,40},{56,48},{64,56},{72,6... | collective-permute-start | bytes 24584 | tf_op jit(solution)/shard_map/ppermute | solution.py:24
  21.1 15.6 %copy-start.25 = (s32[16,128]{1,0:T(8,128)S(1)}, s32[16,128]{1,0:T(8,128)}, u32[]{:S(2)}) copy-start(s32[16,128]{1,0:T(8,128)} %param.8) | copy-start | bytes 24580
  24.7 73.1 %all-to-all-start = ((f32[128,1,1056]{2,1,0:T(1,128)}), f32[128,1,1056]{2,1,0:T(1,128)}, u32[]{:S(2)}, u32[]{:S(2)}) async-start(f32[128,1,1056]{2,1,0:T(1,128)} %reshape.699), calls=%async_computation | async-start | bytes 1179648 | tf_op jit(solution)/shard_map/all_to_all | solution.py:226
  36.7 170.9 %copy-start.21 = (f32[20]{0:T(128)}, f32[20]{0:T(128)S(1)}, u32[]{:S(2)}) copy-start(f32[20]{0:T(128)S(1)} %and_convert_fusion) | copy-start | bytes 244
  36.7 14.2 %copy-start.2 = (f32[32,16,4]{2,0,1:T(8,128)}, f32[32,16,4]{2,0,1:T(8,128)S(1)}, u32[]{:S(2)}) copy-start(f32[32,16,4]{2,0,1:T(8,128)S(1)} %collective-permute-done) | copy-start | bytes 24580
  36.7 14.2 %copy-start.3 = (f32[32,16,4]{2,0,1:T(8,128)}, f32[32,16,4]{2,0,1:T(8,128)S(1)}, u32[]{:S(2)}) copy-start(f32[32,16,4]{2,0,1:T(8,128)S(1)} %collective-permute-done.1) | copy-start | bytes 24580
  37.1 13.7 %collective-permute-start.2 = (f32[32,4,136]{2,0,1:T(8,128)S(1)}, f32[32,4,136]{2,0,1:T(8,128)S(1)}, u32[]{:S(2)}, u32[]{:S(2)}) collective-permute-start(f32[32,4,136]{2,0,1:T(8,128)S(1)} %get-tuple-element.46), channel_id=1, source_target_pairs={{0,1},{1,2},{2,3},{3,4},{4,5},{5,6},{6,7},{7,0},{8,9},{9,10},{10,1... | collective-permute-start | bytes 208904 | tf_op jit(solution)/shard_map/ppermute | solution.py:22
  38.6 12.2 %collective-permute-start.3 = (f32[32,4,136]{2,0,1:T(8,128)S(1)}, f32[32,4,136]{2,0,1:T(8,128)S(1)}, u32[]{:S(2)}, u32[]{:S(2)}) collective-permute-start(f32[32,4,136]{2,0,1:T(8,128)S(1)} %get-tuple-element.47), channel_id=1, source_target_pairs={{1,0},{2,1},{3,2},{4,3},{5,4},{6,5},{7,6},{0,7},{9,8},{10,9},{11,1... | collective-permute-start | bytes 208904 | tf_op jit(solution)/shard_map/ppermute | solution.py:24
  63.1 5.3 %collective-permute-start.4 = (f32[32,16,4]{2,0,1:T(8,128)S(1)}, f32[32,16,4]{2,0,1:T(8,128)S(1)}, u32[]{:S(2)}, u32[]{:S(2)}) collective-permute-start(f32[32,16,4]{2,0,1:T(8,128)S(1)} %get-tuple-element.58), channel_id=1, source_target_pairs={{0,8},{8,16},{16,24},{24,32},{32,40},{40,48},{48,56},{56,64},{64,7... | collective-permute-start | bytes 24584 | tf_op jit(solution)/shard_map/ppermute | solution.py:22
  65.0 6.1 %collective-permute-start.5 = (f32[32,16,4]{2,0,1:T(8,128)S(1)}, f32[32,16,4]{2,0,1:T(8,128)S(1)}, u32[]{:S(2)}, u32[]{:S(2)}) collective-permute-start(f32[32,16,4]{2,0,1:T(8,128)S(1)} %get-tuple-element.59), channel_id=1, source_target_pairs={{8,0},{16,8},{24,16},{32,24},{40,32},{48,40},{56,48},{64,56},{72,6... | collective-permute-start | bytes 24584 | tf_op jit(solution)/shard_map/ppermute | solution.py:24
  65.1 150.4 %copy-start.26 = (bf16[20]{0:T(256)(128)(2,1)}, bf16[20]{0:T(256)(128)(2,1)S(1)}, u32[]{:S(2)}) copy-start(bf16[20]{0:T(256)(128)(2,1)S(1)} %fusion.232) | copy-start | bytes 124
  71.4 6.0 %collective-permute-start.6 = (f32[32,4,136]{2,0,1:T(8,128)S(1)}, f32[32,4,136]{2,0,1:T(8,128)S(1)}, u32[]{:S(2)}, u32[]{:S(2)}) collective-permute-start(f32[32,4,136]{2,0,1:T(8,128)S(1)} %get-tuple-element.44), channel_id=1, source_target_pairs={{0,1},{1,2},{2,3},{3,4},{4,5},{5,6},{6,7},{7,0},{8,9},{9,10},{10,1... | collective-permute-start | bytes 208904 | tf_op jit(solution)/shard_map/ppermute | solution.py:22
  71.5 5.9 %collective-permute-start.7 = (f32[32,4,136]{2,0,1:T(8,128)S(1)}, f32[32,4,136]{2,0,1:T(8,128)S(1)}, u32[]{:S(2)}, u32[]{:S(2)}) collective-permute-start(f32[32,4,136]{2,0,1:T(8,128)S(1)} %get-tuple-element.45), channel_id=1, source_target_pairs={{1,0},{2,1},{3,2},{4,3},{5,4},{6,5},{7,6},{0,7},{9,8},{10,9},{11,1... | collective-permute-start | bytes 208904 | tf_op jit(solution)/shard_map/ppermute | solution.py:24
  128.2 4.1 %copy-start.1 = (f32[4096,32]{1,0:T(8,128)S(1)}, f32[4096,32]{1,0:T(8,128)}, u32[]{:S(2)}) copy-start(f32[4096,32]{1,0:T(8,128)} %gather_fusion) | copy-start | bytes 1572868
  170.2 5.0 %collective-permute-start.8 = (f32[32,16,2]{2,0,1:T(8,128)S(1)}, f32[32,16,2]{2,0,1:T(8,128)S(1)}, u32[]{:S(2)}, u32[]{:S(2)}) collective-permute-start(f32[32,16,2]{2,0,1:T(8,128)S(1)} %get-tuple-element.56), channel_id=1, source_target_pairs={{0,8},{8,16},{16,24},{24,32},{32,40},{40,48},{48,56},{56,64},{64,7... | collective-permute-start | bytes 12296 | tf_op jit(solution)/shard_map/ppermute | solution.py:22
  171.9 5.8 %collective-permute-start.9 = (f32[32,16,2]{2,0,1:T(8,128)S(1)}, f32[32,16,2]{2,0,1:T(8,128)S(1)}, u32[]{:S(2)}, u32[]{:S(2)}) collective-permute-start(f32[32,16,2]{2,0,1:T(8,128)S(1)} %get-tuple-element.57), channel_id=1, source_target_pairs={{8,0},{16,8},{24,16},{32,24},{40,32},{48,40},{56,48},{64,56},{72,6... | collective-permute-start | bytes 12296 | tf_op jit(solution)/shard_map/ppermute | solution.py:24
  175.2 9.3 %copy-start.5 = (f32[32,16,2]{2,0,1:T(8,128)}, f32[32,16,2]{2,0,1:T(8,128)S(1)}, u32[]{:S(2)}) copy-start(f32[32,16,2]{2,0,1:T(8,128)S(1)} %collective-permute-done.8) | copy-start | bytes 12292
  177.7 6.8 %copy-start.7 = (f32[32,16,2]{2,0,1:T(8,128)}, f32[32,16,2]{2,0,1:T(8,128)S(1)}, u32[]{:S(2)}) copy-start(f32[32,16,2]{2,0,1:T(8,128)S(1)} %collective-permute-done.9) | copy-start | bytes 12292
  178.0 5.7 %collective-permute-start.10 = (f32[32,2,132]{2,0,1:T(8,128)S(1)}, f32[32,2,132]{2,0,1:T(8,128)S(1)}, u32[]{:S(2)}, u32[]{:S(2)}) collective-permute-start(f32[32,2,132]{2,0,1:T(8,128)S(1)} %get-tuple-element.42), channel_id=1, source_target_pairs={{0,1},{1,2},{2,3},{3,4},{4,5},{5,6},{6,7},{7,0},{8,9},{9,10},{10,1... | collective-permute-start | bytes 101384 | tf_op jit(solution)/shard_map/ppermute | solution.py:22
  178.1 5.6 %collective-permute-start.11 = (f32[32,2,132]{2,0,1:T(8,128)S(1)}, f32[32,2,132]{2,0,1:T(8,128)S(1)}, u32[]{:S(2)}, u32[]{:S(2)}) collective-permute-start(f32[32,2,132]{2,0,1:T(8,128)S(1)} %get-tuple-element.43), channel_id=1, source_target_pairs={{1,0},{2,1},{3,2},{4,3},{5,4},{6,5},{7,6},{0,7},{9,8},{10,9},{11,1... | collective-permute-start | bytes 101384 | tf_op jit(solution)/shard_map/ppermute | solution.py:24
  198.8 8.8 %copy-start.6 = (f32[32,16,2]{2,0,1:T(8,128)S(1)}, f32[32,16,2]{2,0,1:T(8,128)}, u32[]{:S(2)}) copy-start(f32[32,16,2]{2,0,1:T(8,128)} %copy-done.5) | copy-start | bytes 12292
  198.8 8.7 %copy-start.8 = (f32[32,16,2]{2,0,1:T(8,128)S(1)}, f32[32,16,2]{2,0,1:T(8,128)}, u32[]{:S(2)}) copy-start(f32[32,16,2]{2,0,1:T(8,128)} %copy-done.7) | copy-start | bytes 12292
  200.7 7.8 %collective-permute-start.12 = (bf16[64,16,2]{2,0,1:T(8,128)(2,1)S(1)}, bf16[64,16,2]{2,0,1:T(8,128)(2,1)S(1)}, u32[]{:S(2)}, u32[]{:S(2)}) collective-permute-start(bf16[64,16,2]{2,0,1:T(8,128)(2,1)S(1)} %get-tuple-element.54), channel_id=1, source_target_pairs={{0,8},{8,16},{16,24},{24,32},{32,40},{40,48},{48,56},{56,64},{64,7... | collective-permute-start | bytes 12296 | tf_op jit(solution)/shard_map/ppermute | solution.py:22
  201.7 7.0 %collective-permute-start.13 = (bf16[64,16,2]{2,0,1:T(8,128)(2,1)S(1)}, bf16[64,16,2]{2,0,1:T(8,128)(2,1)S(1)}, u32[]{:S(2)}, u32[]{:S(2)}) collective-permute-start(bf16[64,16,2]{2,0,1:T(8,128)(2,1)S(1)} %get-tuple-element.55), channel_id=1, source_target_pairs={{8,0},{16,8},{24,16},{32,24},{40,32},{48,40},{56,48},{64,56},{72,6... | collective-permute-start | bytes 12296 | tf_op jit(solution)/shard_map/ppermute | solution.py:24
  207.9 5.9 %copy-start.15 = (f32[64,32,5,5]{0,1,3,2:T(8,128)}, f32[64,32,5,5]{0,1,3,2:T(8,128)S(1)}, u32[]{:S(2)}) copy-start(f32[64,32,5,5]{0,1,3,2:T(8,128)S(1)} %constant_dynamic-update-slice_fusion) | copy-start | bytes 614404
  209.1 6.1 %collective-permute-start.14 = (bf16[64,2,132]{2,0,1:T(8,128)(2,1)S(1)}, bf16[64,2,132]{2,0,1:T(8,128)(2,1)S(1)}, u32[]{:S(2)}, u32[]{:S(2)}) collective-permute-start(bf16[64,2,132]{2,0,1:T(8,128)(2,1)S(1)} %get-tuple-element.40), channel_id=1, source_target_pairs={{0,1},{1,2},{2,3},{3,4},{4,5},{5,6},{6,7},{7,0},{8,9},{9,10},{10,1... | collective-permute-start | bytes 101384 | tf_op jit(solution)/shard_map/ppermute | solution.py:22
  209.2 6.2 %collective-permute-start.15 = (bf16[64,2,132]{2,0,1:T(8,128)(2,1)S(1)}, bf16[64,2,132]{2,0,1:T(8,128)(2,1)S(1)}, u32[]{:S(2)}, u32[]{:S(2)}) collective-permute-start(bf16[64,2,132]{2,0,1:T(8,128)(2,1)S(1)} %get-tuple-element.41), channel_id=1, source_target_pairs={{1,0},{2,1},{3,2},{4,3},{5,4},{6,5},{7,6},{0,7},{9,8},{10,9},{11,1... | collective-permute-start | bytes 101384 | tf_op jit(solution)/shard_map/ppermute | solution.py:24
  231.5 10.7 %copy-start.14 = (f32[32,64,5,5]{1,0,3,2:T(8,128)S(1)}, f32[32,64,5,5]{1,0,3,2:T(8,128)}, u32[]{:S(2)}) copy-start(f32[32,64,5,5]{1,0,3,2:T(8,128)} %copy-done.13) | copy-start | bytes 614404
  231.5 10.7 %copy-start.20 = (f32[32,64,5]{1,0,2:T(8,128)S(1)}, f32[32,64,5]{1,0,2:T(8,128)}, u32[]{:S(2)}) copy-start(f32[32,64,5]{1,0,2:T(8,128)} %copy-done.19) | copy-start | bytes 122884
  232.8 19.3 %collective-permute-start.16 = (f32[32,16,2]{2,0,1:T(8,128)S(1)}, f32[32,16,2]{2,0,1:T(8,128)S(1)}, u32[]{:S(2)}, u32[]{:S(2)}) collective-permute-start(f32[32,16,2]{2,0,1:T(8,128)S(1)} %get-tuple-element.52), channel_id=1, source_target_pairs={{0,8},{8,16},{16,24},{24,32},{32,40},{40,48},{48,56},{56,64},{64,7... | collective-permute-start | bytes 12296 | tf_op jit(solution)/shard_map/ppermute | solution.py:22
  232.9 19.2 %collective-permute-start.17 = (f32[32,16,2]{2,0,1:T(8,128)S(1)}, f32[32,16,2]{2,0,1:T(8,128)S(1)}, u32[]{:S(2)}, u32[]{:S(2)}) collective-permute-start(f32[32,16,2]{2,0,1:T(8,128)S(1)} %get-tuple-element.53), channel_id=1, source_target_pairs={{8,0},{16,8},{24,16},{32,24},{40,32},{48,40},{56,48},{64,56},{72,6... | collective-permute-start | bytes 12296 | tf_op jit(solution)/shard_map/ppermute | solution.py:24
  252.1 6.1 %copy-start.22 = (f32[20]{0:T(128)S(1)}, f32[20]{0:T(128)}, u32[]{:S(2)}) copy-start(f32[20]{0:T(128)} %copy-done.21) | copy-start | bytes 244
  252.5 5.8 %collective-permute-start.18 = (f32[32,2,132]{2,0,1:T(8,128)S(1)}, f32[32,2,132]{2,0,1:T(8,128)S(1)}, u32[]{:S(2)}, u32[]{:S(2)}) collective-permute-start(f32[32,2,132]{2,0,1:T(8,128)S(1)} %get-tuple-element.38), channel_id=1, source_target_pairs={{0,1},{1,2},{2,3},{3,4},{4,5},{5,6},{6,7},{7,0},{8,9},{9,10},{10,1... | collective-permute-start | bytes 101384 | tf_op jit(solution)/shard_map/ppermute | solution.py:22
  252.5 5.7 %collective-permute-start.19 = (f32[32,2,132]{2,0,1:T(8,128)S(1)}, f32[32,2,132]{2,0,1:T(8,128)S(1)}, u32[]{:S(2)}, u32[]{:S(2)}) collective-permute-start(f32[32,2,132]{2,0,1:T(8,128)S(1)} %get-tuple-element.39), channel_id=1, source_target_pairs={{1,0},{2,1},{3,2},{4,3},{5,4},{6,5},{7,6},{0,7},{9,8},{10,9},{11,1... | collective-permute-start | bytes 101384 | tf_op jit(solution)/shard_map/ppermute | solution.py:24
  270.5 8.1 %copy-start.16 = (f32[64,32,5,5]{0,1,3,2:T(8,128)S(1)}, f32[64,32,5,5]{0,1,3,2:T(8,128)}, u32[]{:S(2)}) copy-start(f32[64,32,5,5]{0,1,3,2:T(8,128)} %copy-done.15) | copy-start | bytes 614404
  272.1 33.1 %collective-permute-start.20 = (bf16[64,16,2]{2,0,1:T(8,128)(2,1)}, bf16[64,16,2]{2,0,1:T(8,128)(2,1)S(1)}, u32[]{:S(2)}, u32[]{:S(2)}) collective-permute-start(bf16[64,16,2]{2,0,1:T(8,128)(2,1)} %get-tuple-element.50), channel_id=1, source_target_pairs={{0,8},{8,16},{16,24},{24,32},{32,40},{40,48},{48,56},{56,64},{64,7... | collective-permute-start | bytes 12296 | tf_op jit(solution)/shard_map/ppermute | solution.py:22
  272.2 33.1 %collective-permute-start.21 = (bf16[64,16,2]{2,0,1:T(8,128)(2,1)}, bf16[64,16,2]{2,0,1:T(8,128)(2,1)S(1)}, u32[]{:S(2)}, u32[]{:S(2)}) collective-permute-start(bf16[64,16,2]{2,0,1:T(8,128)(2,1)} %get-tuple-element.51), channel_id=1, source_target_pairs={{8,0},{16,8},{24,16},{32,24},{40,32},{48,40},{56,48},{64,56},{72,6... | collective-permute-start | bytes 12296 | tf_op jit(solution)/shard_map/ppermute | solution.py:24
  291.3 13.6 %copy-start.23 = (f32[20]{0:T(128)S(1)}, f32[20]{0:T(128)}, u32[]{:S(2)}) copy-start(f32[20]{0:T(128)} %copy-done.21) | copy-start | bytes 244
  293.5 24.4 %all-to-all-start.1 = ((f32[128,1,801]{2,1,0:T(1,128)}), f32[128,1,801]{2,1,0:T(1,128)S(1)}, u32[]{:S(2)}, u32[]{:S(2)}) async-start(f32[128,1,801]{2,1,0:T(1,128)} %all_to_all.21), calls=%async_computation.1 | async-start | bytes 917504 | tf_op jit(solution)/shard_map/all_to_all | solution.py:177
  305.2 10.4 %copy-start.27 = (bf16[20]{0:T(256)(128)(2,1)S(1)}, bf16[20]{0:T(256)(128)(2,1)}, u32[]{:S(2)}) copy-start(bf16[20]{0:T(256)(128)(2,1)} %copy-done.26) | copy-start | bytes 124
  305.6 10.0 %collective-permute-start.22 = (bf16[64,2,132]{2,0,1:T(8,128)(2,1)S(1)}, bf16[64,2,132]{2,0,1:T(8,128)(2,1)S(1)}, u32[]{:S(2)}, u32[]{:S(2)}) collective-permute-start(bf16[64,2,132]{2,0,1:T(8,128)(2,1)S(1)} %get-tuple-element.36), channel_id=1, source_target_pairs={{0,1},{1,2},{2,3},{3,4},{4,5},{5,6},{6,7},{7,0},{8,9},{9,10},{10,1... | collective-permute-start | bytes 101384 | tf_op jit(solution)/shard_map/ppermute | solution.py:22
  307.1 8.5 %collective-permute-start.23 = (bf16[64,2,132]{2,0,1:T(8,128)(2,1)S(1)}, bf16[64,2,132]{2,0,1:T(8,128)(2,1)S(1)}, u32[]{:S(2)}, u32[]{:S(2)}) collective-permute-start(bf16[64,2,132]{2,0,1:T(8,128)(2,1)S(1)} %get-tuple-element.37), channel_id=1, source_target_pairs={{1,0},{2,1},{3,2},{4,3},{5,4},{6,5},{7,6},{0,7},{9,8},{10,9},{11,1... | collective-permute-start | bytes 101384 | tf_op jit(solution)/shard_map/ppermute | solution.py:24
  316.6 9.9 %copy-start.35 = (pred[8,17]{0,1:T(8,128)(4,1)S(1)}, pred[8,17]{0,1:T(8,128)(4,1)}, u32[]{:S(2)}) copy-start(pred[8,17]{0,1:T(8,128)(4,1)} %constant.83) | copy-start | bytes 412
  319.2 20.1 %all-to-all-start.2 = ((f32[128,1,801]{2,1,0:T(1,128)}), f32[128,1,801]{2,1,0:T(1,128)S(1)}, u32[]{:S(2)}, u32[]{:S(2)}) async-start(f32[128,1,801]{2,1,0:T(1,128)} %broadcast_in_dim.42), calls=%async_computation.2 | async-start | bytes 917504 | tf_op jit(solution)/shard_map/all_to_all | solution.py:178
  (15 other events, 17.5 us)

commit v4 on v3

--- a/solution.py
+++ b/solution.py
@@ -12,20 +12,41 @@
 diffusion = 0.2
 
 
-def extended_2(cells, sides, width):
-    for axis, dim in sides:
-        count = lax.axis_size(axis)
-        head = lax.slice_in_dim(cells, 0, width, axis=dim)
-        tail = lax.slice_in_dim(cells, cells.shape[dim] - width, cells.shape[dim], axis=dim)
-        cells = jnp.concatenate(
-            [
-                lax.ppermute(tail, axis, [(i, (i + 1) % count) for i in range(count)]),
-                cells,
-                lax.ppermute(head, axis, [((i + 1) % count, i) for i in range(count)]),
-            ],
-            axis=dim,
-        )
-    return cells
+def extended_2(cells, width):
+    n_lon = lax.axis_size("lon")
+    n_lat = lax.axis_size("lat")
+
+    def shift(block, d_lon, d_lat):
+        pairs = []
+        for i in range(n_lon):
+            for j in range(n_lat):
+                if 0 <= j + d_lat < n_lat:
+                    pairs.append((i * n_lat + j, ((i + d_lon) % n_lon) * n_lat + j + d_lat))
+        return lax.ppermute(block, ("lon", "lat"), pairs)
+
+    rows, cols = cells.shape[1], cells.shape[2]
+    low_rows, high_rows = cells[:, rows - width :], cells[:, :width]
+    top = jnp.concatenate(
+        [
+            shift(low_rows[:, :, cols - width :], 1, 1),
+            shift(low_rows, 0, 1),
+            shift(low_rows[:, :, :width], -1, 1),
+        ],
+        axis=2,
+    )
+    middle = jnp.concatenate(
+        [shift(cells[:, :, cols - width :], 1, 0), cells, shift(cells[:, :, :width], -1, 0)],
+        axis=2,
+    )
+    bottom = jnp.concatenate(
+        [
+            shift(high_rows[:, :, cols - width :], 1, -1),
+            shift(high_rows, 0, -1),
+            shift(high_rows[:, :, :width], -1, -1),
+        ],
+        axis=2,
+    )
+    return jnp.concatenate([top, middle, bottom], axis=1)
 
 
 def laplace(extended, border):
@@ -199,7 +220,7 @@
     current = state
     history = []
     for step_index in range(STEPS):
-        extended = extended_2(current, (("lon", 2), ("lat", 1)), 4) * inside_rows(tile_rows, 4)
+        extended = extended_2(current, 4)
         coarse = extended.astype(jnp.bfloat16)
         activity = jnp.tanh(conv_valid(coarse, w_in))
         hidden = (activity * inside_rows(tile_rows, 2)).astype(jnp.bfloat16)
@@ -242,13 +263,11 @@
         forcing_low = forcing.astype(jnp.bfloat16)
         grad_out = grad_out + kernel_grad(hidden, forcing_low)
         derivative = 1.0 - activity * activity
-        beside_all = extended_2(forcing, (("lon", 2), ("lat", 1)), 2) * inside_rows(tile_rows, 2)
+        beside_all = extended_2(forcing, 2)
         spread = conv_valid(beside_all.astype(jnp.bfloat16), back_out)
         sensitivity = (spread * derivative[:, 2:-2, 2:-2]).astype(jnp.bfloat16)
         grad_in = grad_in + kernel_grad(coarse, sensitivity)
-        margin = extended_2(sensitivity, (("lon", 2), ("lat", 1)), 2) * inside_rows(
-            tile_rows, 2
-        ).astype(jnp.bfloat16)
+        margin = extended_2(sensitivity, 2)
         tangent = tangent + diffusion * laplace(beside_all, 2) + conv_valid(margin, back_in)
     grad_in, grad_out, square_sum = all_sum((grad_in, grad_out, square_sum), ("lon", "lat"))
     misfit = square_sum / (2.0 * profile_dev * devices * levels)

time: 371 us -> 506 us (1.36)
  starting transfers between devices: 87.1 us -> 202 us
  waiting for transfers between devices: 34.3 us -> 47.2 us
  local copies, waits for them, and re-layouts: 115 us -> 127 us
    ppermute x24 -> x48, starting transfers between devices: 56.4 us -> 161 us  [shift(): return lax.ppermute(block, ('lon', 'lat'), pairs)]
    ppermute x24 -> x48, waiting for transfers between devices: 28.7 us -> 41 us  [shift(): return lax.ppermute(block, ('lon', 'lat'), pairs)]
    all_to_all x1, starting transfers between devices: 11.4 us -> 17.4 us  [all_sum(): mine = jnp.sum(lax.all_to_all(rows, axes, 0, 0, tiled=True), axis=0)]
    slice x12 -> x18, local copies, waits for them, and re-layouts: 2.37 us -> 8.19 us  [the longest x6 3.73 us: extended_2(): cells[:, :, cols - width:]]
    all_to_all x1, starting transfers between devices: 7.28 us -> 12.8 us  [all_sum(): lax.all_to_all(jnp.broadcast_to(mine[None], (count, chunk)), axes, 0, 0,...]
    unnamed x108 -> x166, local copies, waits for them, and re-layouts: 43.8 us -> 49 us
  transfers between devices with their start and end apart: 27 -> 51, of which waited for: 15 -> 18; matrix products, arithmetic and copies ran while one was open for 22% -> 17% of each run, Pallas kernels for 2% -> 1%
where the time goes in v4:
time: 506 us; the launch traced here: 499 us
  starting transfers between devices  202 us (40%)
  local copies, waits for them, and re-layouts  127 us (25%)
  other arithmetic  57.5 us (11%)
  matrix products  53.6 us (11%)
  waiting for transfers between devices  47.2 us (9%)
  Pallas kernels  7.04 us (1%)
    ppermute x48, starting transfers between devices, shift(): return lax.ppermute(block, ('lon', 'lat'), pairs)  161 us
    unnamed x166, local copies, waits for them, and re-layouts  49 us
    ppermute x48, waiting for transfers between devices, shift(): return lax.ppermute(block, ('lon', 'lat'), pairs)  41 us
    conv_general_dilated x8, matrix products, conv_valid(): lax.conv_general_dilated(padded[None], kernel, (1, 1), 'VALID', dimension...  27.3 us
    dot_general x100, matrix products, kernel_grad(): jnp.einsum('ohw,chw->oc', cotangent, window, preferred_element_type=jnp.f...  26.2 us
    scatter-add x1, other arithmetic, on_device(): jnp.zeros((levels, cell_count), jnp.float32)  25.2 us
    all_to_all x1, starting transfers between devices, all_sum(): mine = jnp.sum(lax.all_to_all(rows, axes, 0, 0, tiled=True), axis=0)  17.4 us
    gather x1, local copies, waits for them, and re-layouts, on_device(): jnp.take(flat_state, target[0], axis=1, mode='clip') - received_values  14.1 us
  transfers between devices with their start and end apart: 51, of which 18 were waited for; matrix products, arithmetic and copies ran while one was open for 17% of the time, Pallas kernels for 1%

profile of v4, /device:TPU:1, one launch (start us, length us, event | category | flops | bytes accessed | tf_op | source)
XLA Modules:
  0.0 498.6 jit_solution(6092096430422480176)
XLA Ops:
  2.4 4.3 collective-permute-start.1
  8.8 6.8 %collective-permute-start = (f32[32,4,4]{2,0,1:T(8,128)}, f32[32,4,4]{2,0,1:T(8,128)}, u32[]{:S(2)}, u32[]{:S(2)}) collective-permute-start(f32[32,4,4]{2,0,1:T(8,128)} %get-tuple-element.74), channel_id=1, source_target_pairs={{0,9},{1,10},{2,11},{3,12},{4,13},{5,14},{6,15},{8,17},{9,18},{10,... | collective-permute-start | bytes 6152 | tf_op jit(solution)/shard_map/ppermute | solution.py:25
  19.1 7.0 %shard_map.110 = f32[33,4096]{1,0:T(8,128)} custom-call(f32[33,1024]{1,0:T(8,128)} %pad_maximum_fusion.43.values_ref, s32[1,4096]{1,0:T(1,128)} %broadcast_select_fusion.index_ref), custom_call_target="tpu_custom_call" | custom-call | tf_op jit(solution)/shard_map/pallas_call | solution.py:127
  28.0 3.6 reshape.604
  31.5 10.7 %all-to-all-start = ((f32[128,1,1056]{2,1,0:T(1,128)}), f32[128,1,1056]{2,1,0:T(1,128)}, u32[]{:S(2)}, u32[]{:S(2)}) async-start(f32[128,1,1056]{2,1,0:T(1,128)} %reshape.604), calls=%async_computation | async-start | bytes 1179648 | tf_op jit(solution)/shard_map/all_to_all | solution.py:247
  46.7 4.8 collective-permute-done.7
  51.5 5.7 %collective-permute-start.2 = (f32[32,4,4]{2,0,1:T(8,128)S(1)}, f32[32,4,4]{2,0,1:T(8,128)S(1)}, u32[]{:S(2)}, u32[]{:S(2)}) collective-permute-start(f32[32,4,4]{2,0,1:T(8,128)S(1)} %copy-done.44), channel_id=1, source_target_pairs={{0,121},{1,122},{2,123},{3,124},{4,125},{5,126},{6,127},{8,1},{9,2... | collective-permute-start | bytes 6152 | tf_op jit(solution)/shard_map/ppermute | solution.py:25
  65.1 4.0 fusion.26
  73.5 4.7 collective-permute-start.12
  83.7 4.2 collective-permute-start.8
  95.3 3.7 collective-permute-done.15
  99.0 11.5 %collective-permute-start.10 = (f32[32,4,4]{2,0,1:T(8,128)S(1)}, f32[32,4,4]{2,0,1:T(8,128)S(1)}, u32[]{:S(2)}, u32[]{:S(2)}) collective-permute-start(f32[32,4,4]{2,0,1:T(8,128)S(1)} %copy-done.47), channel_id=1, source_target_pairs={{0,121},{1,122},{2,123},{3,124},{4,125},{5,126},{6,127},{8,1},{9,2... | collective-permute-start | bytes 6152 | tf_op jit(solution)/shard_map/ppermute | solution.py:25
  116.9 4.0 fusion.30
  133.3 4.0 reduce.4
  137.3 4.7 reshape.605
  142.0 3.5 slice.881
  148.8 14.1 %gather_fusion = f32[4096,32]{1,0:T(8,128)} fusion(f32[32,2048]{0,1:T(8,128)S(1)} %bitcast.379, s32[4096]{0:T(1024)S(1)} %broadcast_clamp_fusion), kind=kCustom, calls=%fused_computation | custom fusion | bytes 1064960 | tf_op jit(solution)/shard_map/jit(_take)/gather | solution.py:253
  162.9 4.1 fusion.329
  170.2 25.2 %scatter_custom_fusion = f32[32,2048]{0,1:T(8,128)S(1)} fusion(s32[4096]{0:T(1024)S(1)} %bitcast.407, f32[32,4096]{0,1:T(8,128)} %fusion.3, f32[]{:T(128)} %constant.7.clone.1), kind=kCustom, calls=%fused_computation.2 | custom fusion | flops 131072 | bytes 786436 | tf_op jit(solution)/shard_map/scatter-add | solution.py:255
  198.7 3.8 collective-permute-start.17
  210.9 8.2 %collective-permute-start.20 = (f32[32,16,2]{2,0,1:T(8,128)S(1)}, f32[32,16,2]{2,0,1:T(8,128)S(1)}, u32[]{:S(2)}, u32[]{:S(2)}) collective-permute-start(f32[32,16,2]{2,0,1:T(8,128)S(1)} %get-tuple-element.65), channel_id=1, source_target_pairs={{0,120},{1,121},{2,122},{3,123},{4,124},{5,125},{6,126},{7,127},{8... | collective-permute-start | bytes 12296 | tf_op jit(solution)/shard_map/ppermute | solution.py:25
  226.2 15.8 %collective-permute-start.18 = (f32[32,2,2]{2,0,1:T(8,128)S(1)}, f32[32,2,2]{2,0,1:T(8,128)S(1)}, u32[]{:S(2)}, u32[]{:S(2)}) collective-permute-start(f32[32,2,2]{2,0,1:T(8,128)S(1)} %get-tuple-element.61), channel_id=1, source_target_pairs={{0,121},{1,122},{2,123},{3,124},{4,125},{5,126},{6,127},{8,1},{9,2... | collective-permute-start | bytes 1544 | tf_op jit(solution)/shard_map/ppermute | solution.py:25
  254.3 4.0 collective-permute-start.25
  264.8 4.5 collective-permute-start.24
  272.1 14.5 %collective-permute-start.26 = (bf16[64,2,2]{2,0,1:T(8,128)(2,1)S(1)}, bf16[64,2,2]{2,0,1:T(8,128)(2,1)S(1)}, u32[]{:S(2)}, u32[]{:S(2)}) collective-permute-start(bf16[64,2,2]{2,0,1:T(8,128)(2,1)S(1)} %get-tuple-element.53), channel_id=1, source_target_pairs={{0,121},{1,122},{2,123},{3,124},{4,125},{5,126},{6,127},{8,1},{9,2... | collective-permute-start | bytes 1544 | tf_op jit(solution)/shard_map/ppermute | solution.py:25
  296.4 4.0 convolution_select_fusion.2
  307.8 3.3 collective-permute-start.33
  318.0 3.5 collective-permute-start.32
  321.6 6.1 %collective-permute-start.36 = (f32[32,16,2]{2,0,1:T(8,128)S(1)}, f32[32,16,2]{2,0,1:T(8,128)S(1)}, u32[]{:S(2)}, u32[]{:S(2)}) collective-permute-start(f32[32,16,2]{2,0,1:T(8,128)S(1)} %get-tuple-element.49), channel_id=1, source_target_pairs={{0,120},{1,121},{2,122},{3,123},{4,124},{5,125},{6,126},{7,127},{8... | collective-permute-start | bytes 12296 | tf_op jit(solution)/shard_map/ppermute | solution.py:25
  327.9 4.8 copy.211
  332.7 5.0 add.156
  340.5 3.5 collective-permute-done.39
  344.1 11.4 %collective-permute-start.34 = (f32[32,2,2]{2,0,1:T(8,128)S(1)}, f32[32,2,2]{2,0,1:T(8,128)S(1)}, u32[]{:S(2)}, u32[]{:S(2)}) collective-permute-start(f32[32,2,2]{2,0,1:T(8,128)S(1)} %copy-done.50), channel_id=1, source_target_pairs={{0,121},{1,122},{2,123},{3,124},{4,125},{5,126},{6,127},{8,1},{9,2... | collective-permute-start | bytes 1544 | tf_op jit(solution)/shard_map/ppermute | solution.py:25
  372.5 7.6 %copy.210 = f32[64,32,5,5]{3,2,1,0:T(8,128)} copy(f32[64,32,5,5]{0,1,3,2:T(8,128)S(1)} %add.153) | data formatting | bytes 409600 | tf_op jit(solution)/shard_map/add | solution.py:269
  380.1 5.0 add.154
  387.3 17.4 %all-to-all-start.1 = ((f32[128,1,801]{2,1,0:T(1,128)}), f32[128,1,801]{2,1,0:T(1,128)S(1)}, u32[]{:S(2)}, u32[]{:S(2)}) async-start(f32[128,1,801]{2,1,0:T(1,128)} %all_to_all.21), calls=%async_computation.1 | async-start | bytes 917504 | tf_op jit(solution)/shard_map/all_to_all | solution.py:198
  404.8 3.4 collective-permute-start.41
  411.4 5.7 %collective-permute-start.40 = (bf16[64,2,2]{2,0,1:T(8,128)(2,1)S(1)}, bf16[64,2,2]{2,0,1:T(8,128)(2,1)S(1)}, u32[]{:S(2)}, u32[]{:S(2)}) collective-permute-start(bf16[64,2,2]{2,0,1:T(8,128)(2,1)S(1)} %get-tuple-element.34), channel_id=1, source_target_pairs={{0,9},{1,10},{2,11},{3,12},{4,13},{5,14},{6,15},{8,17},{9,18},{10,... | collective-permute-start | bytes 1544 | tf_op jit(solution)/shard_map/ppermute | solution.py:25
  419.6 5.2 %collective-permute-done.47 = bf16[64,2,2]{2,0,1:T(8,128)(2,1)S(1)} collective-permute-done((bf16[64,2,2]{2,0,1:T(8,128)(2,1)S(1)}, bf16[64,2,2]{2,0,1:T(8,128)(2,1)S(1)}, u32[]{:S(2)}, u32[]{:S(2)}) %collective-permute-start.47) | collective-permute-done | bytes 544 | tf_op jit(solution)/shard_map/ppermute | solution.py:25
  426.2 10.2 %collective-permute-done.45 = bf16[64,2,2]{2,0,1:T(8,128)(2,1)S(1)} collective-permute-done((bf16[64,2,2]{2,0,1:T(8,128)(2,1)S(1)}, bf16[64,2,2]{2,0,1:T(8,128)(2,1)S(1)}, u32[]{:S(2)}, u32[]{:S(2)}) %collective-permute-start.45) | collective-permute-done | bytes 544 | tf_op jit(solution)/shard_map/ppermute | solution.py:25
  436.4 8.1 %collective-permute-start.42 = (bf16[64,2,2]{2,0,1:T(8,128)(2,1)S(1)}, bf16[64,2,2]{2,0,1:T(8,128)(2,1)S(1)}, u32[]{:S(2)}, u32[]{:S(2)}) collective-permute-start(bf16[64,2,2]{2,0,1:T(8,128)(2,1)S(1)} %get-tuple-element.37), channel_id=1, source_target_pairs={{0,121},{1,122},{2,123},{3,124},{4,125},{5,126},{6,127},{8,1},{9,2... | collective-permute-start | bytes 1544 | tf_op jit(solution)/shard_map/ppermute | solution.py:25
  448.3 12.8 %all-to-all-start.2 = ((f32[128,1,801]{2,1,0:T(1,128)}), f32[128,1,801]{2,1,0:T(1,128)S(1)}, u32[]{:S(2)}, u32[]{:S(2)}) async-start(f32[128,1,801]{2,1,0:T(1,128)} %broadcast_in_dim.71), calls=%async_computation.2 | async-start | bytes 917504 | tf_op jit(solution)/shard_map/all_to_all | solution.py:199
  461.1 4.0 convolution_select_fusion
  467.8 6.3 %all-to-all-done.2 = f32[128,1,801]{2,1,0:T(1,128)S(1)} async-done(((f32[128,1,801]{2,1,0:T(1,128)}), f32[128,1,801]{2,1,0:T(1,128)S(1)}, u32[]{:S(2)}, u32[]{:S(2)}) %all-to-all-start.2) | async-done | bytes 410144 | tf_op jit(solution)/shard_map/all_to_all | solution.py:199
  476.0 4.5 reshape.401
  480.5 5.6 %copy.221 = f32[32,64,5,5]{1,0,3,2:T(8,128)} copy(f32[32,64,5,5]{3,2,1,0:T(8,128)} %reshape.401) | data formatting | bytes 409600
  486.1 4.5 reshape.400
  490.5 6.2 %copy.220 = f32[64,32,5,5]{0,1,3,2:T(8,128)} copy(f32[64,32,5,5]{3,2,1,0:T(8,128)} %reshape.400) | data formatting | bytes 409600
  (467 shorter events, 164.3 us)
Async XLA Ops:
  2.4 56.2 %collective-permute-start.1 = (f32[32,4,128]{2,0,1:T(8,128)}, f32[32,4,128]{2,0,1:T(8,128)S(1)}, u32[]{:S(2)}, u32[]{:S(2)}) collective-permute-start(f32[32,4,128]{2,0,1:T(8,128)} %get-tuple-element.78), channel_id=1, source_target_pairs={{0,1},{1,2},{2,3},{3,4},{4,5},{5,6},{6,7},{8,9},{9,10},{10,11},{11... | collective-permute-start | bytes 196616 | tf_op jit(solution)/shard_map/ppermute | solution.py:25
  6.8 50.5 %collective-permute-start.6 = (f32[32,4,128]{2,0,1:T(8,128)}, f32[32,4,128]{2,0,1:T(8,128)}, u32[]{:S(2)}, u32[]{:S(2)}) collective-permute-start(f32[32,4,128]{2,0,1:T(8,128)} %get-tuple-element.79), channel_id=1, source_target_pairs={{1,0},{2,1},{3,2},{4,3},{5,4},{6,5},{7,6},{9,8},{10,9},{11,10},{12... | collective-permute-start | bytes 196616 | tf_op jit(solution)/shard_map/ppermute | solution.py:25
  8.8 49.4 %collective-permute-start = (f32[32,4,4]{2,0,1:T(8,128)}, f32[32,4,4]{2,0,1:T(8,128)}, u32[]{:S(2)}, u32[]{:S(2)}) collective-permute-start(f32[32,4,4]{2,0,1:T(8,128)} %get-tuple-element.74), channel_id=1, source_target_pairs={{0,9},{1,10},{2,11},{3,12},{4,13},{5,14},{6,15},{8,17},{9,18},{10,... | collective-permute-start | bytes 6152 | tf_op jit(solution)/shard_map/ppermute | solution.py:25
  16.5 26.4 %collective-permute-start.3 = (f32[32,16,4]{2,0,1:T(8,128)}, f32[32,16,4]{2,0,1:T(8,128)S(1)}, u32[]{:S(2)}, u32[]{:S(2)}) collective-permute-start(f32[32,16,4]{2,0,1:T(8,128)} %get-tuple-element.80), channel_id=1, source_target_pairs={{0,8},{1,9},{2,10},{3,11},{4,12},{5,13},{6,14},{7,15},{8,16},{9,17... | collective-permute-start | bytes 24584 | tf_op jit(solution)/shard_map/ppermute | solution.py:25
  16.5 27.7 %collective-permute-start.4 = (f32[32,16,4]{2,0,1:T(8,128)}, f32[32,16,4]{2,0,1:T(8,128)}, u32[]{:S(2)}, u32[]{:S(2)}) collective-permute-start(f32[32,16,4]{2,0,1:T(8,128)} %get-tuple-element.81), channel_id=1, source_target_pairs={{0,120},{1,121},{2,122},{3,123},{4,124},{5,125},{6,126},{7,127},{8... | collective-permute-start | bytes 24584 | tf_op jit(solution)/shard_map/ppermute | solution.py:25
  31.5 101.2 %all-to-all-start = ((f32[128,1,1056]{2,1,0:T(1,128)}), f32[128,1,1056]{2,1,0:T(1,128)}, u32[]{:S(2)}, u32[]{:S(2)}) async-start(f32[128,1,1056]{2,1,0:T(1,128)} %reshape.604), calls=%async_computation | async-start | bytes 1179648 | tf_op jit(solution)/shard_map/all_to_all | solution.py:247
  42.8 8.6 %collective-permute-start.7 = (f32[32,4,4]{2,0,1:T(8,128)S(1)}, f32[32,4,4]{2,0,1:T(8,128)S(1)}, u32[]{:S(2)}, u32[]{:S(2)}) collective-permute-start(f32[32,4,4]{2,0,1:T(8,128)S(1)} %copy-done.46), channel_id=1, source_target_pairs={{1,120},{2,121},{3,122},{4,123},{5,124},{6,125},{7,126},{9,0},{10,... | collective-permute-start | bytes 6152 | tf_op jit(solution)/shard_map/ppermute | solution.py:25
  44.2 13.1 %collective-permute-start.5 = (f32[32,4,4]{2,0,1:T(8,128)S(1)}, f32[32,4,4]{2,0,1:T(8,128)S(1)}, u32[]{:S(2)}, u32[]{:S(2)}) collective-permute-start(f32[32,4,4]{2,0,1:T(8,128)S(1)} %copy-done.45), channel_id=1, source_target_pairs={{1,8},{2,9},{3,10},{4,11},{5,12},{6,13},{7,14},{9,16},{10,17},{11,... | collective-permute-start | bytes 6152 | tf_op jit(solution)/shard_map/ppermute | solution.py:25
  51.5 7.2 %collective-permute-start.2 = (f32[32,4,4]{2,0,1:T(8,128)S(1)}, f32[32,4,4]{2,0,1:T(8,128)S(1)}, u32[]{:S(2)}, u32[]{:S(2)}) collective-permute-start(f32[32,4,4]{2,0,1:T(8,128)S(1)} %copy-done.44), channel_id=1, source_target_pairs={{0,121},{1,122},{2,123},{3,124},{4,125},{5,126},{6,127},{8,1},{9,2... | collective-permute-start | bytes 6152 | tf_op jit(solution)/shard_map/ppermute | solution.py:25
  73.5 19.0 %collective-permute-start.11 = (f32[32,16,4]{2,0,1:T(8,128)}, f32[32,16,4]{2,0,1:T(8,128)S(1)}, u32[]{:S(2)}, u32[]{:S(2)}) collective-permute-start(f32[32,16,4]{2,0,1:T(8,128)} %get-tuple-element.72), channel_id=1, source_target_pairs={{0,8},{1,9},{2,10},{3,11},{4,12},{5,13},{6,14},{7,15},{8,16},{9,17... | collective-permute-start | bytes 24584 | tf_op jit(solution)/shard_map/ppermute | solution.py:25
  73.5 20.3 %collective-permute-start.12 = (f32[32,16,4]{2,0,1:T(8,128)S(1)}, f32[32,16,4]{2,0,1:T(8,128)S(1)}, u32[]{:S(2)}, u32[]{:S(2)}) collective-permute-start(f32[32,16,4]{2,0,1:T(8,128)S(1)} %get-tuple-element.73), channel_id=1, source_target_pairs={{0,120},{1,121},{2,122},{3,123},{4,124},{5,125},{6,126},{7,127},{8... | collective-permute-start | bytes 24584 | tf_op jit(solution)/shard_map/ppermute | solution.py:25
  79.2 32.5 %collective-permute-start.9 = (f32[32,4,128]{2,0,1:T(8,128)}, f32[32,4,128]{2,0,1:T(8,128)S(1)}, u32[]{:S(2)}, u32[]{:S(2)}) collective-permute-start(f32[32,4,128]{2,0,1:T(8,128)} %get-tuple-element.70), channel_id=1, source_target_pairs={{0,1},{1,2},{2,3},{3,4},{4,5},{5,6},{6,7},{8,9},{9,10},{10,11},{11... | collective-permute-start | bytes 196616 | tf_op jit(solution)/shard_map/ppermute | solution.py:25
  82.4 28.3 %collective-permute-start.14 = (f32[32,4,128]{2,0,1:T(8,128)}, f32[32,4,128]{2,0,1:T(8,128)S(1)}, u32[]{:S(2)}, u32[]{:S(2)}) collective-permute-start(f32[32,4,128]{2,0,1:T(8,128)} %get-tuple-element.71), channel_id=1, source_target_pairs={{1,0},{2,1},{3,2},{4,3},{5,4},{6,5},{7,6},{9,8},{10,9},{11,10},{12... | collective-permute-start | bytes 196616 | tf_op jit(solution)/shard_map/ppermute | solution.py:25
  83.7 27.1 %collective-permute-start.8 = (f32[32,4,4]{2,0,1:T(8,128)}, f32[32,4,4]{2,0,1:T(8,128)S(1)}, u32[]{:S(2)}, u32[]{:S(2)}) collective-permute-start(f32[32,4,4]{2,0,1:T(8,128)} %get-tuple-element.66), channel_id=1, source_target_pairs={{0,9},{1,10},{2,11},{3,12},{4,13},{5,14},{6,15},{8,17},{9,18},{10,... | collective-permute-start | bytes 6152 | tf_op jit(solution)/shard_map/ppermute | solution.py:25
  92.5 6.5 %collective-permute-start.15 = (f32[32,4,4]{2,0,1:T(8,128)S(1)}, f32[32,4,4]{2,0,1:T(8,128)S(1)}, u32[]{:S(2)}, u32[]{:S(2)}) collective-permute-start(f32[32,4,4]{2,0,1:T(8,128)S(1)} %copy-done.49), channel_id=1, source_target_pairs={{1,120},{2,121},{3,122},{4,123},{5,124},{6,125},{7,126},{9,0},{10,... | collective-permute-start | bytes 6152 | tf_op jit(solution)/shard_map/ppermute | solution.py:25
  93.8 16.9 %collective-permute-start.13 = (f32[32,4,4]{2,0,1:T(8,128)S(1)}, f32[32,4,4]{2,0,1:T(8,128)S(1)}, u32[]{:S(2)}, u32[]{:S(2)}) collective-permute-start(f32[32,4,4]{2,0,1:T(8,128)S(1)} %copy-done.48), channel_id=1, source_target_pairs={{1,8},{2,9},{3,10},{4,11},{5,12},{6,13},{7,14},{9,16},{10,17},{11,... | collective-permute-start | bytes 6152 | tf_op jit(solution)/shard_map/ppermute | solution.py:25
  99.0 12.7 %collective-permute-start.10 = (f32[32,4,4]{2,0,1:T(8,128)S(1)}, f32[32,4,4]{2,0,1:T(8,128)S(1)}, u32[]{:S(2)}, u32[]{:S(2)}) collective-permute-start(f32[32,4,4]{2,0,1:T(8,128)S(1)} %copy-done.47), channel_id=1, source_target_pairs={{0,121},{1,122},{2,123},{3,124},{4,125},{5,126},{6,127},{8,1},{9,2... | collective-permute-start | bytes 6152 | tf_op jit(solution)/shard_map/ppermute | solution.py:25
  198.7 43.9 %collective-permute-start.17 = (f32[32,2,128]{2,0,1:T(8,128)S(1)}, f32[32,2,128]{2,0,1:T(8,128)S(1)}, u32[]{:S(2)}, u32[]{:S(2)}) collective-permute-start(f32[32,2,128]{2,0,1:T(8,128)S(1)} %get-tuple-element.62), channel_id=1, source_target_pairs={{0,1},{1,2},{2,3},{3,4},{4,5},{5,6},{6,7},{8,9},{9,10},{10,11},{11... | collective-permute-start | bytes 98312 | tf_op jit(solution)/shard_map/ppermute | solution.py:25
  202.5 39.4 %collective-permute-start.22 = (f32[32,2,128]{2,0,1:T(8,128)S(1)}, f32[32,2,128]{2,0,1:T(8,128)S(1)}, u32[]{:S(2)}, u32[]{:S(2)}) collective-permute-start(f32[32,2,128]{2,0,1:T(8,128)S(1)} %get-tuple-element.63), channel_id=1, source_target_pairs={{1,0},{2,1},{3,2},{4,3},{5,4},{6,5},{7,6},{9,8},{10,9},{11,10},{12... | collective-permute-start | bytes 98312 | tf_op jit(solution)/shard_map/ppermute | solution.py:25
  209.5 32.6 %collective-permute-start.16 = (f32[32,2,2]{2,0,1:T(8,128)S(1)}, f32[32,2,2]{2,0,1:T(8,128)S(1)}, u32[]{:S(2)}, u32[]{:S(2)}) collective-permute-start(f32[32,2,2]{2,0,1:T(8,128)S(1)} %get-tuple-element.58), channel_id=1, source_target_pairs={{0,9},{1,10},{2,11},{3,12},{4,13},{5,14},{6,15},{8,17},{9,18},{10,... | collective-permute-start | bytes 1544 | tf_op jit(solution)/shard_map/ppermute | solution.py:25
  210.8 9.3 %collective-permute-start.19 = (f32[32,16,2]{2,0,1:T(8,128)S(1)}, f32[32,16,2]{2,0,1:T(8,128)S(1)}, u32[]{:S(2)}, u32[]{:S(2)}) collective-permute-start(f32[32,16,2]{2,0,1:T(8,128)S(1)} %get-tuple-element.64), channel_id=1, source_target_pairs={{0,8},{1,9},{2,10},{3,11},{4,12},{5,13},{6,14},{7,15},{8,16},{9,17... | collective-permute-start | bytes 12296 | tf_op jit(solution)/shard_map/ppermute | solution.py:25
  210.9 10.5 %collective-permute-start.20 = (f32[32,16,2]{2,0,1:T(8,128)S(1)}, f32[32,16,2]{2,0,1:T(8,128)S(1)}, u32[]{:S(2)}, u32[]{:S(2)}) collective-permute-start(f32[32,16,2]{2,0,1:T(8,128)S(1)} %get-tuple-element.65), channel_id=1, source_target_pairs={{0,120},{1,121},{2,122},{3,123},{4,124},{5,125},{6,126},{7,127},{8... | collective-permute-start | bytes 12296 | tf_op jit(solution)/shard_map/ppermute | solution.py:25
  221.4 20.6 %collective-permute-start.21 = (f32[32,2,2]{2,0,1:T(8,128)S(1)}, f32[32,2,2]{2,0,1:T(8,128)S(1)}, u32[]{:S(2)}, u32[]{:S(2)}) collective-permute-start(f32[32,2,2]{2,0,1:T(8,128)S(1)} %get-tuple-element.60), channel_id=1, source_target_pairs={{1,8},{2,9},{3,10},{4,11},{5,12},{6,13},{7,14},{9,16},{10,17},{11,... | collective-permute-start | bytes 1544 | tf_op jit(solution)/shard_map/ppermute | solution.py:25
  226.2 16.4 %collective-permute-start.18 = (f32[32,2,2]{2,0,1:T(8,128)S(1)}, f32[32,2,2]{2,0,1:T(8,128)S(1)}, u32[]{:S(2)}, u32[]{:S(2)}) collective-permute-start(f32[32,2,2]{2,0,1:T(8,128)S(1)} %get-tuple-element.61), channel_id=1, source_target_pairs={{0,121},{1,122},{2,123},{3,124},{4,125},{5,126},{6,127},{8,1},{9,2... | collective-permute-start | bytes 1544 | tf_op jit(solution)/shard_map/ppermute | solution.py:25
  254.3 38.7 %collective-permute-start.25 = (bf16[64,2,128]{2,0,1:T(8,128)(2,1)S(1)}, bf16[64,2,128]{2,0,1:T(8,128)(2,1)S(1)}, u32[]{:S(2)}, u32[]{:S(2)}) collective-permute-start(bf16[64,2,128]{2,0,1:T(8,128)(2,1)S(1)} %get-tuple-element.54), channel_id=1, source_target_pairs={{0,1},{1,2},{2,3},{3,4},{4,5},{5,6},{6,7},{8,9},{9,10},{10,11},{11... | collective-permute-start | bytes 98312 | tf_op jit(solution)/shard_map/ppermute | solution.py:25
  258.3 34.7 %collective-permute-start.30 = (bf16[64,2,128]{2,0,1:T(8,128)(2,1)S(1)}, bf16[64,2,128]{2,0,1:T(8,128)(2,1)S(1)}, u32[]{:S(2)}, u32[]{:S(2)}) collective-permute-start(bf16[64,2,128]{2,0,1:T(8,128)(2,1)S(1)} %get-tuple-element.55), channel_id=1, source_target_pairs={{1,0},{2,1},{3,2},{4,3},{5,4},{6,5},{7,6},{9,8},{10,9},{11,10},{12... | collective-permute-start | bytes 98312 | tf_op jit(solution)/shard_map/ppermute | solution.py:25
  264.8 7.2 %collective-permute-start.24 = (bf16[64,2,2]{2,0,1:T(8,128)(2,1)S(1)}, bf16[64,2,2]{2,0,1:T(8,128)(2,1)S(1)}, u32[]{:S(2)}, u32[]{:S(2)}) collective-permute-start(bf16[64,2,2]{2,0,1:T(8,128)(2,1)S(1)} %get-tuple-element.50), channel_id=1, source_target_pairs={{0,9},{1,10},{2,11},{3,12},{4,13},{5,14},{6,15},{8,17},{9,18},{10,... | collective-permute-start | bytes 1544 | tf_op jit(solution)/shard_map/ppermute | solution.py:25
  269.4 17.2 %collective-permute-start.31 = (bf16[64,2,2]{2,0,1:T(8,128)(2,1)S(1)}, bf16[64,2,2]{2,0,1:T(8,128)(2,1)S(1)}, u32[]{:S(2)}, u32[]{:S(2)}) collective-permute-start(bf16[64,2,2]{2,0,1:T(8,128)(2,1)S(1)} %get-tuple-element.51), channel_id=1, source_target_pairs={{1,120},{2,121},{3,122},{4,123},{5,124},{6,125},{7,126},{9,0},{10,... | collective-permute-start | bytes 1544 | tf_op jit(solution)/shard_map/ppermute | solution.py:25
  270.7 16.0 %collective-permute-start.29 = (bf16[64,2,2]{2,0,1:T(8,128)(2,1)S(1)}, bf16[64,2,2]{2,0,1:T(8,128)(2,1)S(1)}, u32[]{:S(2)}, u32[]{:S(2)}) collective-permute-start(bf16[64,2,2]{2,0,1:T(8,128)(2,1)S(1)} %get-tuple-element.52), channel_id=1, source_target_pairs={{1,8},{2,9},{3,10},{4,11},{5,12},{6,13},{7,14},{9,16},{10,17},{11,... | collective-permute-start | bytes 1544 | tf_op jit(solution)/shard_map/ppermute | solution.py:25
  272.1 15.5 %collective-permute-start.26 = (bf16[64,2,2]{2,0,1:T(8,128)(2,1)S(1)}, bf16[64,2,2]{2,0,1:T(8,128)(2,1)S(1)}, u32[]{:S(2)}, u32[]{:S(2)}) collective-permute-start(bf16[64,2,2]{2,0,1:T(8,128)(2,1)S(1)} %get-tuple-element.53), channel_id=1, source_target_pairs={{0,121},{1,122},{2,123},{3,124},{4,125},{5,126},{6,127},{8,1},{9,2... | collective-permute-start | bytes 1544 | tf_op jit(solution)/shard_map/ppermute | solution.py:25
  307.8 48.3 %collective-permute-start.33 = (f32[32,2,128]{2,0,1:T(8,128)}, f32[32,2,128]{2,0,1:T(8,128)S(1)}, u32[]{:S(2)}, u32[]{:S(2)}) collective-permute-start(f32[32,2,128]{2,0,1:T(8,128)} %get-tuple-element.46), channel_id=1, source_target_pairs={{0,1},{1,2},{2,3},{3,4},{4,5},{5,6},{6,7},{8,9},{9,10},{10,11},{11... | collective-permute-start | bytes 98312 | tf_op jit(solution)/shard_map/ppermute | solution.py:25
  311.1 44.4 %collective-permute-start.38 = (f32[32,2,128]{2,0,1:T(8,128)}, f32[32,2,128]{2,0,1:T(8,128)S(1)}, u32[]{:S(2)}, u32[]{:S(2)}) collective-permute-start(f32[32,2,128]{2,0,1:T(8,128)} %get-tuple-element.47), channel_id=1, source_target_pairs={{1,0},{2,1},{3,2},{4,3},{5,4},{6,5},{7,6},{9,8},{10,9},{11,10},{12... | collective-permute-start | bytes 98312 | tf_op jit(solution)/shard_map/ppermute | solution.py:25
  318.0 37.6 %collective-permute-start.32 = (f32[32,2,2]{2,0,1:T(8,128)}, f32[32,2,2]{2,0,1:T(8,128)S(1)}, u32[]{:S(2)}, u32[]{:S(2)}) collective-permute-start(f32[32,2,2]{2,0,1:T(8,128)} %get-tuple-element.42), channel_id=1, source_target_pairs={{0,9},{1,10},{2,11},{3,12},{4,13},{5,14},{6,15},{8,17},{9,18},{10,... | collective-permute-start | bytes 1544 | tf_op jit(solution)/shard_map/ppermute | solution.py:25
  321.6 16.1 %collective-permute-start.35 = (f32[32,16,2]{2,0,1:T(8,128)}, f32[32,16,2]{2,0,1:T(8,128)S(1)}, u32[]{:S(2)}, u32[]{:S(2)}) collective-permute-start(f32[32,16,2]{2,0,1:T(8,128)} %get-tuple-element.48), channel_id=1, source_target_pairs={{0,8},{1,9},{2,10},{3,11},{4,12},{5,13},{6,14},{7,15},{8,16},{9,17... | collective-permute-start | bytes 12296 | tf_op jit(solution)/shard_map/ppermute | solution.py:25
  321.6 17.4 %collective-permute-start.36 = (f32[32,16,2]{2,0,1:T(8,128)S(1)}, f32[32,16,2]{2,0,1:T(8,128)S(1)}, u32[]{:S(2)}, u32[]{:S(2)}) collective-permute-start(f32[32,16,2]{2,0,1:T(8,128)S(1)} %get-tuple-element.49), channel_id=1, source_target_pairs={{0,120},{1,121},{2,122},{3,123},{4,124},{5,125},{6,126},{7,127},{8... | collective-permute-start | bytes 12296 | tf_op jit(solution)/shard_map/ppermute | solution.py:25
  337.7 6.3 %collective-permute-start.39 = (f32[32,2,2]{2,0,1:T(8,128)}, f32[32,2,2]{2,0,1:T(8,128)S(1)}, u32[]{:S(2)}, u32[]{:S(2)}) collective-permute-start(f32[32,2,2]{2,0,1:T(8,128)} %get-tuple-element.43), channel_id=1, source_target_pairs={{1,120},{2,121},{3,122},{4,123},{5,124},{6,125},{7,126},{9,0},{10,... | collective-permute-start | bytes 1544 | tf_op jit(solution)/shard_map/ppermute | solution.py:25
  339.1 16.4 %collective-permute-start.37 = (f32[32,2,2]{2,0,1:T(8,128)S(1)}, f32[32,2,2]{2,0,1:T(8,128)S(1)}, u32[]{:S(2)}, u32[]{:S(2)}) collective-permute-start(f32[32,2,2]{2,0,1:T(8,128)S(1)} %copy-done.51), channel_id=1, source_target_pairs={{1,8},{2,9},{3,10},{4,11},{5,12},{6,13},{7,14},{9,16},{10,17},{11,... | collective-permute-start | bytes 1544 | tf_op jit(solution)/shard_map/ppermute | solution.py:25
  344.1 12.0 %collective-permute-start.34 = (f32[32,2,2]{2,0,1:T(8,128)S(1)}, f32[32,2,2]{2,0,1:T(8,128)S(1)}, u32[]{:S(2)}, u32[]{:S(2)}) collective-permute-start(f32[32,2,2]{2,0,1:T(8,128)S(1)} %copy-done.50), channel_id=1, source_target_pairs={{0,121},{1,122},{2,123},{3,124},{4,125},{5,126},{6,127},{8,1},{9,2... | collective-permute-start | bytes 1544 | tf_op jit(solution)/shard_map/ppermute | solution.py:25
  387.3 59.6 %all-to-all-start.1 = ((f32[128,1,801]{2,1,0:T(1,128)}), f32[128,1,801]{2,1,0:T(1,128)S(1)}, u32[]{:S(2)}, u32[]{:S(2)}) async-start(f32[128,1,801]{2,1,0:T(1,128)} %all_to_all.21), calls=%async_computation.1 | async-start | bytes 917504 | tf_op jit(solution)/shard_map/all_to_all | solution.py:198
  404.8 40.8 %collective-permute-start.41 = (bf16[64,2,128]{2,0,1:T(8,128)(2,1)S(1)}, bf16[64,2,128]{2,0,1:T(8,128)(2,1)S(1)}, u32[]{:S(2)}, u32[]{:S(2)}) collective-permute-start(bf16[64,2,128]{2,0,1:T(8,128)(2,1)S(1)} %get-tuple-element.38), channel_id=1, source_target_pairs={{0,1},{1,2},{2,3},{3,4},{4,5},{5,6},{6,7},{8,9},{9,10},{10,11},{11... | collective-permute-start | bytes 98312 | tf_op jit(solution)/shard_map/ppermute | solution.py:25
  408.2 37.4 %collective-permute-start.46 = (bf16[64,2,128]{2,0,1:T(8,128)(2,1)S(1)}, bf16[64,2,128]{2,0,1:T(8,128)(2,1)S(1)}, u32[]{:S(2)}, u32[]{:S(2)}) collective-permute-start(bf16[64,2,128]{2,0,1:T(8,128)(2,1)S(1)} %get-tuple-element.39), channel_id=1, source_target_pairs={{1,0},{2,1},{3,2},{4,3},{5,4},{6,5},{7,6},{9,8},{10,9},{11,10},{12... | collective-permute-start | bytes 98312 | tf_op jit(solution)/shard_map/ppermute | solution.py:25
  409.5 36.1 %collective-permute-start.43 = (bf16[64,16,2]{2,0,1:T(8,128)(2,1)S(1)}, bf16[64,16,2]{2,0,1:T(8,128)(2,1)S(1)}, u32[]{:S(2)}, u32[]{:S(2)}) collective-permute-start(bf16[64,16,2]{2,0,1:T(8,128)(2,1)S(1)} %copy-done.28), channel_id=1, source_target_pairs={{0,8},{1,9},{2,10},{3,11},{4,12},{5,13},{6,14},{7,15},{8,16},{9,17... | collective-permute-start | bytes 12296 | tf_op jit(solution)/shard_map/ppermute | solution.py:25
  411.3 34.2 %collective-permute-start.44 = (bf16[64,16,2]{2,0,1:T(8,128)(2,1)S(1)}, bf16[64,16,2]{2,0,1:T(8,128)(2,1)S(1)}, u32[]{:S(2)}, u32[]{:S(2)}) collective-permute-start(bf16[64,16,2]{2,0,1:T(8,128)(2,1)S(1)} %copy-done.27), channel_id=1, source_target_pairs={{0,120},{1,121},{2,122},{3,123},{4,124},{5,125},{6,126},{7,127},{8... | collective-permute-start | bytes 12296 | tf_op jit(solution)/shard_map/ppermute | solution.py:25
  411.4 6.7 %collective-permute-start.40 = (bf16[64,2,2]{2,0,1:T(8,128)(2,1)S(1)}, bf16[64,2,2]{2,0,1:T(8,128)(2,1)S(1)}, u32[]{:S(2)}, u32[]{:S(2)}) collective-permute-start(bf16[64,2,2]{2,0,1:T(8,128)(2,1)S(1)} %get-tuple-element.34), channel_id=1, source_target_pairs={{0,9},{1,10},{2,11},{3,12},{4,13},{5,14},{6,15},{8,17},{9,18},{10,... | collective-permute-start | bytes 1544 | tf_op jit(solution)/shard_map/ppermute | solution.py:25
  418.2 6.7 %collective-permute-start.47 = (bf16[64,2,2]{2,0,1:T(8,128)(2,1)S(1)}, bf16[64,2,2]{2,0,1:T(8,128)(2,1)S(1)}, u32[]{:S(2)}, u32[]{:S(2)}) collective-permute-start(bf16[64,2,2]{2,0,1:T(8,128)(2,1)S(1)} %get-tuple-element.35), channel_id=1, source_target_pairs={{1,120},{2,121},{3,122},{4,123},{5,124},{6,125},{7,126},{9,0},{10,... | collective-permute-start | bytes 1544 | tf_op jit(solution)/shard_map/ppermute | solution.py:25
  424.9 11.5 %collective-permute-start.45 = (bf16[64,2,2]{2,0,1:T(8,128)(2,1)S(1)}, bf16[64,2,2]{2,0,1:T(8,128)(2,1)S(1)}, u32[]{:S(2)}, u32[]{:S(2)}) collective-permute-start(bf16[64,2,2]{2,0,1:T(8,128)(2,1)S(1)} %get-tuple-element.36), channel_id=1, source_target_pairs={{1,8},{2,9},{3,10},{4,11},{5,12},{6,13},{7,14},{9,16},{10,17},{11,... | collective-permute-start | bytes 1544 | tf_op jit(solution)/shard_map/ppermute | solution.py:25
  436.4 9.2 %collective-permute-start.42 = (bf16[64,2,2]{2,0,1:T(8,128)(2,1)S(1)}, bf16[64,2,2]{2,0,1:T(8,128)(2,1)S(1)}, u32[]{:S(2)}, u32[]{:S(2)}) collective-permute-start(bf16[64,2,2]{2,0,1:T(8,128)(2,1)S(1)} %get-tuple-element.37), channel_id=1, source_target_pairs={{0,121},{1,122},{2,123},{3,124},{4,125},{5,126},{6,127},{8,1},{9,2... | collective-permute-start | bytes 1544 | tf_op jit(solution)/shard_map/ppermute | solution.py:25
  448.3 25.8 %all-to-all-start.2 = ((f32[128,1,801]{2,1,0:T(1,128)}), f32[128,1,801]{2,1,0:T(1,128)S(1)}, u32[]{:S(2)}, u32[]{:S(2)}) async-start(f32[128,1,801]{2,1,0:T(1,128)} %broadcast_in_dim.71), calls=%async_computation.2 | async-start | bytes 917504 | tf_op jit(solution)/shard_map/all_to_all | solution.py:199
  (69 other events, 598.5 us)
